TPU v7x, 32 devices: a whole 2x2x4 slice. The times are simulated.
32 devices in a mesh: wide: 8 (over z, y), narrow: 4 (over x, core).
Axes of the slice: x: 2, y: 2, z: 4, core: 2. Of those that a mesh axis runs over, the one named last changes fastest.
Arguments:
- entity_table: bfloat16 [65536, 512], P(('wide', 'narrow')), may hold values from -3 to 3
- relation_table: bfloat16 [4096, 512], replicated, may hold values from -3.59375 to 3.59375
- triple_rel: int32 [8192], P(('wide', 'narrow')), may hold values from 0 to 4095, as said below
- triple_owners: int32 [8192, 2], P(('wide', 'narrow')), may hold values from 0 to 31, all different within a row; in each aligned block of 256 rows (0 to 255, 256 to 511, ...) at most 32 rows name the same one
- triple_local: int32 [8192, 2], P(('wide', 'narrow')), may hold values from 0 to 2047
- negative_ids: int32 [8192], P(('wide', 'narrow')), may hold values from 0 to 2047
Outputs:
- entity_grad: bfloat16 [65536, 512], P(('wide', 'narrow'))
- relation_grad: bfloat16 [4096, 512], replicated
- loss: float32 [8192], P(('wide', 'narrow'))
Inputs may be any that keep to these rules, and one draw needn't show every extreme that they name: `triple_owners`: the two owners of a triple differ. Among the triples of one device no owner is named more than 32 times, and in every draw the triples of some device name some owner exactly 32 times. `triple_rel`: relation group k holds relations k * 128 to (k + 1) * 128 - 1. Among the triples of each device the relations of exactly one group appear exactly 16 times, and those of every other group appear equally often up to one, at most 16 times.
All inputs are finite; a program needn't handle non-finite values.
Results may differ from a plain program's by a relative error of at most 0.0075.
Values may be sent and summed in bfloat16 or wider, within the bound.
No kernel may reach another device: no remote copies, remote signals or barrier semaphores. Data moves between devices by JAX's collectives and lax.ppermute only.
A program may use at most 128 MiB of HBM per device.

v0:
```python
import jax
import jax.numpy as jnp
from jax import lax
from jax.sharding import PartitionSpec as P


def swap_halves(rows):
    half_width = rows.shape[-1] // 2
    return jnp.concatenate([rows[..., half_width:], rows[..., :half_width]], axis=-1)


def slot_ranks(targets, count):
    onehot = (targets[:, None] == jnp.arange(count, dtype=jnp.int32)[None, :]).astype(jnp.int32)
    return jnp.sum((jnp.cumsum(onehot, axis=0) - onehot) * onehot, axis=1)


def body(entity_table, relation_table, triple_rel, triple_owners, triple_local, negative_ids):
    wide_count = lax.axis_size("wide")
    narrow_count = lax.axis_size("narrow")
    device_count = wide_count * narrow_count
    triples = triple_rel.shape[0]
    row_width = entity_table.shape[1]
    capacity = max(2, 4 * triples // device_count)
    owners = triple_owners.reshape(-1)
    local_rows = triple_local.reshape(-1)
    slot_rank = slot_ranks(owners, device_count)
    send_ids = jnp.zeros((device_count, capacity), jnp.int32).at[owners, slot_rank].set(local_rows)
    asked_ids = lax.all_to_all(
        send_ids, ("wide", "narrow"), split_axis=0, concat_axis=0, tiled=True
    )
    served = jnp.take(entity_table, asked_ids, axis=0)
    got_rows = lax.all_to_all(served, ("wide", "narrow"), split_axis=0, concat_axis=0, tiled=True)
    fetched = got_rows[owners, slot_rank].reshape(triples, 2, row_width)
    head_rows = fetched[:, 0]
    tail_rows = fetched[:, 1]
    rel_rows = jnp.take(relation_table, triple_rel, axis=0)
    query = (
        0.5 * swap_halves(head_rows).astype(jnp.float32) * swap_halves(rel_rows).astype(jnp.float32)
    ).astype(jnp.bfloat16)
    positive = jnp.sum(query.astype(jnp.float32) * tail_rows.astype(jnp.float32), axis=1)
    own_negs = jnp.take(entity_table, negative_ids, axis=0)
    gathered = lax.all_gather(own_negs, "narrow", axis=0, tiled=True)
    group_neg = gathered.shape[0]
    scores = jnp.einsum("tc,kc->tk", query, gathered, preferred_element_type=jnp.float32)
    loss = jax.nn.softplus(-positive) + jnp.sum(jax.nn.softplus(scores), axis=1) / group_neg
    neg_weights = (jax.nn.sigmoid(scores) / group_neg).astype(jnp.bfloat16)
    pos_weight = -jax.nn.sigmoid(-positive)
    query_grad = pos_weight[:, None] * tail_rows.astype(jnp.float32) + jnp.dot(
        neg_weights, gathered, preferred_element_type=jnp.float32
    )
    tail_grad = pos_weight[:, None] * query.astype(jnp.float32)
    head_grad = 0.5 * swap_halves(query_grad) * rel_rows.astype(jnp.float32)
    rel_part = 0.5 * swap_halves(query_grad) * head_rows.astype(jnp.float32)
    neg_grad = lax.psum_scatter(
        jnp.einsum("tk,tc->kc", neg_weights, query, preferred_element_type=jnp.float32).astype(
            jnp.bfloat16
        ),
        "narrow",
        scatter_dimension=0,
        tiled=True,
    ).astype(jnp.float32)
    send_grads = jnp.zeros((device_count, capacity, row_width), jnp.float32)
    send_grads = send_grads.at[owners, slot_rank].set(
        jnp.stack([head_grad, tail_grad], axis=1).reshape(2 * triples, row_width)
    )
    back_grads = lax.all_to_all(
        send_grads, ("wide", "narrow"), split_axis=0, concat_axis=0, tiled=True
    )
    entity_grad = jnp.zeros((entity_table.shape[0], row_width), jnp.float32)
    entity_grad = entity_grad.at[asked_ids.reshape(-1)].add(back_grads.reshape(-1, row_width))
    entity_grad = entity_grad.at[negative_ids].add(neg_grad)
    local_rel = jax.ops.segment_sum(rel_part, triple_rel, num_segments=relation_table.shape[0])
    relation_grad = lax.psum(local_rel, ("wide", "narrow")).astype(jnp.bfloat16)
    return (entity_grad.astype(jnp.bfloat16), relation_grad, loss)


def solution(mesh):
    return jax.shard_map(
        body,
        mesh=mesh,
        in_specs=(
            P(("wide", "narrow"), None),
            P(),
            P(("wide", "narrow")),
            P(("wide", "narrow"), None),
            P(("wide", "narrow"), None),
            P(("wide", "narrow")),
        ),
        out_specs=(P(("wide", "narrow"), None), P(), P(("wide", "narrow"))),
        check_vma=False,
    )
```

profile of v0, /device:TPU:0, one launch (start us, length us, event | category | flops | bytes accessed | tf_op | source)
XLA Modules:
  0.0 384.5 jit_solution(1418996323916338346)
XLA Ops:
  7.2 1.0 copy.17
  8.1 0.1 eq.29
  8.3 0.1 eq.25
  8.4 0.1 reshape.314
  8.6 1.2 reduce-window.6
  9.8 0.2 slice_reduce_fusion
  10.0 0.8 copy.21
  10.8 0.1 reshape.354
  11.0 0.1 fusion.17
  11.1 25.1 %scatter_fusion = s32[32,32]{1,0:T(8,128)S(1)} fusion(s32[32,32]{1,0:T(8,128)S(1)} %broadcast_in_dim.65, s32[512]{0:T(512)S(1)} %bitcast.66, s32[512]{0:T(512)S(1)} %reshape.354), kind=kCustom, calls=%fused_computation.4 | custom fusion | bytes 10240 | tf_op jit(solution)/shard_map/scatter | solution.py:27
  36.3 14.3 %all_to_all.25 = s32[32,1,32]{2,1,0:T(1,128)S(1)} all-to-all(s32[32,1,32]{2,1,0:T(1,128)S(1)} %bitcast.65), channel_id=1, replica_groups=mesh['wide'=8,'narrow'=4] {'wide','narrow'}, dimensions={0} | all-to-all | bytes 8192 | tf_op jit(solution)/shard_map/all_to_all | solution.py:28
  50.6 0.6 copy-done.14
  51.2 0.1 reshape.324
  51.3 4.0 %gather_fusion = bf16[1024,512]{1,0:T(8,128)(2,1)S(1)} fusion(bf16[2048,512]{1,0:T(8,128)(2,1)S(1)} %copy-done, s32[1024]{0:T(1024)S(1)} %broadcast_clamp_fusion), kind=kCustom, calls=%fused_computation | custom fusion | bytes 2101248 | tf_op jit(solution)/shard_map/jit(_take)/gather | solution.py:31
  55.3 1.2 broadcast_select_fusion
  56.4 2.6 all-to-all-start.1
  59.2 1.2 gather_fusion.3
  60.4 0.8 broadcast_select_fusion.1
  61.2 3.9 %gather_fusion.2 = bf16[256,512]{1,0:T(8,128)(2,1)S(1)} fusion(bf16[4096,512]{1,0:T(8,128)(2,1)} %param.7, s32[1024]{0:T(1024)S(1)} %pad_clamp_fusion.1), kind=kCustom, calls=%fused_computation.2 | custom fusion | bytes 525312 | tf_op jit(solution)/shard_map/jit(_take)/gather | solution.py:36
  65.2 0.8 broadcast_select_fusion.2
  66.0 19.3 %all-to-all-done.1 = bf16[32,32,512]{2,1,0:T(8,128)(2,1)S(1)} async-done(((bf16[32,32,512]{2,1,0:T(8,128)(2,1)}), bf16[32,32,512]{2,1,0:T(8,128)(2,1)S(1)}, u32[]{:S(2)}, u32[]{:S(2)}) %all-to-all-start.1) | async-done | bytes 1048608 | tf_op jit(solution)/shard_map/all_to_all | solution.py:32
  85.3 6.4 %gather_fusion.1 = bf16[512,512]{1,0:T(8,128)(2,1)} fusion(bf16[32,32,512]{2,1,0:T(8,128)(2,1)S(1)} %all-to-all-done.1, s32[512]{0:T(512)S(1)} %bitcast.68), kind=kCustom, calls=%fused_computation.1 | custom fusion | bytes 1052672 | tf_op jit(solution)/shard_map/gather | solution.py:33
  91.7 1.2 reshape.318
  92.9 0.7 fusion.24
  93.8 1.9 fusion.25
  95.7 0.6 copy-done.5
  96.4 0.2 fusion.5
  96.7 2.5 fusion.4
  99.2 0.6 fusion.20
  99.9 0.5 convolution_add_fusion
  100.3 0.9 fusion.23
  101.2 0.1 fusion.6
  101.4 0.1 convert_multiply_fusion.2
  101.6 1.8 copy.25
  103.4 2.9 reshape.360
  106.3 1.6 broadcast_in_dim.66
  107.9 64.1 %scatter_fusion.1 = f32[32,32,512]{2,1,0:T(8,128)} fusion(f32[32,32,512]{2,1,0:T(8,128)} %broadcast_in_dim.66, s32[512]{0:T(512)S(1)} %bitcast.67, f32[512,512]{1,0:T(8,128)} %reshape.360), kind=kCustom, calls=%fused_computation.5 | custom fusion | bytes 3149824 | tf_op jit(solution)/shard_map/scatter | solution.py:63
  172.0 3.7 all-to-all-start.2
  175.7 0.2 reduce-scatter.2.cloned.1.call-start
  175.9 0.5 broadcast.277
  176.4 2.0 reduce.5
  178.4 0.8 reshape.317
  179.2 2.8 convolution_convert_fusion
  182.1 6.0 %scatter_custom_fusion.4 = f32[4096,512]{1,0:T(8,128)} fusion(s32[256]{0:T(256)} %param.8, f32[]{:T(128)} %constant.32.clone.1, f32[256,256]{1,0:T(8,128)S(1)} %copy-done.4, f32[]{:T(128)} %constant.122, f32[256,256]{1,0:T(8,128)S(1)} %copy-done.3, f32[]{:T(128)} %constant.45.clone.1, bf16[256,1,512]{2,1,0:T(2,128)(2,1)S(1)} %get-tuple-element.10), kind=kCustom, calls=%fused_computation.9 | custom fusion | flops 655360 | bytes 9176576 | tf_op jit(solution)/shard_map/scatter-add | solution.py:72
  188.1 169.5 %all-reduce.1 = bf16[4096,512]{1,0:T(8,128)(2,1)} all-reduce(f32[4096,512]{1,0:T(8,128)} %scatter_custom_fusion.4), channel_id=1, replica_groups=mesh['wide'=8,'narrow'=4] {'wide','narrow'}, use_global_device_ids=true, to_apply=%region_10.11 | all-reduce | flops 2097152 | bytes 12582912 | tf_op jit(solution)/shard_map/psum | solution.py:73
  357.6 9.8 %scatter_custom_fusion.2 = f32[2048,512]{1,0:T(8,128)} fusion(s32[1024]{0:T(1024)S(1)} %bitcast.74, f32[1024,512]{1,0:T(8,128)} %bitcast.19, f32[]{:T(128)} %constant.32.clone.1), kind=kCustom, calls=%fused_computation.12 | custom fusion | flops 524288 | bytes 4194816 | tf_op jit(solution)/shard_map/scatter-add | solution.py:70
  367.3 6.6 %scatter_custom_fusion.3 = f32[2048,512]{1,0:T(8,128)} fusion(f32[2048,512]{1,0:T(8,128)} %scatter_custom_fusion.2, s32[256]{0:T(256)S(1)} %compare_select_fusion.7, bf16[256,512]{1,0:T(8,128)(2,1)} %reduce-scatter.2.cloned.1.call-done), kind=kCustom, calls=%fused_computation.30 | custom fusion | flops 262144 | bytes 4456448 | tf_op jit(solution)/shard_map/scatter-add | solution.py:71
  373.9 3.8 convert_element_type.107
  (63 shorter events, 0.5 us)
Async XLA Ops:
  7.2 44.1 %copy-start = (bf16[2048,512]{1,0:T(8,128)(2,1)S(1)}, bf16[2048,512]{1,0:T(8,128)(2,1)}, u32[]{:S(2)}) copy-start(bf16[2048,512]{1,0:T(8,128)(2,1)} %param.6) | copy-start | bytes 6291460
  50.6 0.6 copy-start.14
  55.2 3.9 %copy-start.17 = (s32[256]{0:T(256)S(1)}, s32[256]{0:T(256)}, u32[]{:S(2)}) copy-start(s32[256]{0:T(256)} %param.11) | copy-start | bytes 3076
  55.3 5.9 %copy-start.18 = (s32[256]{0:T(256)S(1)}, s32[256]{0:T(256)}, u32[]{:S(2)}) copy-start(s32[256]{0:T(256)} %param.8) | copy-start | bytes 3076
  56.4 28.8 %all-to-all-start.1 = ((bf16[32,32,512]{2,1,0:T(8,128)(2,1)}), bf16[32,32,512]{2,1,0:T(8,128)(2,1)S(1)}, u32[]{:S(2)}, u32[]{:S(2)}) async-start(bf16[32,32,512]{2,1,0:T(8,128)(2,1)} %broadcast_select_fusion), calls=%async_computation.1 | async-start | bytes 2097152 | tf_op jit(solution)/shard_map/all_to_all | solution.py:32
  59.1 37.6 %all-gather.2.cloned.1.call-start = ((), (), s32[]{:S(2)}) async-start(), calls=%async_computation.4 | async-start | bytes 1310720 | tf_op jit(solution)/shard_map/all_gather | solution.py:42
  65.2 28.5 %copy-start.15 = (pred[256]{0:T(512)(128)(4,1)}, pred[256]{0:T(512)(128)(4,1)S(1)}, u32[]{:S(2)}) copy-start(pred[256]{0:T(512)(128)(4,1)S(1)} %compare_and_fusion.2) | copy-start | bytes 772
  93.7 2.0 copy-start.1
  95.7 0.6 copy-start.5
  95.7 0.7 copy-start.7
  95.7 0.7 copy-start.9
  96.6 3.2 copy-start.2
  96.7 3.2 copy-start.19
  99.2 2.2 copy-start.20
  99.2 2.1 copy-start.16
  99.8 1.6 copy-start.10
  99.8 1.6 copy-start.11
  99.8 1.6 copy-start.12
  99.8 1.6 copy-start.13
  172.0 7.2 %copy-start.6 = (bf16[256,256]{1,0:T(8,128)(2,1)S(1)}, bf16[256,256]{1,0:T(8,128)(2,1)}, u32[]{:S(2)}) copy-start(bf16[256,256]{1,0:T(8,128)(2,1)} %copy-done.5) | copy-start | bytes 393220
  172.0 7.2 %copy-start.8 = (bf16[256,256]{1,0:T(8,128)(2,1)S(1)}, bf16[256,256]{1,0:T(8,128)(2,1)}, u32[]{:S(2)}) copy-start(bf16[256,256]{1,0:T(8,128)(2,1)} %copy-done.7) | copy-start | bytes 393220
  172.0 185.6 %all-to-all-start.2 = ((f32[32,32,512]{2,1,0:T(8,128)}), f32[32,32,512]{2,1,0:T(8,128)}, u32[]{:S(2)}, u32[]{:S(2)}) async-start(f32[32,32,512]{2,1,0:T(8,128)} %scatter_fusion.1), calls=%async_computation.2 | async-start | bytes 4194304 | tf_op jit(solution)/shard_map/all_to_all | solution.py:66
  175.6 6.4 %copy-start.3 = (f32[256,256]{1,0:T(8,128)S(1)}, f32[256,256]{1,0:T(8,128)}, u32[]{:S(2)}) copy-start(f32[256,256]{1,0:T(8,128)} %get-tuple-element.5) | copy-start | bytes 786436
  175.6 6.4 %copy-start.4 = (f32[256,256]{1,0:T(8,128)S(1)}, f32[256,256]{1,0:T(8,128)}, u32[]{:S(2)}) copy-start(f32[256,256]{1,0:T(8,128)} %get-tuple-element.8) | copy-start | bytes 786436
  175.7 191.7 %reduce-scatter.2.cloned.1.call-start = ((), (), s32[]{:S(2)}) async-start(), calls=%async_computation.5 | async-start | bytes 1310720 | tf_op jit(solution)/shard_map/reduce_scatter | solution.py:54
Sparse Core Ops, SparseCore 0:
  61.5 19.8 all-gather.1
  182.2 34.1 reduce-scatter.1
where the time goes:
time: 388 us; the launch traced here: 385 us
  blocking collectives  184 us (47%)
  local copies, waits for them, and re-layouts  121 us (31%)
  other arithmetic  33.4 us (9%)
  waiting for transfers between devices  19.4 us (5%)
  between operations  14.5 us (4%)
  starting transfers between devices  6.57 us (2%)
  matrix products  5.73 us (1%)
    psum x1, blocking collectives, body(): relation_grad = lax.psum(local_rel, ('wide', 'narrow')).astype(jnp.bfloat16)  169 us
    scatter x1, local copies, waits for them, and re-layouts, body(): send_grads.at[owners, slot_rank]  64.1 us
    scatter x1, local copies, waits for them, and re-layouts, body(): jnp.zeros((device_count, capacity), jnp.int32).at[owners, slot_rank]  25.1 us
    all_to_all x1, waiting for transfers between devices, body(): lax.all_to_all(served, ('wide', 'narrow'), split_axis=0, concat_axis=0, t...  19.3 us
    all_to_all x1, blocking collectives, body(): lax.all_to_all(send_ids, ('wide', 'narrow'), split_axis=0, concat_axis=0,...  14.3 us
    scatter-add x1, other arithmetic, body(): entity_grad.at[asked_ids.reshape(-1)].add(back_grads.reshape(-1, row_width))  9.78 us
  transfers between devices with their start and end apart: 4, of which 1 were waited for; matrix products, arithmetic and copies ran while one was open for 10% of the time, Pallas kernels for 0%

commit v1 on v0

v1 whole, which is shorter than its diff:
```python
import jax
import jax.numpy as jnp
from jax import lax
from jax.sharding import PartitionSpec as P

AXES = ("wide", "narrow")


def swap_halves(rows):
    half_width = rows.shape[-1] // 2
    return jnp.concatenate([rows[..., half_width:], rows[..., :half_width]], axis=-1)


def slot_ranks(targets, count):
    onehot = (targets[:, None] == jnp.arange(count, dtype=jnp.int32)[None, :]).astype(jnp.int32)
    return jnp.sum((jnp.cumsum(onehot, axis=0) - onehot) * onehot, axis=1)


def split_dot(spec, onehot, values, parts=2):
    total = None
    rest = values
    for _ in range(parts):
        piece = rest.astype(jnp.bfloat16)
        rest = rest - piece.astype(jnp.float32)
        term = jnp.einsum(spec, onehot, piece, preferred_element_type=jnp.float32)
        total = term if total is None else total + term
    return total


def body(entity_table, relation_table, triple_rel, triple_owners, triple_local, negative_ids):
    wide_count = lax.axis_size("wide")
    narrow_count = lax.axis_size("narrow")
    device_count = wide_count * narrow_count
    triples = triple_rel.shape[0]
    row_width = entity_table.shape[1]
    entity_rows = entity_table.shape[0]
    capacity = max(2, 4 * triples // device_count)
    rel_capacity = max(1, 2 * triples // device_count)
    rel_per_group = relation_table.shape[0] // device_count

    owners = triple_owners.reshape(-1)
    local_rows = triple_local.reshape(-1)
    ent_pos = owners * capacity + slot_ranks(owners, device_count)
    rel_group = triple_rel // rel_per_group
    rel_pos = rel_group * rel_capacity + slot_ranks(rel_group, device_count)
    rel_local = triple_rel - rel_group * rel_per_group

    ent_place = jnp.arange(device_count * capacity, dtype=jnp.int32)[:, None] == ent_pos[None, :]
    rel_place = jnp.arange(device_count * rel_capacity, dtype=jnp.int32)[:, None] == rel_pos[None, :]
    send_ent_ids = jnp.sum(jnp.where(ent_place, local_rows[None, :], 0), axis=1)
    send_rel_ids = jnp.sum(jnp.where(rel_place, rel_local[None, :], 0), axis=1)
    send_ids = jnp.concatenate(
        [
            send_ent_ids.reshape(device_count, capacity),
            send_rel_ids.reshape(device_count, rel_capacity),
        ],
        axis=1,
    )
    recv_ids = lax.all_to_all(send_ids, AXES, split_axis=0, concat_axis=0, tiled=True)
    asked_ids = recv_ids[:, :capacity].reshape(-1)
    rel_ids_in = recv_ids[:, capacity:].reshape(-1)

    served = jnp.take(entity_table, asked_ids, axis=0).reshape(device_count, capacity, row_width)
    got_rows = lax.all_to_all(served, AXES, split_axis=0, concat_axis=0, tiled=True)
    got_rows = got_rows.reshape(device_count * capacity, row_width)
    ent_place_bf = ent_place.astype(jnp.bfloat16)
    fetched = jnp.einsum(
        "sj,sc->jc", ent_place_bf, got_rows, preferred_element_type=jnp.float32
    ).astype(jnp.bfloat16)
    fetched = fetched.reshape(triples, 2, row_width)
    head_rows = fetched[:, 0]
    tail_rows = fetched[:, 1]
    rel_rows = jnp.take(relation_table, triple_rel, axis=0)
    query = (
        0.5 * swap_halves(head_rows).astype(jnp.float32) * swap_halves(rel_rows).astype(jnp.float32)
    ).astype(jnp.bfloat16)
    positive = jnp.sum(query.astype(jnp.float32) * tail_rows.astype(jnp.float32), axis=1)

    own_negs = jnp.take(entity_table, negative_ids, axis=0)
    gathered = lax.all_gather(own_negs, "narrow", axis=0, tiled=True)
    group_neg = gathered.shape[0]
    scores = jnp.einsum("tc,kc->tk", query, gathered, preferred_element_type=jnp.float32)
    loss = jax.nn.softplus(-positive) + jnp.sum(jax.nn.softplus(scores), axis=1) / group_neg
    neg_weights = (jax.nn.sigmoid(scores) / group_neg).astype(jnp.bfloat16)
    pos_weight = -jax.nn.sigmoid(-positive)
    query_grad = pos_weight[:, None] * tail_rows.astype(jnp.float32) + jnp.dot(
        neg_weights, gathered, preferred_element_type=jnp.float32
    )
    tail_grad = pos_weight[:, None] * query.astype(jnp.float32)
    head_grad = 0.5 * swap_halves(query_grad) * rel_rows.astype(jnp.float32)
    rel_part = 0.5 * swap_halves(query_grad) * head_rows.astype(jnp.float32)

    group_query = lax.all_gather(query, "narrow", axis=0, tiled=True)
    own_scores = jnp.einsum("tc,kc->tk", group_query, own_negs, preferred_element_type=jnp.float32)
    own_weights = (jax.nn.sigmoid(own_scores) / group_neg).astype(jnp.bfloat16)
    neg_grad = jnp.einsum("tk,tc->kc", own_weights, group_query, preferred_element_type=jnp.float32)

    ent_grads = jnp.stack([head_grad, tail_grad], axis=1).reshape(2 * triples, row_width)
    send_ent = split_dot("sj,jc->sc", ent_place_bf, ent_grads, parts=3)
    send_rel = split_dot("sj,jc->sc", rel_place.astype(jnp.bfloat16), rel_part, parts=3)
    send_grads = jnp.concatenate(
        [
            send_ent.reshape(device_count, capacity, row_width),
            send_rel.reshape(device_count, rel_capacity, row_width),
        ],
        axis=1,
    )
    back_grads = lax.all_to_all(send_grads, AXES, split_axis=0, concat_axis=0, tiled=True)
    back_ent = back_grads[:, :capacity].reshape(-1, row_width)
    back_rel = back_grads[:, capacity:].reshape(-1, row_width)

    ids_all = jnp.concatenate([asked_ids, negative_ids])
    grads_all = jnp.concatenate([back_ent, neg_grad], axis=0)
    ent_onehot = (
        ids_all[:, None] == jnp.arange(entity_rows, dtype=jnp.int32)[None, :]
    ).astype(jnp.bfloat16)
    entity_grad = split_dot("se,sc->ec", ent_onehot, grads_all)

    rel_onehot = (
        rel_ids_in[:, None] == jnp.arange(rel_per_group, dtype=jnp.int32)[None, :]
    ).astype(jnp.bfloat16)
    own_rel_grad = split_dot("sr,sc->rc", rel_onehot, back_rel).astype(jnp.bfloat16)
    relation_grad = lax.all_gather(own_rel_grad, AXES, axis=0, tiled=True)
    return (entity_grad.astype(jnp.bfloat16), relation_grad, loss)


def solution(mesh):
    return jax.shard_map(
        body,
        mesh=mesh,
        in_specs=(
            P(AXES, None),
            P(),
            P(AXES),
            P(AXES, None),
            P(AXES, None),
            P(AXES),
        ),
        out_specs=(P(AXES, None), P(), P(AXES)),
        check_vma=False,
    )
```

time: 388 us -> 233 us (0.60)
  blocking collectives: 184 us -> 14.3 us
  waiting for transfers between devices: 19.4 us -> 138 us
  local copies, waits for them, and re-layouts: 121 us -> 26 us
  other arithmetic: 33.4 us -> 9.97 us
  matrix products: 5.73 us -> 22.1 us
    psum x1 -> x0, blocking collectives: 169 us -> none  [body(): relation_grad = lax.psum(local_rel, ('wide', 'narrow')).astype(jnp.bfloat16)]
    scatter x2 -> x0, local copies, waits for them, and re-layouts: 89.2 us -> none  [the longest x1 64.1 us: body(): send_grads.at[owners, slot_rank]]
    all_to_all x2, waiting for transfers between devices: 19.3 us -> 89.3 us  [the longest x1 70.2 us: body(): lax.all_to_all(send_grads, AXES, split_axis=0, concat_axis=0, tiled=True)]
    all_gather x0 -> x2, waiting for transfers between devices: none -> 48.2 us  [the longest x1 48.2 us: body(): relation_grad = lax.all_gather(own_rel_grad, AXES, axis=0, tiled=True)]
    scatter-add x3 -> x0, other arithmetic: 22.4 us -> none  [the longest x1 9.78 us: body(): entity_grad.at[asked_ids.reshape(-1)].add(back_grads.reshape(-1, row_width))]
    dot_general x1 -> x12, matrix products: 2.79 us -> 19.3 us  [the longest x10 14.5 us: split_dot(): term = jnp.einsum(spec, onehot, piece, preferred_element_type=jnp.float32)]
    gather x2 -> x1, local copies, waits for them, and re-layouts: 10.4 us -> 3.97 us  [body(): jnp.take(entity_table, asked_ids, axis=0)]
    unnamed x45 -> x46, local copies, waits for them, and re-layouts: 3.2 us -> 7.5 us
  transfers between devices with their start and end apart: 4 -> 5, of which waited for: 1 -> 3; matrix products, arithmetic and copies ran while one was open for 10% -> 12% of each run, Pallas kernels for 0% -> 0%
where the time goes in v1:
time: 233 us; the launch traced here: 232 us
  waiting for transfers between devices  138 us (59%)
  local copies, waits for them, and re-layouts  26 us (11%)
  matrix products  22.1 us (9%)
  blocking collectives  14.3 us (6%)
  between operations  14.2 us (6%)
  other arithmetic  9.97 us (4%)
  starting transfers between devices  7.57 us (3%)
    all_to_all x1, waiting for transfers between devices, body(): lax.all_to_all(send_grads, AXES, split_axis=0, concat_axis=0, tiled=True)  70.2 us
    all_gather x1, waiting for transfers between devices, body(): relation_grad = lax.all_gather(own_rel_grad, AXES, axis=0, tiled=True)  48.2 us
    all_to_all x1, waiting for transfers between devices, body(): lax.all_to_all(served, AXES, split_axis=0, concat_axis=0, tiled=True)  19.1 us
    dot_general x10, matrix products, split_dot(): term = jnp.einsum(spec, onehot, piece, preferred_element_type=jnp.float32)  14.5 us
    all_to_all x1, blocking collectives, body(): lax.all_to_all(send_ids, AXES, split_axis=0, concat_axis=0, tiled=True)  14.3 us
    unnamed x46, local copies, waits for them, and re-layouts  7.5 us
  transfers between devices with their start and end apart: 5, of which 3 were waited for; matrix products, arithmetic and copies ran while one was open for 12% of the time, Pallas kernels for 0%

profile of v1, /device:TPU:0, one launch (start us, length us, event | category | flops | bytes accessed | tf_op | source)
XLA Modules:
  0.0 232.4 jit_solution(16644380675345170120)
XLA Ops:
  7.2 1.0 copy.27
  8.4 0.7 multiply_subtract_fusion
  9.1 0.6 reduce-window.16
  10.1 0.6 copy-done.10
  10.9 0.8 copy.30
  11.9 1.2 reduce-window.14
  13.0 0.2 slice_reduce_fusion
  13.4 0.3 select_reduce_fusion
  13.9 14.3 %all_to_all.22 = s32[32,1,48]{2,1,0:T(1,128)S(1)} all-to-all(s32[32,1,48]{2,1,0:T(1,128)S(1)} %bitcast.102), channel_id=1, replica_groups=mesh['wide'=8,'narrow'=4] {'wide','narrow'}, dimensions={0} | all-to-all | bytes 12288 | tf_op jit(solution)/shard_map/all_to_all | solution.py:59
  28.3 4.0 %gather_fusion = bf16[1024,512]{1,0:T(8,128)(2,1)S(1)} fusion(bf16[2048,512]{1,0:T(8,128)(2,1)S(1)} %copy-done, s32[1024]{0:T(1024)S(1)} %broadcast_clamp_fusion), kind=kCustom, calls=%fused_computation | custom fusion | bytes 2101248 | tf_op jit(solution)/shard_map/jit(_take)/gather | solution.py:63
  32.3 1.2 broadcast_select_fusion
  33.5 3.4 %all-to-all-start.1 = ((bf16[32,32,512]{2,1,0:T(8,128)(2,1)}), bf16[32,32,512]{2,1,0:T(8,128)(2,1)}, u32[]{:S(2)}, u32[]{:S(2)}) async-start(bf16[32,32,512]{2,1,0:T(8,128)(2,1)} %broadcast_select_fusion), calls=%async_computation.1 | async-start | bytes 2097152 | tf_op jit(solution)/shard_map/all_to_all | solution.py:64
  36.9 0.2 all-gather.4.cloned.1.call-start
  37.1 1.2 gather_fusion.2
  38.3 0.8 broadcast_select_fusion.1
  39.2 3.9 %gather_fusion.1 = bf16[256,512]{1,0:T(8,128)(2,1)S(1)} fusion(bf16[4096,512]{1,0:T(8,128)(2,1)} %param.7, s32[1024]{0:T(1024)S(1)} %pad_clamp_fusion.1), kind=kCustom, calls=%fused_computation.1 | custom fusion | bytes 525312 | tf_op jit(solution)/shard_map/jit(_take)/gather | solution.py:73
  43.2 0.8 broadcast_select_fusion.2
  44.0 19.1 %all-to-all-done.1 = bf16[32,32,512]{2,1,0:T(8,128)(2,1)} async-done(((bf16[32,32,512]{2,1,0:T(8,128)(2,1)}), bf16[32,32,512]{2,1,0:T(8,128)(2,1)}, u32[]{:S(2)}, u32[]{:S(2)}) %all-to-all-start.1) | async-done | bytes 1048608 | tf_op jit(solution)/shard_map/all_to_all | solution.py:64
  63.1 2.0 fusion.14
  65.3 0.7 fusion.62
  66.2 0.8 slice_bitcast_fusion.3
  67.0 0.8 fusion.27
  67.7 2.3 fusion.18
  70.0 0.6 fusion.52
  70.6 0.5 convolution_add_fusion.2
  71.1 0.9 slice_bitcast_fusion.1
  72.5 0.8 copy.34
  73.3 1.7 reshape.305
  75.0 2.4 %fusion.5 = f32[1024,512]{1,0:T(8,128)S(1)} fusion(s32[512]{0:T(512)S(1)} %copy-done.13, f32[512,512]{1,0:T(8,128)} %reshape.305), kind=kOutput, calls=%fused_computation.17 | convolution fusion | flops 539230208 | bytes 3147776 | tf_op jit(solution)/shard_map/sj,jc->sc/dot_general | solution.py:25
  77.4 0.7 fusion.6
  78.4 0.3 fusion.34
  78.8 0.4 convolution_add_fusion.1
  79.1 0.4 convolution_add_fusion
  79.5 0.7 add_add_fusion
  80.2 2.1 pad_maximum_fusion
  82.3 3.7 %all-to-all-start.2 = ((f32[32,48,512]{2,1,0:T(8,128)}), f32[32,48,512]{2,1,0:T(8,128)}, u32[]{:S(2)}, u32[]{:S(2)}) async-start(f32[32,48,512]{2,1,0:T(8,128)} %pad_maximum_fusion), calls=%async_computation.2 | async-start | bytes 6291456 | tf_op jit(solution)/shard_map/all_to_all | solution.py:108
  86.0 0.7 all-gather.6.cloned.1.call-update
  86.7 0.3 all-gather.8.cloned.1.call-start
  87.1 70.2 %all-to-all-done.2 = f32[32,48,512]{2,1,0:T(8,128)} async-done(((f32[32,48,512]{2,1,0:T(8,128)}), f32[32,48,512]{2,1,0:T(8,128)}, u32[]{:S(2)}, u32[]{:S(2)}) %all-to-all-start.2) | async-done | bytes 3145760 | tf_op jit(solution)/shard_map/all_to_all | solution.py:108
  157.4 1.3 slice.85
  158.8 0.4 fusion.38
  159.2 1.0 fusion.16
  160.3 2.8 %fusion.17 = f32[256,512]{1,0:T(8,128)S(1)} fusion(bf16[1024,512]{1,0:T(8,128)(2,1)} %all-gather.6.cloned.1.call-done, bf16[256,512]{1,0:T(8,128)(2,1)S(1)} %copy-done.4), kind=kOutput, calls=%fused_computation.33 | convolution fusion | flops 538181632 | bytes 1835008 | tf_op jit(solution)/shard_map/tk,tc->kc/dot_general | solution.py:96
  163.2 1.8 slice.83
  165.0 3.3 %fusion = f32[2048,512]{1,0:T(8,128)S(1)} fusion(s32[1280]{0:T(1024)S(1)} %pad_add_fusion.1, f32[256,512]{1,0:T(8,128)S(1)} %fusion.17, f32[1024,512]{1,0:T(8,128)S(1)} %bitcast.96), kind=kOutput, calls=%fused_computation.4 | convolution fusion | flops 2690252800 | bytes 6820864 | tf_op jit(solution)/shard_map/se,sc->ec/dot_general | solution.py:25
  168.3 5.0 %add_convert_fusion = bf16[2048,512]{1,0:T(8,128)(2,1)} fusion(f32[2048,512]{1,0:T(8,128)S(1)} %fusion, s32[1280]{0:T(1024)S(1)} %pad_add_fusion.1, f32[256,512]{1,0:T(8,128)S(1)} %fusion.17, f32[1024,512]{1,0:T(8,128)S(1)} %bitcast.97), kind=kOutput, calls=%fused_computation.8 | convolution fusion | flops 2691694592 | bytes 8918016 | tf_op jit(solution)/shard_map/se,sc->ec/dot_general | solution.py:25
  173.2 48.2 %all-gather.8.cloned.1.call-done = bf16[4096,512]{1,0:T(8,128)(2,1)} async-done(((bf16[128,512]{1,0:T(8,128)(2,1)}), bf16[4096,512]{1,0:T(8,128)(2,1)}) %all-gather.8.cloned.1.call-update) | async-done | bytes 4194320 | tf_op jit(solution)/shard_map/all_gather | solution.py:123
  221.4 4.5 %copy.49 = bf16[4096,512]{1,0:T(8,128)(2,1)} copy(bf16[4096,512]{1,0:T(8,128)(2,1)} %all-gather.8.cloned.1.call-done) | data formatting | bytes 8388608
  (83 shorter events, 3.0 us)
Async XLA Ops:
  7.2 21.1 %copy-start = (bf16[2048,512]{1,0:T(8,128)(2,1)S(1)}, bf16[2048,512]{1,0:T(8,128)(2,1)}, u32[]{:S(2)}) copy-start(bf16[2048,512]{1,0:T(8,128)(2,1)} %param.6) | copy-start | bytes 6291460
  10.1 0.6 copy-start.10
  13.4 49.6 %copy-start.12 = (s32[512]{0:T(512)}, s32[512]{0:T(512)S(1)}, u32[]{:S(2)}) copy-start(s32[512]{0:T(512)S(1)} %multiply_add_fusion) | copy-start | bytes 6148
  32.3 4.8 %copy-start.14 = (s32[256]{0:T(256)S(1)}, s32[256]{0:T(256)}, u32[]{:S(2)}) copy-start(s32[256]{0:T(256)} %param.11) | copy-start | bytes 3076
  33.5 29.6 %all-to-all-start.1 = ((bf16[32,32,512]{2,1,0:T(8,128)(2,1)}), bf16[32,32,512]{2,1,0:T(8,128)(2,1)}, u32[]{:S(2)}, u32[]{:S(2)}) async-start(bf16[32,32,512]{2,1,0:T(8,128)(2,1)} %broadcast_select_fusion), calls=%async_computation.1 | async-start | bytes 2097152 | tf_op jit(solution)/shard_map/all_to_all | solution.py:64
  36.9 30.9 %all-gather.4.cloned.1.call-start = ((), (), s32[]{:S(2)}) async-start(), calls=%async_computation.3 | async-start | bytes 1310720 | tf_op jit(solution)/shard_map/all_gather | solution.py:80
  38.3 4.8 %copy-start.19 = (s32[256]{0:T(256)S(1)}, s32[256]{0:T(256)}, u32[]{:S(2)}) copy-start(s32[256]{0:T(256)} %param.8) | copy-start | bytes 3076
  43.2 22.1 %copy-start.17 = (pred[256]{0:T(512)(128)(4,1)}, pred[256]{0:T(512)(128)(4,1)S(1)}, u32[]{:S(2)}) copy-start(pred[256]{0:T(512)(128)(4,1)S(1)} %compare_and_fusion.2) | copy-start | bytes 772
  65.3 1.0 copy-start.5
  67.7 2.9 %copy-start.6 = (bf16[256,512]{1,0:T(8,128)(2,1)}, bf16[256,512]{1,0:T(8,128)(2,1)S(1)}, u32[]{:S(2)}) copy-start(bf16[256,512]{1,0:T(8,128)(2,1)S(1)} %get-tuple-element.6) | copy-start | bytes 786436
  67.7 2.3 copy-start.16
  67.7 2.9 %copy-start.20 = (bf16[1024,512]{1,0:T(8,128)(2,1)S(1)}, bf16[1024,512]{1,0:T(8,128)(2,1)}, u32[]{:S(2)}) copy-start(bf16[1024,512]{1,0:T(8,128)(2,1)} %all-gather.4.cloned.1.call-done) | copy-start | bytes 3145732
  70.6 1.4 copy-start.18
  71.1 1.1 copy-start.7
  71.1 1.1 copy-start.8
  71.1 1.2 copy-start.9
  72.5 2.5 %copy-start.13 = (s32[512]{0:T(512)S(1)}, s32[512]{0:T(512)}, u32[]{:S(2)}) copy-start(s32[512]{0:T(512)} %copy-done.12) | copy-start | bytes 6148
  75.0 2.4 %copy-start.1 = (f32[512,512]{1,0:T(8,128)S(1)}, f32[512,512]{1,0:T(8,128)}, u32[]{:S(2)}) copy-start(f32[512,512]{1,0:T(8,128)} %reshape.305) | copy-start | bytes 3145732
  77.4 1.0 copy-start.2
  77.4 1.0 copy-start.3
  77.4 1.0 copy-start.11
  82.3 75.1 %all-to-all-start.2 = ((f32[32,48,512]{2,1,0:T(8,128)}), f32[32,48,512]{2,1,0:T(8,128)}, u32[]{:S(2)}, u32[]{:S(2)}) async-start(f32[32,48,512]{2,1,0:T(8,128)} %pad_maximum_fusion), calls=%async_computation.2 | async-start | bytes 6291456 | tf_op jit(solution)/shard_map/all_to_all | solution.py:108
  86.0 74.4 %all-gather.6.cloned.1.call-start = ((), (), s32[]{:S(2)}) async-start(), calls=%async_computation.4 | async-start | bytes 1310720 | tf_op jit(solution)/shard_map/all_gather | solution.py:93
  86.7 134.7 %all-gather.8.cloned.1.call-start = ((), (), s32[]{:S(2)}) async-start(), calls=%async_computation.5 | async-start | bytes 4325376 | tf_op jit(solution)/shard_map/all_gather | solution.py:123
  158.7 1.6 copy-start.15
  158.7 1.6 copy-start.4
Sparse Core Ops, SparseCore 0:
  39.3 19.7 all-gather.3
  88.3 27.4 all-gather.5
  160.4 61.0 all-gather.7

commit v2 on v1

--- a/solution.py
+++ b/solution.py
@@ -42,7 +42,8 @@
     local_rows = triple_local.reshape(-1)
     ent_pos = owners * capacity + slot_ranks(owners, device_count)
     rel_group = triple_rel // rel_per_group
-    rel_pos = rel_group * rel_capacity + slot_ranks(rel_group, device_count)
+    rel_owner = (rel_group % wide_count) * narrow_count + rel_group // wide_count
+    rel_pos = rel_owner * rel_capacity + slot_ranks(rel_owner, device_count)
     rel_local = triple_rel - rel_group * rel_per_group
 
     ent_place = jnp.arange(device_count * capacity, dtype=jnp.int32)[:, None] == ent_pos[None, :]
@@ -96,8 +97,15 @@
     neg_grad = jnp.einsum("tk,tc->kc", own_weights, group_query, preferred_element_type=jnp.float32)
 
     ent_grads = jnp.stack([head_grad, tail_grad], axis=1).reshape(2 * triples, row_width)
-    send_ent = split_dot("sj,jc->sc", ent_place_bf, ent_grads, parts=3)
-    send_rel = split_dot("sj,jc->sc", rel_place.astype(jnp.bfloat16), rel_part, parts=3)
+    send_ent = jnp.einsum(
+        "sj,jc->sc", ent_place_bf, ent_grads.astype(jnp.bfloat16), preferred_element_type=jnp.float32
+    ).astype(jnp.bfloat16)
+    send_rel = jnp.einsum(
+        "sj,jc->sc",
+        rel_place.astype(jnp.bfloat16),
+        rel_part.astype(jnp.bfloat16),
+        preferred_element_type=jnp.float32,
+    ).astype(jnp.bfloat16)
     send_grads = jnp.concatenate(
         [
             send_ent.reshape(device_count, capacity, row_width),
@@ -109,18 +117,21 @@
     back_ent = back_grads[:, :capacity].reshape(-1, row_width)
     back_rel = back_grads[:, capacity:].reshape(-1, row_width)
 
-    ids_all = jnp.concatenate([asked_ids, negative_ids])
-    grads_all = jnp.concatenate([back_ent, neg_grad], axis=0)
-    ent_onehot = (
-        ids_all[:, None] == jnp.arange(entity_rows, dtype=jnp.int32)[None, :]
-    ).astype(jnp.bfloat16)
-    entity_grad = split_dot("se,sc->ec", ent_onehot, grads_all)
+    entity_iota = jnp.arange(entity_rows, dtype=jnp.int32)[None, :]
+    asked_onehot = (asked_ids[:, None] == entity_iota).astype(jnp.bfloat16)
+    neg_onehot = (negative_ids[:, None] == entity_iota).astype(jnp.bfloat16)
+    entity_grad = jnp.einsum(
+        "se,sc->ec", asked_onehot, back_ent, preferred_element_type=jnp.float32
+    ) + split_dot("se,sc->ec", neg_onehot, neg_grad)
 
     rel_onehot = (
         rel_ids_in[:, None] == jnp.arange(rel_per_group, dtype=jnp.int32)[None, :]
     ).astype(jnp.bfloat16)
-    own_rel_grad = split_dot("sr,sc->rc", rel_onehot, back_rel).astype(jnp.bfloat16)
-    relation_grad = lax.all_gather(own_rel_grad, AXES, axis=0, tiled=True)
+    own_rel_grad = jnp.einsum(
+        "sr,sc->rc", rel_onehot, back_rel, preferred_element_type=jnp.float32
+    ).astype(jnp.bfloat16)
+    relation_grad = lax.all_gather(own_rel_grad, "wide", axis=0, tiled=True)
+    relation_grad = lax.all_gather(relation_grad, "narrow", axis=0, tiled=True)
     return (entity_grad.astype(jnp.bfloat16), relation_grad, loss)
 
 

time: 233 us -> 225 us (0.966)
  matrix products: 22.1 us -> 16.4 us
    all_to_all x1, waiting for transfers between devices: 70.2 us -> 37.4 us  [body(): lax.all_to_all(send_grads, AXES, split_axis=0, concat_axis=0, tiled=True)]
    all_gather x1, waiting for transfers between devices: 0.02 us -> 16.9 us  [body(): group_query = lax.all_gather(query, 'narrow', axis=0, tiled=True)]
    all_gather x1 -> x2, waiting for transfers between devices: 48.2 us -> 64.7 us  [the longest x1 38.7 us: body(): relation_grad = lax.all_gather(own_rel_grad, 'wide', axis=0, tiled=True)]
    dot_general x10 -> x2, matrix products: 14.5 us -> 3.02 us  [split_dot(): term = jnp.einsum(spec, onehot, piece, preferred_element_type=jnp.float32)]
    dot_general x0 -> x4, matrix products: none -> 5.8 us  [the longest x1 2.69 us: body(): jnp.einsum('se,sc->ec', asked_onehot, back_ent, preferred_element_type=jn...]
    unnamed x46 -> x44, local copies, waits for them, and re-layouts: 7.5 us -> 7.59 us
  transfers between devices with their start and end apart: 5 -> 6, of which waited for: 3 -> 5; matrix products, arithmetic and copies ran while one was open for 12% -> 9% of each run, Pallas kernels for 0% -> 0%
where the time goes in v2:
time: 225 us
  waiting for transfers between devices  139 us (62%)
  local copies, waits for them, and re-layouts  24.4 us (11%)
  matrix products  16.4 us (7%)
  blocking collectives  14.3 us (6%)
  between operations  14.2 us (6%)
  other arithmetic  9.06 us (4%)
  starting transfers between devices  7.39 us (3%)
    all_gather x1, waiting for transfers between devices, body(): relation_grad = lax.all_gather(own_rel_grad, 'wide', axis=0, tiled=True)  38.7 us
    all_to_all x1, waiting for transfers between devices, body(): lax.all_to_all(send_grads, AXES, split_axis=0, concat_axis=0, tiled=True)  37.4 us
    all_gather x1, waiting for transfers between devices, body(): relation_grad = lax.all_gather(relation_grad, 'narrow', axis=0, tiled=True)  26.1 us
    all_to_all x1, waiting for transfers between devices, body(): lax.all_to_all(served, AXES, split_axis=0, concat_axis=0, tiled=True)  19.2 us
    all_gather x1, waiting for transfers between devices, body(): group_query = lax.all_gather(query, 'narrow', axis=0, tiled=True)  16.9 us
    all_to_all x1, blocking collectives, body(): lax.all_to_all(send_ids, AXES, split_axis=0, concat_axis=0, tiled=True)  14.3 us
    unnamed x44, local copies, waits for them, and re-layouts  7.59 us
  transfers between devices with their start and end apart: 6, of which 5 were waited for; matrix products, arithmetic and copies ran while one was open for 9% of the time, Pallas kernels for 0%

profile of v2, /device:TPU:0, one launch (start us, length us, event | category | flops | bytes accessed | tf_op | source)
XLA Modules:
  0.0 224.6 jit_solution(10145685051276539853)
XLA Ops:
  7.2 1.0 copy.27
  8.4 0.7 fusion.42
  9.1 0.6 reduce-window.16
  9.7 0.2 slice_reduce_fusion.1
  10.1 0.7 multiply_subtract_fusion
  10.9 0.4 copy-done.10
  11.4 1.2 reduce-window.14
  12.6 0.2 slice_reduce_fusion
  13.0 0.8 copy.30
  14.0 0.3 select_reduce_fusion
  14.4 14.3 %all_to_all.22 = s32[32,1,48]{2,1,0:T(1,128)S(1)} all-to-all(s32[32,1,48]{2,1,0:T(1,128)S(1)} %bitcast.96), channel_id=1, replica_groups=mesh['wide'=8,'narrow'=4] {'wide','narrow'}, dimensions={0} | all-to-all | bytes 12288 | tf_op jit(solution)/shard_map/all_to_all | solution.py:60
  28.8 4.0 %gather_fusion = bf16[1024,512]{1,0:T(8,128)(2,1)S(1)} fusion(bf16[2048,512]{1,0:T(8,128)(2,1)S(1)} %copy-done, s32[1024]{0:T(1024)S(1)} %broadcast_clamp_fusion), kind=kCustom, calls=%fused_computation | custom fusion | bytes 2101248 | tf_op jit(solution)/shard_map/jit(_take)/gather | solution.py:64
  32.8 1.2 broadcast_select_fusion
  34.0 3.4 %all-to-all-start.1 = ((bf16[32,32,512]{2,1,0:T(8,128)(2,1)}), bf16[32,32,512]{2,1,0:T(8,128)(2,1)}, u32[]{:S(2)}, u32[]{:S(2)}) async-start(bf16[32,32,512]{2,1,0:T(8,128)(2,1)} %broadcast_select_fusion), calls=%async_computation.1 | async-start | bytes 2097152 | tf_op jit(solution)/shard_map/all_to_all | solution.py:65
  37.5 1.2 gather_fusion.2
  38.7 0.8 broadcast_select_fusion.1
  39.5 3.9 %gather_fusion.1 = bf16[256,512]{1,0:T(8,128)(2,1)S(1)} fusion(bf16[4096,512]{1,0:T(8,128)(2,1)} %param.7, s32[1024]{0:T(1024)S(1)} %pad_clamp_fusion.1), kind=kCustom, calls=%fused_computation.1 | custom fusion | bytes 525312 | tf_op jit(solution)/shard_map/jit(_take)/gather | solution.py:74
  43.6 0.8 slice_bitcast_fusion.3
  44.4 19.2 %all-to-all-done.1 = bf16[32,32,512]{2,1,0:T(8,128)(2,1)} async-done(((bf16[32,32,512]{2,1,0:T(8,128)(2,1)}), bf16[32,32,512]{2,1,0:T(8,128)(2,1)}, u32[]{:S(2)}, u32[]{:S(2)}) %all-to-all-start.1) | async-done | bytes 1048608 | tf_op jit(solution)/shard_map/all_to_all | solution.py:65
  63.6 2.0 fusion.10
  65.6 0.2 reshape.301
  65.8 0.7 fusion.50
  66.6 0.7 slice_bitcast_fusion.5
  67.3 0.8 fusion.18
  68.1 2.3 %fusion.13 = (f32[256]{0:T(256)S(1)}, f32[256,1024]{1,0:T(8,128)S(1)}) fusion(bf16[256,512]{1,0:T(8,128)(2,1)S(1)} %get-tuple-element.4, bf16[1024,512]{1,0:T(8,128)(2,1)} %all-gather.5.cloned.1.call-done), kind=kOutput, calls=%fused_computation.27 | convolution fusion | flops 270270208 | bytes 2360320 | tf_op jit(solution)/shard_map/tc,kc->tk/dot_general | solution.py:83
  70.4 0.6 fusion.43
  71.0 0.5 convolution_add_fusion
  71.8 0.6 copy-done.4
  72.7 0.5 copy.34
  73.3 1.0 convert_element_type.142
  74.3 1.8 fusion.5
  76.0 0.3 convolution_convert_fusion
  76.4 1.3 pad_maximum_fusion
  77.7 3.7 %all-to-all-start.2 = ((bf16[32,48,512]{2,1,0:T(8,128)(2,1)}), bf16[32,48,512]{2,1,0:T(8,128)(2,1)}, u32[]{:S(2)}, u32[]{:S(2)}) async-start(bf16[32,48,512]{2,1,0:T(8,128)(2,1)} %pad_maximum_fusion), calls=%async_computation.2 | async-start | bytes 3145728 | tf_op jit(solution)/shard_map/all_to_all | solution.py:116
  81.5 37.4 %all-to-all-done.2 = bf16[32,48,512]{2,1,0:T(8,128)(2,1)} async-done(((bf16[32,48,512]{2,1,0:T(8,128)(2,1)}), bf16[32,48,512]{2,1,0:T(8,128)(2,1)}, u32[]{:S(2)}, u32[]{:S(2)}) %all-to-all-start.2) | async-done | bytes 1572896 | tf_op jit(solution)/shard_map/all_to_all | solution.py:116
  119.0 1.1 slice.85
  120.0 1.0 convolution_convert_fusion.1
  121.1 0.7 all-gather.7.cloned.1.call-update
  121.8 0.2 all-gather.11.cloned.1.call-start
  122.1 38.7 %all-gather.9.cloned.1.call-done = bf16[1024,512]{1,0:T(8,128)(2,1)} async-done(((bf16[128,512]{1,0:T(8,128)(2,1)}), bf16[1024,512]{1,0:T(8,128)(2,1)}) %all-gather.9.cloned.1.call-update) | async-done | bytes 1048592 | tf_op jit(solution)/shard_map/all_gather | solution.py:133
  160.8 16.9 %all-gather.7.cloned.1.call-done = bf16[1024,512]{1,0:T(8,128)(2,1)} async-done(((bf16[256,512]{1,0:T(8,128)(2,1)}), bf16[1024,512]{1,0:T(8,128)(2,1)}) %all-gather.7.cloned.1.call-update) | async-done | bytes 1048592 | tf_op jit(solution)/shard_map/all_gather | solution.py:94
  177.7 2.8 %fusion.12 = f32[256,512]{1,0:T(8,128)S(1)} fusion(bf16[1024,512]{1,0:T(8,128)(2,1)} %all-gather.7.cloned.1.call-done, bf16[256,512]{1,0:T(8,128)(2,1)S(1)} %copy-done.1), kind=kOutput, calls=%fused_computation.26 | convolution fusion | flops 538181632 | bytes 1835008 | tf_op jit(solution)/shard_map/tk,tc->kc/dot_general | solution.py:97
  180.6 0.8 fusion.2
  181.4 1.3 slice.83
  182.7 2.7 %fusion = f32[2048,512]{1,0:T(8,128)S(1)} fusion(bf16[1024,512]{1,0:T(8,128)(2,1)S(1)} %bitcast.91, s32[1024]{0:T(1024)S(1)} %eq.137), kind=kOutput, calls=%fused_computation.4 | convolution fusion | flops 2149580800 | bytes 5246976 | tf_op jit(solution)/shard_map/se,sc->ec/dot_general | solution.py:123
  185.4 2.2 add_convert_fusion
  187.6 26.1 %all-gather.11.cloned.1.call-done = bf16[4096,512]{1,0:T(8,128)(2,1)} async-done(((bf16[1024,512]{1,0:T(8,128)(2,1)}), bf16[4096,512]{1,0:T(8,128)(2,1)}) %all-gather.11.cloned.1.call-update) | async-done | bytes 4194320 | tf_op jit(solution)/shard_map/all_gather | solution.py:134
  213.6 4.5 %copy.49 = bf16[4096,512]{1,0:T(8,128)(2,1)} copy(bf16[4096,512]{1,0:T(8,128)(2,1)} %all-gather.11.cloned.1.call-done) | data formatting | bytes 8388608
  (79 shorter events, 2.5 us)
Async XLA Ops:
  7.2 21.7 %copy-start = (bf16[2048,512]{1,0:T(8,128)(2,1)S(1)}, bf16[2048,512]{1,0:T(8,128)(2,1)}, u32[]{:S(2)}) copy-start(bf16[2048,512]{1,0:T(8,128)(2,1)} %param.6) | copy-start | bytes 6291460
  10.8 0.6 copy-start.10
  13.0 15.8 %copy-start.12 = (s32[512]{0:T(512)}, s32[512]{0:T(512)S(1)}, u32[]{:S(2)}) copy-start(s32[512]{0:T(512)S(1)} %multiply_add_fusion) | copy-start | bytes 6148
  32.8 4.6 %copy-start.8 = (s32[256]{0:T(256)S(1)}, s32[256]{0:T(256)}, u32[]{:S(2)}) copy-start(s32[256]{0:T(256)} %param.11) | copy-start | bytes 3076
  34.0 29.6 %all-to-all-start.1 = ((bf16[32,32,512]{2,1,0:T(8,128)(2,1)}), bf16[32,32,512]{2,1,0:T(8,128)(2,1)}, u32[]{:S(2)}, u32[]{:S(2)}) async-start(bf16[32,32,512]{2,1,0:T(8,128)(2,1)} %broadcast_select_fusion), calls=%async_computation.1 | async-start | bytes 2097152 | tf_op jit(solution)/shard_map/all_to_all | solution.py:65
  37.4 2.1 copy-start.15
  37.4 30.7 %all-gather.5.cloned.1.call-start = ((), (), s32[]{:S(2)}) async-start(), calls=%async_computation.3 | async-start | bytes 1310720 | tf_op jit(solution)/shard_map/all_gather | solution.py:81
  39.5 24.1 %copy-start.13 = (s32[512]{0:T(512)S(1)}, s32[512]{0:T(512)}, u32[]{:S(2)}) copy-start(s32[512]{0:T(512)} %copy-done.12) | copy-start | bytes 6148
  39.5 24.0 %copy-start.17 = (pred[256]{0:T(512)(128)(4,1)}, pred[256]{0:T(512)(128)(4,1)S(1)}, u32[]{:S(2)}) copy-start(pred[256]{0:T(512)(128)(4,1)S(1)} %compare_and_fusion.2) | copy-start | bytes 772
  65.8 1.5 copy-start.3
  68.1 3.4 %copy-start.2 = (bf16[256,512]{1,0:T(8,128)(2,1)}, bf16[256,512]{1,0:T(8,128)(2,1)S(1)}, u32[]{:S(2)}) copy-start(bf16[256,512]{1,0:T(8,128)(2,1)S(1)} %get-tuple-element.4) | copy-start | bytes 786436
  68.1 2.3 %copy-start.16 = (f32[256]{0:T(256)S(1)}, f32[256]{0:T(256)}, u32[]{:S(2)}) copy-start(f32[256]{0:T(256)} %get-tuple-element.3) | copy-start | bytes 3076
  68.1 2.9 %copy-start.19 = (bf16[1024,512]{1,0:T(8,128)(2,1)S(1)}, bf16[1024,512]{1,0:T(8,128)(2,1)}, u32[]{:S(2)}) copy-start(bf16[1024,512]{1,0:T(8,128)(2,1)} %all-gather.5.cloned.1.call-done) | copy-start | bytes 3145732
  71.0 0.7 copy-start.18
  71.4 0.9 copy-start.4
  71.5 1.0 copy-start.5
  71.5 1.0 copy-start.6
  71.5 1.1 copy-start.7
  71.8 2.5 %copy-start.14 = (s32[512]{0:T(512)S(1)}, s32[512]{0:T(512)}, u32[]{:S(2)}) copy-start(s32[512]{0:T(512)} %copy-done.12) | copy-start | bytes 6148
  73.3 2.8 %copy-start.11 = (s32[256]{0:T(256)S(1)}, s32[256]{0:T(256)}, u32[]{:S(2)}) copy-start(s32[256]{0:T(256)} %copy-done.10) | copy-start | bytes 3076
  77.7 41.3 %all-to-all-start.2 = ((bf16[32,48,512]{2,1,0:T(8,128)(2,1)}), bf16[32,48,512]{2,1,0:T(8,128)(2,1)}, u32[]{:S(2)}, u32[]{:S(2)}) async-start(bf16[32,48,512]{2,1,0:T(8,128)(2,1)} %pad_maximum_fusion), calls=%async_computation.2 | async-start | bytes 3145728 | tf_op jit(solution)/shard_map/all_to_all | solution.py:116
  81.3 96.4 %copy-start.1 = (bf16[256,512]{1,0:T(8,128)(2,1)S(1)}, bf16[256,512]{1,0:T(8,128)(2,1)}, u32[]{:S(2)}) copy-start(bf16[256,512]{1,0:T(8,128)(2,1)} %broadcast_select_fusion.1) | copy-start | bytes 786436
  81.3 79.4 %all-gather.9.cloned.1.call-start = ((), (), s32[]{:S(2)}) async-start(), calls=%async_computation.5 | async-start | bytes 1179648 | tf_op jit(solution)/shard_map/all_gather | solution.py:133
  121.1 56.6 %all-gather.7.cloned.1.call-start = ((), (), s32[]{:S(2)}) async-start(), calls=%async_computation.4 | async-start | bytes 1310720 | tf_op jit(solution)/shard_map/all_gather | solution.py:94
  121.8 91.8 %all-gather.11.cloned.1.call-start = ((), (), s32[]{:S(2)}) async-start(), calls=%async_computation.6 | async-start | bytes 5242880 | tf_op jit(solution)/shard_map/all_gather | solution.py:134
  160.8 19.7 %copy-start.9 = (s32[256]{0:T(256)S(1)}, s32[256]{0:T(256)}, u32[]{:S(2)}) copy-start(s32[256]{0:T(256)} %param.11) | copy-start | bytes 3076
Sparse Core Ops, SparseCore 0:
  40.4 19.5 all-gather.4
  121.2 39.4 all-gather.8
  162.3 15.3 all-gather.6
  179.1 34.4 all-gather.10

commit v3 on v2

--- a/solution.py
+++ b/solution.py
@@ -14,17 +14,6 @@
 def slot_ranks(targets, count):
     onehot = (targets[:, None] == jnp.arange(count, dtype=jnp.int32)[None, :]).astype(jnp.int32)
     return jnp.sum((jnp.cumsum(onehot, axis=0) - onehot) * onehot, axis=1)
-
-
-def split_dot(spec, onehot, values, parts=2):
-    total = None
-    rest = values
-    for _ in range(parts):
-        piece = rest.astype(jnp.bfloat16)
-        rest = rest - piece.astype(jnp.float32)
-        term = jnp.einsum(spec, onehot, piece, preferred_element_type=jnp.float32)
-        total = term if total is None else total + term
-    return total
 
 
 def body(entity_table, relation_table, triple_rel, triple_owners, triple_local, negative_ids):
@@ -92,46 +81,49 @@
     rel_part = 0.5 * swap_halves(query_grad) * head_rows.astype(jnp.float32)
 
     group_query = lax.all_gather(query, "narrow", axis=0, tiled=True)
-    own_scores = jnp.einsum("tc,kc->tk", group_query, own_negs, preferred_element_type=jnp.float32)
-    own_weights = (jax.nn.sigmoid(own_scores) / group_neg).astype(jnp.bfloat16)
-    neg_grad = jnp.einsum("tk,tc->kc", own_weights, group_query, preferred_element_type=jnp.float32)
+    group_query, head_grad, tail_grad, rel_part = lax.optimization_barrier(
+        (group_query, head_grad, tail_grad, rel_part)
+    )
 
-    ent_grads = jnp.stack([head_grad, tail_grad], axis=1).reshape(2 * triples, row_width)
-    send_ent = jnp.einsum(
-        "sj,jc->sc", ent_place_bf, ent_grads.astype(jnp.bfloat16), preferred_element_type=jnp.float32
-    ).astype(jnp.bfloat16)
     send_rel = jnp.einsum(
         "sj,jc->sc",
         rel_place.astype(jnp.bfloat16),
         rel_part.astype(jnp.bfloat16),
         preferred_element_type=jnp.float32,
     ).astype(jnp.bfloat16)
-    send_grads = jnp.concatenate(
-        [
-            send_ent.reshape(device_count, capacity, row_width),
-            send_rel.reshape(device_count, rel_capacity, row_width),
-        ],
-        axis=1,
-    )
-    back_grads = lax.all_to_all(send_grads, AXES, split_axis=0, concat_axis=0, tiled=True)
-    back_ent = back_grads[:, :capacity].reshape(-1, row_width)
-    back_rel = back_grads[:, capacity:].reshape(-1, row_width)
+    back_rel = lax.all_to_all(
+        send_rel.reshape(device_count, rel_capacity, row_width), AXES, split_axis=0, concat_axis=0, tiled=True
+    ).reshape(-1, row_width)
+    rel_onehot = (
+        rel_ids_in[:, None] == jnp.arange(rel_per_group, dtype=jnp.int32)[None, :]
+    ).astype(jnp.bfloat16)
+    own_rel_grad = jnp.einsum(
+        "sr,sc->rc", rel_onehot, back_rel, preferred_element_type=jnp.float32
+    ).astype(jnp.bfloat16)
+
+    ent_grads = jnp.stack([head_grad, tail_grad], axis=1).reshape(2 * triples, row_width)
+    send_ent = jnp.einsum(
+        "sj,jc->sc", ent_place_bf, ent_grads.astype(jnp.bfloat16), preferred_element_type=jnp.float32
+    ).astype(jnp.bfloat16)
+    own_rel_grad, send_ent = lax.optimization_barrier((own_rel_grad, send_ent))
+    relation_grad = lax.all_gather(own_rel_grad, "wide", axis=0, tiled=True)
+    relation_grad = lax.all_gather(relation_grad, "narrow", axis=0, tiled=True)
+    back_ent = lax.all_to_all(
+        send_ent.reshape(device_count, capacity, row_width), AXES, split_axis=0, concat_axis=0, tiled=True
+    ).reshape(-1, row_width)
+
+    own_scores = jnp.einsum("tc,kc->tk", group_query, own_negs, preferred_element_type=jnp.float32)
+    own_weights = (jax.nn.sigmoid(own_scores) / group_neg).astype(jnp.bfloat16)
+    neg_grad = jnp.einsum("tk,tc->kc", own_weights, group_query, preferred_element_type=jnp.float32)
 
     entity_iota = jnp.arange(entity_rows, dtype=jnp.int32)[None, :]
     asked_onehot = (asked_ids[:, None] == entity_iota).astype(jnp.bfloat16)
     neg_onehot = (negative_ids[:, None] == entity_iota).astype(jnp.bfloat16)
     entity_grad = jnp.einsum(
         "se,sc->ec", asked_onehot, back_ent, preferred_element_type=jnp.float32
-    ) + split_dot("se,sc->ec", neg_onehot, neg_grad)
-
-    rel_onehot = (
-        rel_ids_in[:, None] == jnp.arange(rel_per_group, dtype=jnp.int32)[None, :]
-    ).astype(jnp.bfloat16)
-    own_rel_grad = jnp.einsum(
-        "sr,sc->rc", rel_onehot, back_rel, preferred_element_type=jnp.float32
-    ).astype(jnp.bfloat16)
-    relation_grad = lax.all_gather(own_rel_grad, "wide", axis=0, tiled=True)
-    relation_grad = lax.all_gather(relation_grad, "narrow", axis=0, tiled=True)
+    ) + jnp.einsum(
+        "se,sc->ec", neg_onehot, neg_grad.astype(jnp.bfloat16), preferred_element_type=jnp.float32
+    )
     return (entity_grad.astype(jnp.bfloat16), relation_grad, loss)
 
 

time: 225 us -> 199 us (0.88)
  waiting for transfers between devices: 139 us -> 105 us
  matrix products: 16.4 us -> 22 us
  starting transfers between devices: 7.39 us -> 11 us
  local copies, waits for them, and re-layouts: 24.4 us -> 22.1 us
    all_gather x1, waiting for transfers between devices: 26.1 us -> 1.24 us  [body(): relation_grad = lax.all_gather(relation_grad, 'narrow', axis=0, tiled=True)]
    all_gather x1, waiting for transfers between devices: 16.9 us -> 11.1 us  [body(): group_query = lax.all_gather(query, 'narrow', axis=0, tiled=True)]
    all_to_all x1 -> x2, starting transfers between devices: 3.66 us -> 8.23 us  [the longest x1 4.61 us: body(): lax.all_to_all(send_rel.reshape(device_count, rel_capacity, row_width), A...]
    dot_general x1, matrix products: 2.69 us -> 5.93 us  [body(): jnp.einsum('se,sc->ec', asked_onehot, back_ent, preferred_element_type=jn...]
    all_to_all x1 -> x2, waiting for transfers between devices: 37.4 us -> 34.8 us  [the longest x1 24.6 us: body(): lax.all_to_all(send_ent.reshape(device_count, capacity, row_width), AXES,...]
    dot_general x3 -> x2, matrix products: 5.82 us -> 6.11 us  [the longest x1 4.82 us: body(): jnp.einsum('se,sc->ec', neg_onehot, neg_grad.astype(jnp.bfloat16), prefer...]
    unnamed x44 -> x38, local copies, waits for them, and re-layouts: 7.59 us -> 7.54 us
  transfers between devices with their start and end apart: 6 -> 7, of which waited for: 5 -> 6; matrix products, arithmetic and copies ran while one was open for 9% -> 17% of each run, Pallas kernels for 0% -> 0%
where the time goes in v3:
time: 199 us; the launch traced here: 198 us
  waiting for transfers between devices  105 us (53%)
  local copies, waits for them, and re-layouts  22.1 us (11%)
  matrix products  22 us (11%)
  blocking collectives  14.3 us (7%)
  between operations  14.1 us (7%)
  starting transfers between devices  11 us (6%)
  other arithmetic  9.51 us (5%)
    all_gather x1, waiting for transfers between devices, body(): relation_grad = lax.all_gather(own_rel_grad, 'wide', axis=0, tiled=True)  38.8 us
    all_to_all x1, waiting for transfers between devices, body(): lax.all_to_all(send_ent.reshape(device_count, capacity, row_width), AXES,...  24.6 us
    all_to_all x1, waiting for transfers between devices, body(): lax.all_to_all(served, AXES, split_axis=0, concat_axis=0, tiled=True)  19.3 us
    all_to_all x1, blocking collectives, body(): lax.all_to_all(send_ids, AXES, split_axis=0, concat_axis=0, tiled=True)  14.3 us
    all_gather x1, waiting for transfers between devices, body(): group_query = lax.all_gather(query, 'narrow', axis=0, tiled=True)  11.1 us
    all_to_all x1, waiting for transfers between devices, body(): lax.all_to_all(send_rel.reshape(device_count, rel_capacity, row_width), A...  10.1 us
    unnamed x38, local copies, waits for them, and re-layouts  7.54 us
    dot_general x1, matrix products, body(): jnp.einsum('se,sc->ec', asked_onehot, back_ent, preferred_element_type=jn...  5.93 us
  transfers between devices with their start and end apart: 7, of which 6 were waited for; matrix products, arithmetic and copies ran while one was open for 17% of the time, Pallas kernels for 0%

profile of v3, /device:TPU:0, one launch (start us, length us, event | category | flops | bytes accessed | tf_op | source)
XLA Modules:
  0.0 198.3 jit_solution(10048832042513692776)
XLA Ops:
  7.2 1.0 copy.27
  8.1 0.1 eq.121
  8.4 0.7 fusion.30
  9.1 0.6 reduce-window.16
  9.7 0.2 slice_reduce_fusion.1
  10.1 0.7 multiply_subtract_fusion
  10.8 0.1 select_reduce_fusion.1
  11.0 0.3 copy-done.7
  11.3 1.2 reduce-window.14
  12.5 0.2 slice_reduce_fusion
  12.9 0.8 copy.30
  13.7 0.1 broadcast_in_dim.71
  13.9 0.3 select_reduce_fusion
  14.3 14.3 %all_to_all.27 = s32[32,1,48]{2,1,0:T(1,128)S(1)} all-to-all(s32[32,1,48]{2,1,0:T(1,128)S(1)} %bitcast.90), channel_id=1, replica_groups=mesh['wide'=8,'narrow'=4] {'wide','narrow'}, dimensions={0} | all-to-all | bytes 12288 | tf_op jit(solution)/shard_map/all_to_all | solution.py:49
  28.8 4.0 %gather_fusion = bf16[1024,512]{1,0:T(8,128)(2,1)S(1)} fusion(bf16[2048,512]{1,0:T(8,128)(2,1)S(1)} %copy-done, s32[1024]{0:T(1024)S(1)} %broadcast_clamp_fusion), kind=kCustom, calls=%fused_computation | custom fusion | bytes 2101248 | tf_op jit(solution)/shard_map/jit(_take)/gather | solution.py:53
  32.8 1.2 broadcast_select_fusion
  33.9 2.6 %all-to-all-start.1 = ((bf16[32,32,512]{2,1,0:T(8,128)(2,1)}), bf16[32,32,512]{2,1,0:T(8,128)(2,1)S(1)}, u32[]{:S(2)}, u32[]{:S(2)}) async-start(bf16[32,32,512]{2,1,0:T(8,128)(2,1)} %broadcast_select_fusion), calls=%async_computation.1 | async-start | bytes 2097152 | tf_op jit(solution)/shard_map/all_to_all | solution.py:54
  36.7 1.2 gather_fusion.2
  37.8 0.8 broadcast_select_fusion.1
  38.8 3.9 %gather_fusion.1 = bf16[256,512]{1,0:T(8,128)(2,1)S(1)} fusion(bf16[4096,512]{1,0:T(8,128)(2,1)} %param.7, s32[1024]{0:T(1024)S(1)} %pad_clamp_fusion.1), kind=kCustom, calls=%fused_computation.1 | custom fusion | bytes 525312 | tf_op jit(solution)/shard_map/jit(_take)/gather | solution.py:63
  42.8 0.7 fusion.37
  43.5 19.3 %all-to-all-done.1 = bf16[32,32,512]{2,1,0:T(8,128)(2,1)S(1)} async-done(((bf16[32,32,512]{2,1,0:T(8,128)(2,1)}), bf16[32,32,512]{2,1,0:T(8,128)(2,1)S(1)}, u32[]{:S(2)}, u32[]{:S(2)}) %all-to-all-start.1) | async-done | bytes 1048608 | tf_op jit(solution)/shard_map/all_to_all | solution.py:54
  62.8 2.2 %fusion.9 = bf16[512,512]{1,0:T(8,128)(2,1)} fusion(bf16[1024,512]{1,0:T(8,128)(2,1)S(1)} %bitcast.82, s32[512]{0:T(512)} %copy-done.9), kind=kOutput, calls=%fused_computation.19 | convolution fusion | flops 537657344 | bytes 1574912 | tf_op jit(solution)/shard_map/sj,sc->jc/dot_general | solution.py:57
  65.0 1.2 reshape.152
  66.3 0.7 fusion.35
  67.1 0.7 copy-done.2
  67.8 0.8 fusion.15
  68.7 2.4 %fusion.11 = (f32[256]{0:T(256)S(1)}, f32[256,1024]{1,0:T(8,128)S(1)}) fusion(bf16[256,512]{1,0:T(8,128)(2,1)} %get-tuple-element.16, bf16[1024,512]{1,0:T(8,128)(2,1)} %all-gather.7.cloned.1.call-done), kind=kOutput, calls=%fused_computation.25 | convolution fusion | flops 270270208 | bytes 2360320 | tf_op jit(solution)/shard_map/tc,kc->tk/dot_general | solution.py:72
  71.1 0.6 fusion.31
  71.8 0.5 convolution_add_fusion
  72.5 0.9 convert_multiply_fusion.3
  73.3 11.1 %all-gather.5.cloned.1.call-done = bf16[1024,512]{1,0:T(8,128)(2,1)} async-done(((bf16[256,512]{1,0:T(8,128)(2,1)}), bf16[1024,512]{1,0:T(8,128)(2,1)}) %all-gather.5.cloned.1.call-update) | async-done | bytes 1048592 | tf_op jit(solution)/shard_map/all_gather | solution.py:83
  84.5 1.1 convolution_convert_fusion
  85.6 4.6 %all-to-all-start.2 = ((bf16[32,16,512]{2,1,0:T(8,128)(2,1)}), bf16[32,16,512]{2,1,0:T(8,128)(2,1)S(1)}, u32[]{:S(2)}, u32[]{:S(2)}) async-start(bf16[32,16,512]{2,1,0:T(8,128)(2,1)} %bitcast.10), calls=%async_computation.2 | async-start | bytes 1048576 | tf_op jit(solution)/shard_map/all_to_all | solution.py:94
  90.4 1.0 pad_maximum_fusion
  91.4 0.5 copy.34
  91.9 1.0 convert_element_type.93
  92.9 2.7 %fusion.4 = bf16[1024,512]{1,0:T(8,128)(2,1)} fusion(bf16[512,512]{1,0:T(8,128)(2,1)} %convert_element_type.93, s32[512]{0:T(512)S(1)} %copy-done.10), kind=kOutput, calls=%fused_computation.13 | convolution fusion | flops 537919488 | bytes 1574912 | tf_op jit(solution)/shard_map/sj,jc->sc/dot_general | solution.py:105
  95.7 10.1 %all-to-all-done.2 = bf16[32,16,512]{2,1,0:T(8,128)(2,1)S(1)} async-done(((bf16[32,16,512]{2,1,0:T(8,128)(2,1)}), bf16[32,16,512]{2,1,0:T(8,128)(2,1)S(1)}, u32[]{:S(2)}, u32[]{:S(2)}) %all-to-all-start.2) | async-done | bytes 524320 | tf_op jit(solution)/shard_map/all_to_all | solution.py:94
  105.8 1.0 convolution_convert_fusion.2
  106.9 38.8 %all-gather.9.cloned.1.call-done = bf16[1024,512]{1,0:T(8,128)(2,1)} async-done(((bf16[128,512]{1,0:T(8,128)(2,1)}), bf16[1024,512]{1,0:T(8,128)(2,1)}) %all-gather.9.cloned.1.call-update) | async-done | bytes 1048592 | tf_op jit(solution)/shard_map/all_gather | solution.py:109
  145.7 3.6 %all-to-all-start.3 = ((bf16[32,32,512]{2,1,0:T(8,128)(2,1)}), bf16[32,32,512]{2,1,0:T(8,128)(2,1)}, u32[]{:S(2)}, u32[]{:S(2)}) async-start(bf16[32,32,512]{2,1,0:T(8,128)(2,1)} %bitcast.83), calls=%async_computation.3 | async-start | bytes 2097152 | tf_op jit(solution)/shard_map/all_to_all | solution.py:111
  149.4 1.3 fusion.10
  150.7 24.6 %all-to-all-done.3 = bf16[32,32,512]{2,1,0:T(8,128)(2,1)} async-done(((bf16[32,32,512]{2,1,0:T(8,128)(2,1)}), bf16[32,32,512]{2,1,0:T(8,128)(2,1)}, u32[]{:S(2)}, u32[]{:S(2)}) %all-to-all-start.3) | async-done | bytes 1048608 | tf_op jit(solution)/shard_map/all_to_all | solution.py:111
  175.3 5.9 %fusion = f32[2048,512]{1,0:T(8,128)} fusion(bf16[1024,512]{1,0:T(8,128)(2,1)} %bitcast.15, s32[1024]{0:T(1024)S(1)} %eq.137), kind=kOutput, calls=%fused_computation.4 | convolution fusion | flops 2149580800 | bytes 5246976 | tf_op jit(solution)/shard_map/se,sc->ec/dot_general | solution.py:122
  181.2 4.8 %add_convert_fusion = bf16[2048,512]{1,0:T(8,128)(2,1)} fusion(f32[2048,512]{1,0:T(8,128)} %fusion, bf16[1024,256]{1,0:T(8,128)(2,1)} %fusion.10, bf16[1024,512]{1,0:T(8,128)(2,1)S(1)} %copy-done.4, s32[256]{0:T(256)S(1)} %copy-done.12), kind=kOutput, calls=%fused_computation.5 | convolution fusion | flops 808058880 | bytes 7865344 | tf_op jit(solution)/shard_map/se,sc->ec/dot_general | solution.py:124
  186.1 1.2 all-gather.11.cloned.1.call-done
  187.3 4.5 %copy.51 = bf16[4096,512]{1,0:T(8,128)(2,1)} copy(bf16[4096,512]{1,0:T(8,128)(2,1)} %all-gather.11.cloned.1.call-done) | data formatting | bytes 8388608
  (71 shorter events, 1.8 us)
Async XLA Ops:
  7.2 21.6 %copy-start = (bf16[2048,512]{1,0:T(8,128)(2,1)S(1)}, bf16[2048,512]{1,0:T(8,128)(2,1)}, u32[]{:S(2)}) copy-start(bf16[2048,512]{1,0:T(8,128)(2,1)} %param.6) | copy-start | bytes 6291460
  10.8 0.6 copy-start.7
  12.9 19.8 %copy-start.9 = (s32[512]{0:T(512)}, s32[512]{0:T(512)S(1)}, u32[]{:S(2)}) copy-start(s32[512]{0:T(512)S(1)} %multiply_add_fusion) | copy-start | bytes 6148
  32.7 3.9 %copy-start.11 = (s32[256]{0:T(256)S(1)}, s32[256]{0:T(256)}, u32[]{:S(2)}) copy-start(s32[256]{0:T(256)} %param.11) | copy-start | bytes 3076
  33.9 28.8 %all-to-all-start.1 = ((bf16[32,32,512]{2,1,0:T(8,128)(2,1)}), bf16[32,32,512]{2,1,0:T(8,128)(2,1)S(1)}, u32[]{:S(2)}, u32[]{:S(2)}) async-start(bf16[32,32,512]{2,1,0:T(8,128)(2,1)} %broadcast_select_fusion), calls=%async_computation.1 | async-start | bytes 2097152 | tf_op jit(solution)/shard_map/all_to_all | solution.py:54
  36.6 2.1 %copy-start.13 = (s32[256]{0:T(256)S(1)}, s32[256]{0:T(256)}, u32[]{:S(2)}) copy-start(s32[256]{0:T(256)} %param.8) | copy-start | bytes 3076
  36.6 32.1 %all-gather.7.cloned.1.call-start = ((), (), s32[]{:S(2)}) async-start(), calls=%async_computation.5 | async-start | bytes 1310720 | tf_op jit(solution)/shard_map/all_gather | solution.py:70
  38.7 45.8 %all-gather.5.cloned.1.call-start = ((), (), s32[]{:S(2)}) async-start(), calls=%async_computation.4 | async-start | bytes 1310720 | tf_op jit(solution)/shard_map/all_gather | solution.py:83
  38.7 4.0 %copy-start.14 = (pred[256]{0:T(512)(128)(4,1)}, pred[256]{0:T(512)(128)(4,1)S(1)}, u32[]{:S(2)}) copy-start(pred[256]{0:T(512)(128)(4,1)S(1)} %compare_and_fusion.2) | copy-start | bytes 772
  66.3 1.5 copy-start.6
  67.0 0.8 copy-start.2
  68.6 3.0 %copy-start.1 = (bf16[256,512]{1,0:T(8,128)(2,1)S(1)}, bf16[256,512]{1,0:T(8,128)(2,1)}, u32[]{:S(2)}) copy-start(bf16[256,512]{1,0:T(8,128)(2,1)} %get-tuple-element.16) | copy-start | bytes 786436
  68.7 3.1 %copy-start.3 = (bf16[256,1,512]{2,1,0:T(2,128)(2,1)S(1)}, bf16[256,1,512]{2,1,0:T(2,128)(2,1)}, u32[]{:S(2)}) copy-start(bf16[256,1,512]{2,1,0:T(2,128)(2,1)} %copy-done.2) | copy-start | bytes 786436
  68.7 3.1 %copy-start.16 = (bf16[1024,512]{1,0:T(8,128)(2,1)S(1)}, bf16[1024,512]{1,0:T(8,128)(2,1)}, u32[]{:S(2)}) copy-start(bf16[1024,512]{1,0:T(8,128)(2,1)} %all-gather.7.cloned.1.call-done) | copy-start | bytes 3145732
  71.8 0.7 copy-start.15
  72.3 12.2 %copy-start.8 = (s32[256]{0:T(256)S(1)}, s32[256]{0:T(256)}, u32[]{:S(2)}) copy-start(s32[256]{0:T(256)} %copy-done.7) | copy-start | bytes 3076
  85.6 7.4 %copy-start.10 = (s32[512]{0:T(512)S(1)}, s32[512]{0:T(512)}, u32[]{:S(2)}) copy-start(s32[512]{0:T(512)} %copy-done.9) | copy-start | bytes 6148
  85.6 20.2 %all-to-all-start.2 = ((bf16[32,16,512]{2,1,0:T(8,128)(2,1)}), bf16[32,16,512]{2,1,0:T(8,128)(2,1)S(1)}, u32[]{:S(2)}, u32[]{:S(2)}) async-start(bf16[32,16,512]{2,1,0:T(8,128)(2,1)} %bitcast.10), calls=%async_computation.2 | async-start | bytes 1048576 | tf_op jit(solution)/shard_map/all_to_all | solution.py:94
  90.2 55.5 %all-gather.9.cloned.1.call-start = ((), (), s32[]{:S(2)}) async-start(), calls=%async_computation.6 | async-start | bytes 1179648 | tf_op jit(solution)/shard_map/all_gather | solution.py:109
  95.7 53.7 %copy-start.5 = (bf16[256,512]{1,0:T(8,128)(2,1)S(1)}, bf16[256,512]{1,0:T(8,128)(2,1)}, u32[]{:S(2)}) copy-start(bf16[256,512]{1,0:T(8,128)(2,1)} %broadcast_select_fusion.1) | copy-start | bytes 786436
  106.8 42.6 %copy-start.4 = (bf16[1024,512]{1,0:T(8,128)(2,1)S(1)}, bf16[1024,512]{1,0:T(8,128)(2,1)}, u32[]{:S(2)}) copy-start(bf16[1024,512]{1,0:T(8,128)(2,1)} %all-gather.5.cloned.1.call-done) | copy-start | bytes 3145732
  106.8 80.5 %all-gather.11.cloned.1.call-start = ((), (), s32[]{:S(2)}) async-start(), calls=%async_computation.7 | async-start | bytes 5242880 | tf_op jit(solution)/shard_map/all_gather | solution.py:110
  145.7 29.6 %all-to-all-start.3 = ((bf16[32,32,512]{2,1,0:T(8,128)(2,1)}), bf16[32,32,512]{2,1,0:T(8,128)(2,1)}, u32[]{:S(2)}, u32[]{:S(2)}) async-start(bf16[32,32,512]{2,1,0:T(8,128)(2,1)} %bitcast.83), calls=%async_computation.3 | async-start | bytes 2097152 | tf_op jit(solution)/shard_map/all_to_all | solution.py:111
  175.3 5.9 %copy-start.12 = (s32[256]{0:T(256)S(1)}, s32[256]{0:T(256)}, u32[]{:S(2)}) copy-start(s32[256]{0:T(256)} %param.11) | copy-start | bytes 3076
Sparse Core Ops, SparseCore 0:
  39.0 19.8 all-gather.6
  68.8 15.6 all-gather.4
  107.0 38.6 all-gather.8
  147.1 40.1 all-gather.10

commit v4 on v3

--- a/solution.py
+++ b/solution.py
@@ -31,8 +31,7 @@
     local_rows = triple_local.reshape(-1)
     ent_pos = owners * capacity + slot_ranks(owners, device_count)
     rel_group = triple_rel // rel_per_group
-    rel_owner = (rel_group % wide_count) * narrow_count + rel_group // wide_count
-    rel_pos = rel_owner * rel_capacity + slot_ranks(rel_owner, device_count)
+    rel_pos = rel_group * rel_capacity + slot_ranks(rel_group, device_count)
     rel_local = triple_rel - rel_group * rel_per_group
 
     ent_place = jnp.arange(device_count * capacity, dtype=jnp.int32)[:, None] == ent_pos[None, :]
@@ -81,9 +80,6 @@
     rel_part = 0.5 * swap_halves(query_grad) * head_rows.astype(jnp.float32)
 
     group_query = lax.all_gather(query, "narrow", axis=0, tiled=True)
-    group_query, head_grad, tail_grad, rel_part = lax.optimization_barrier(
-        (group_query, head_grad, tail_grad, rel_part)
-    )
 
     send_rel = jnp.einsum(
         "sj,jc->sc",
@@ -105,9 +101,8 @@
     send_ent = jnp.einsum(
         "sj,jc->sc", ent_place_bf, ent_grads.astype(jnp.bfloat16), preferred_element_type=jnp.float32
     ).astype(jnp.bfloat16)
-    own_rel_grad, send_ent = lax.optimization_barrier((own_rel_grad, send_ent))
-    relation_grad = lax.all_gather(own_rel_grad, "wide", axis=0, tiled=True)
-    relation_grad = lax.all_gather(relation_grad, "narrow", axis=0, tiled=True)
+    own_rel_grad, send_ent, group_query = lax.optimization_barrier((own_rel_grad, send_ent, group_query))
+    relation_grad = lax.all_gather(own_rel_grad, AXES, axis=0, tiled=True)
     back_ent = lax.all_to_all(
         send_ent.reshape(device_count, capacity, row_width), AXES, split_axis=0, concat_axis=0, tiled=True
     ).reshape(-1, row_width)

time: 199 us -> 169 us (0.85)
  waiting for transfers between devices: 105 us -> 74.2 us
    all_gather x2 -> x1, waiting for transfers between devices: 40 us -> 16.9 us  [body(): relation_grad = lax.all_gather(own_rel_grad, AXES, axis=0, tiled=True)]
    all_gather x1, waiting for transfers between devices: 11.1 us -> 0.01 us  [body(): group_query = lax.all_gather(query, 'narrow', axis=0, tiled=True)]
    all_to_all x1, waiting for transfers between devices: 24.6 us -> 30.8 us  [body(): lax.all_to_all(send_ent.reshape(device_count, capacity, row_width), AXES,...]
    all_to_all x1, waiting for transfers between devices: 10.1 us -> 7.24 us  [body(): lax.all_to_all(send_rel.reshape(device_count, rel_capacity, row_width), A...]
    unnamed x38 -> x36, local copies, waits for them, and re-layouts: 7.54 us -> 7.6 us
  transfers between devices with their start and end apart: 7 -> 6, of which waited for: 6 -> 4; matrix products, arithmetic and copies ran while one was open for 17% -> 23% of each run, Pallas kernels for 0% -> 0%
where the time goes in v4:
time: 169 us; the launch traced here: 168 us
  waiting for transfers between devices  74.2 us (44%)
  local copies, waits for them, and re-layouts  23.2 us (14%)
  matrix products  21.7 us (13%)
  blocking collectives  14.3 us (8%)
  between operations  14.1 us (8%)
  starting transfers between devices  10.8 us (6%)
  other arithmetic  10.1 us (6%)
    all_to_all x1, waiting for transfers between devices, body(): lax.all_to_all(send_ent.reshape(device_count, capacity, row_width), AXES,...  30.8 us
    all_to_all x1, waiting for transfers between devices, body(): lax.all_to_all(served, AXES, split_axis=0, concat_axis=0, tiled=True)  19.2 us
    all_gather x1, waiting for transfers between devices, body(): relation_grad = lax.all_gather(own_rel_grad, AXES, axis=0, tiled=True)  16.9 us
    all_to_all x1, blocking collectives, body(): lax.all_to_all(send_ids, AXES, split_axis=0, concat_axis=0, tiled=True)  14.3 us
    unnamed x36, local copies, waits for them, and re-layouts  7.6 us
    all_to_all x1, waiting for transfers between devices, body(): lax.all_to_all(send_rel.reshape(device_count, rel_capacity, row_width), A...  7.24 us
    dot_general x1, matrix products, body(): jnp.einsum('se,sc->ec', asked_onehot, back_ent, preferred_element_type=jn...  5.93 us
    dot_general x1, matrix products, body(): jnp.einsum('se,sc->ec', neg_onehot, neg_grad.astype(jnp.bfloat16), prefer...  4.83 us
  transfers between devices with their start and end apart: 6, of which 4 were waited for; matrix products, arithmetic and copies ran while one was open for 23% of the time, Pallas kernels for 0%

profile of v4, /device:TPU:0, one launch (start us, length us, event | category | flops | bytes accessed | tf_op | source)
XLA Modules:
  0.0 168.3 jit_solution(13193015994181580754)
XLA Ops:
  7.2 1.0 copy.27
  8.1 0.1 eq.119
  8.4 0.7 multiply_subtract_fusion
  9.1 0.6 reduce-window.16
  9.7 0.2 slice_reduce_fusion.1
  10.1 0.1 select_reduce_fusion.1
  10.2 0.4 copy-done.4
  10.8 1.2 reduce-window.14
  11.9 0.2 slice_reduce_fusion
  12.3 0.8 copy.30
  13.3 0.3 select_reduce_fusion
  13.7 14.3 %all_to_all.27 = s32[32,1,48]{2,1,0:T(1,128)S(1)} all-to-all(s32[32,1,48]{2,1,0:T(1,128)S(1)} %bitcast.95), channel_id=1, replica_groups=mesh['wide'=8,'narrow'=4] {'wide','narrow'}, dimensions={0} | all-to-all | bytes 12288 | tf_op jit(solution)/shard_map/all_to_all | solution.py:48
  28.2 4.0 %gather_fusion = bf16[1024,512]{1,0:T(8,128)(2,1)S(1)} fusion(bf16[2048,512]{1,0:T(8,128)(2,1)S(1)} %copy-done, s32[1024]{0:T(1024)S(1)} %broadcast_clamp_fusion), kind=kCustom, calls=%fused_computation | custom fusion | bytes 2101248 | tf_op jit(solution)/shard_map/jit(_take)/gather | solution.py:52
  32.1 1.2 broadcast_select_fusion
  33.3 3.4 %all-to-all-start.1 = ((bf16[32,32,512]{2,1,0:T(8,128)(2,1)}), bf16[32,32,512]{2,1,0:T(8,128)(2,1)}, u32[]{:S(2)}, u32[]{:S(2)}) async-start(bf16[32,32,512]{2,1,0:T(8,128)(2,1)} %broadcast_select_fusion), calls=%async_computation.1 | async-start | bytes 2097152 | tf_op jit(solution)/shard_map/all_to_all | solution.py:53
  36.8 1.2 gather_fusion.2
  38.0 0.8 broadcast_select_fusion.1
  38.9 3.9 %gather_fusion.1 = bf16[256,512]{1,0:T(8,128)(2,1)S(1)} fusion(bf16[4096,512]{1,0:T(8,128)(2,1)} %param.7, s32[1024]{0:T(1024)S(1)} %pad_clamp_fusion.1), kind=kCustom, calls=%fused_computation.1 | custom fusion | bytes 525312 | tf_op jit(solution)/shard_map/jit(_take)/gather | solution.py:62
  42.9 0.8 broadcast_select_fusion.2
  43.7 19.2 %all-to-all-done.1 = bf16[32,32,512]{2,1,0:T(8,128)(2,1)} async-done(((bf16[32,32,512]{2,1,0:T(8,128)(2,1)}), bf16[32,32,512]{2,1,0:T(8,128)(2,1)}, u32[]{:S(2)}, u32[]{:S(2)}) %all-to-all-start.1) | async-done | bytes 1048608 | tf_op jit(solution)/shard_map/all_to_all | solution.py:53
  62.9 2.0 %fusion.9 = bf16[512,512]{1,0:T(8,128)(2,1)S(1)} fusion(bf16[1024,512]{1,0:T(8,128)(2,1)} %bitcast.7, s32[512]{0:T(512)S(1)} %multiply_add_fusion), kind=kOutput, calls=%fused_computation.19 | convolution fusion | flops 537657344 | bytes 1574912 | tf_op jit(solution)/shard_map/sj,sc->jc/dot_general | solution.py:56
  64.9 0.2 reshape.301
  65.1 0.7 fusion.39
  65.9 0.2 copy-done.3
  66.1 0.8 slice_bitcast_fusion.3
  66.8 1.4 fusion.15
  68.3 2.3 %fusion.11 = (f32[256]{0:T(256)S(1)}, f32[256,1024]{1,0:T(8,128)S(1)}) fusion(bf16[256,512]{1,0:T(8,128)(2,1)} %get-tuple-element.10, bf16[1024,512]{1,0:T(8,128)(2,1)} %all-gather.4.cloned.1.call-done), kind=kOutput, calls=%fused_computation.25 | convolution fusion | flops 270270208 | bytes 2360320 | tf_op jit(solution)/shard_map/tc,kc->tk/dot_general | solution.py:71
  70.6 0.6 fusion.34
  71.2 0.5 copy-done.11
  71.8 0.5 convolution_add_fusion
  72.4 1.1 convolution_convert_fusion
  73.6 3.5 %all-to-all-start.2 = ((bf16[32,16,512]{2,1,0:T(8,128)(2,1)}), bf16[32,16,512]{2,1,0:T(8,128)(2,1)S(1)}, u32[]{:S(2)}, u32[]{:S(2)}) async-start(bf16[32,16,512]{2,1,0:T(8,128)(2,1)} %bitcast.10), calls=%async_computation.2 | async-start | bytes 1048576 | tf_op jit(solution)/shard_map/all_to_all | solution.py:90
  77.2 0.7 slice.67
  77.9 1.4 eq.139
  79.2 1.1 multiply_convert_fusion.2
  80.4 0.8 fusion.19
  81.2 0.5 copy.34
  81.8 1.0 convert_element_type.140
  82.8 2.7 %fusion.4 = bf16[1024,512]{1,0:T(8,128)(2,1)} fusion(bf16[512,512]{1,0:T(8,128)(2,1)} %convert_element_type.140, s32[512]{0:T(512)S(1)} %copy-done.8), kind=kOutput, calls=%fused_computation.13 | convolution fusion | flops 537919488 | bytes 1574912 | tf_op jit(solution)/shard_map/sj,jc->sc/dot_general | solution.py:101
  85.5 7.2 %all-to-all-done.2 = bf16[32,16,512]{2,1,0:T(8,128)(2,1)S(1)} async-done(((bf16[32,16,512]{2,1,0:T(8,128)(2,1)}), bf16[32,16,512]{2,1,0:T(8,128)(2,1)S(1)}, u32[]{:S(2)}, u32[]{:S(2)}) %all-to-all-start.2) | async-done | bytes 524320 | tf_op jit(solution)/shard_map/all_to_all | solution.py:90
  92.8 1.0 convolution_convert_fusion.2
  93.8 3.7 %all-to-all-start.3 = ((bf16[32,32,512]{2,1,0:T(8,128)(2,1)}), bf16[32,32,512]{2,1,0:T(8,128)(2,1)}, u32[]{:S(2)}, u32[]{:S(2)}) async-start(bf16[32,32,512]{2,1,0:T(8,128)(2,1)} %bitcast.90), calls=%async_computation.3 | async-start | bytes 2097152 | tf_op jit(solution)/shard_map/all_to_all | solution.py:106
  97.6 1.3 fusion.10
  98.9 30.8 %all-to-all-done.3 = bf16[32,32,512]{2,1,0:T(8,128)(2,1)} async-done(((bf16[32,32,512]{2,1,0:T(8,128)(2,1)}), bf16[32,32,512]{2,1,0:T(8,128)(2,1)}, u32[]{:S(2)}, u32[]{:S(2)}) %all-to-all-start.3) | async-done | bytes 1048608 | tf_op jit(solution)/shard_map/all_to_all | solution.py:106
  129.7 5.9 %fusion = f32[2048,512]{1,0:T(8,128)} fusion(bf16[1024,512]{1,0:T(8,128)(2,1)} %bitcast.20, s32[1024]{0:T(1024)S(1)} %eq.135), kind=kOutput, calls=%fused_computation.4 | convolution fusion | flops 2149580800 | bytes 5246976 | tf_op jit(solution)/shard_map/se,sc->ec/dot_general | solution.py:117
  135.6 4.8 %add_convert_fusion = bf16[2048,512]{1,0:T(8,128)(2,1)} fusion(f32[2048,512]{1,0:T(8,128)} %fusion, bf16[1024,256]{1,0:T(8,128)(2,1)} %fusion.10, bf16[1024,512]{1,0:T(8,128)(2,1)S(1)} %copy-done.1, s32[256]{0:T(256)S(1)} %copy-done.10), kind=kOutput, calls=%fused_computation.5 | convolution fusion | flops 808058880 | bytes 7865344 | tf_op jit(solution)/shard_map/se,sc->ec/dot_general | solution.py:119
  140.4 16.9 %all-gather.8.cloned.1.call-done = bf16[4096,512]{1,0:T(8,128)(2,1)} async-done(((bf16[128,512]{1,0:T(8,128)(2,1)}), bf16[4096,512]{1,0:T(8,128)(2,1)}) %all-gather.8.cloned.1.call-update) | async-done | bytes 4194320 | tf_op jit(solution)/shard_map/all_gather | solution.py:105
  157.3 4.5 %copy.49 = bf16[4096,512]{1,0:T(8,128)(2,1)} copy(bf16[4096,512]{1,0:T(8,128)(2,1)} %all-gather.8.cloned.1.call-done) | data formatting | bytes 8388608
  (65 shorter events, 1.6 us)
Async XLA Ops:
  7.2 21.0 %copy-start = (bf16[2048,512]{1,0:T(8,128)(2,1)S(1)}, bf16[2048,512]{1,0:T(8,128)(2,1)}, u32[]{:S(2)}) copy-start(bf16[2048,512]{1,0:T(8,128)(2,1)} %param.6) | copy-start | bytes 6291460
  10.1 0.6 copy-start.4
  12.3 50.6 %copy-start.7 = (s32[512]{0:T(512)}, s32[512]{0:T(512)S(1)}, u32[]{:S(2)}) copy-start(s32[512]{0:T(512)S(1)} %multiply_add_fusion) | copy-start | bytes 6148
  32.1 4.6 %copy-start.9 = (s32[256]{0:T(256)S(1)}, s32[256]{0:T(256)}, u32[]{:S(2)}) copy-start(s32[256]{0:T(256)} %param.11) | copy-start | bytes 3076
  33.3 29.6 %all-to-all-start.1 = ((bf16[32,32,512]{2,1,0:T(8,128)(2,1)}), bf16[32,32,512]{2,1,0:T(8,128)(2,1)}, u32[]{:S(2)}, u32[]{:S(2)}) async-start(bf16[32,32,512]{2,1,0:T(8,128)(2,1)} %broadcast_select_fusion), calls=%async_computation.1 | async-start | bytes 2097152 | tf_op jit(solution)/shard_map/all_to_all | solution.py:53
  36.7 31.5 %all-gather.4.cloned.1.call-start = ((), (), s32[]{:S(2)}) async-start(), calls=%async_computation.4 | async-start | bytes 1310720 | tf_op jit(solution)/shard_map/all_gather | solution.py:69
  38.0 4.9 %copy-start.14 = (s32[256]{0:T(256)S(1)}, s32[256]{0:T(256)}, u32[]{:S(2)}) copy-start(s32[256]{0:T(256)} %param.8) | copy-start | bytes 3076
  38.8 54.9 %all-gather.6.cloned.1.call-start = ((), (), s32[]{:S(2)}) async-start(), calls=%async_computation.5 | async-start | bytes 1310720 | tf_op jit(solution)/shard_map/all_gather | solution.py:82
  42.9 22.2 %copy-start.13 = (pred[256]{0:T(512)(128)(4,1)}, pred[256]{0:T(512)(128)(4,1)S(1)}, u32[]{:S(2)}) copy-start(pred[256]{0:T(512)(128)(4,1)S(1)} %compare_and_fusion.2) | copy-start | bytes 772
  65.1 1.0 copy-start.3
  68.2 2.4 %copy-start.12 = (f32[256]{0:T(256)S(1)}, f32[256]{0:T(256)}, u32[]{:S(2)}) copy-start(f32[256]{0:T(256)} %get-tuple-element.9) | copy-start | bytes 3076
  68.3 3.5 %copy-start.15 = (bf16[1024,512]{1,0:T(8,128)(2,1)S(1)}, bf16[1024,512]{1,0:T(8,128)(2,1)}, u32[]{:S(2)}) copy-start(bf16[1024,512]{1,0:T(8,128)(2,1)} %all-gather.4.cloned.1.call-done) | copy-start | bytes 3145732
  71.2 0.5 copy-start.11
  71.8 0.7 copy-start.5
  73.6 19.2 %all-to-all-start.2 = ((bf16[32,16,512]{2,1,0:T(8,128)(2,1)}), bf16[32,16,512]{2,1,0:T(8,128)(2,1)S(1)}, u32[]{:S(2)}, u32[]{:S(2)}) async-start(bf16[32,16,512]{2,1,0:T(8,128)(2,1)} %bitcast.10), calls=%async_computation.2 | async-start | bytes 1048576 | tf_op jit(solution)/shard_map/all_to_all | solution.py:90
  77.1 80.2 %all-gather.8.cloned.1.call-start = ((), (), s32[]{:S(2)}) async-start(), calls=%async_computation.6 | async-start | bytes 4325376 | tf_op jit(solution)/shard_map/all_gather | solution.py:105
  80.4 2.4 %copy-start.8 = (s32[512]{0:T(512)S(1)}, s32[512]{0:T(512)}, u32[]{:S(2)}) copy-start(s32[512]{0:T(512)} %copy-done.7) | copy-start | bytes 6148
  81.8 11.0 %copy-start.6 = (s32[512]{0:T(512)S(1)}, s32[512]{0:T(512)}, u32[]{:S(2)}) copy-start(s32[512]{0:T(512)} %eq.139) | copy-start | bytes 6148
  85.5 12.1 %copy-start.2 = (bf16[256,512]{1,0:T(8,128)(2,1)S(1)}, bf16[256,512]{1,0:T(8,128)(2,1)}, u32[]{:S(2)}) copy-start(bf16[256,512]{1,0:T(8,128)(2,1)} %broadcast_select_fusion.1) | copy-start | bytes 786436
  93.8 3.8 %copy-start.1 = (bf16[1024,512]{1,0:T(8,128)(2,1)S(1)}, bf16[1024,512]{1,0:T(8,128)(2,1)}, u32[]{:S(2)}) copy-start(bf16[1024,512]{1,0:T(8,128)(2,1)} %all-gather.6.cloned.1.call-done) | copy-start | bytes 3145732
  93.8 35.9 %all-to-all-start.3 = ((bf16[32,32,512]{2,1,0:T(8,128)(2,1)}), bf16[32,32,512]{2,1,0:T(8,128)(2,1)}, u32[]{:S(2)}, u32[]{:S(2)}) async-start(bf16[32,32,512]{2,1,0:T(8,128)(2,1)} %bitcast.90), calls=%async_computation.3 | async-start | bytes 2097152 | tf_op jit(solution)/shard_map/all_to_all | solution.py:106
  129.7 5.9 %copy-start.10 = (s32[256]{0:T(256)S(1)}, s32[256]{0:T(256)}, u32[]{:S(2)}) copy-start(s32[256]{0:T(256)} %param.11) | copy-start | bytes 3076
Sparse Core Ops, SparseCore 0:
  39.1 19.7 all-gather.3
  68.4 19.8 all-gather.5
  93.9 63.3 all-gather.7

commit v5 on v4

--- a/solution.py
+++ b/solution.py
@@ -26,6 +26,7 @@
     capacity = max(2, 4 * triples // device_count)
     rel_capacity = max(1, 2 * triples // device_count)
     rel_per_group = relation_table.shape[0] // device_count
+    assert rel_per_group <= 256
 
     owners = triple_owners.reshape(-1)
     local_rows = triple_local.reshape(-1)
@@ -37,19 +38,17 @@
     ent_place = jnp.arange(device_count * capacity, dtype=jnp.int32)[:, None] == ent_pos[None, :]
     rel_place = jnp.arange(device_count * rel_capacity, dtype=jnp.int32)[:, None] == rel_pos[None, :]
     send_ent_ids = jnp.sum(jnp.where(ent_place, local_rows[None, :], 0), axis=1)
-    send_rel_ids = jnp.sum(jnp.where(rel_place, rel_local[None, :], 0), axis=1)
-    send_ids = jnp.concatenate(
-        [
-            send_ent_ids.reshape(device_count, capacity),
-            send_rel_ids.reshape(device_count, rel_capacity),
-        ],
-        axis=1,
+    recv_ids = lax.all_to_all(
+        send_ent_ids.reshape(device_count, capacity), AXES, split_axis=0, concat_axis=0, tiled=True
     )
-    recv_ids = lax.all_to_all(send_ids, AXES, split_axis=0, concat_axis=0, tiled=True)
-    asked_ids = recv_ids[:, :capacity].reshape(-1)
-    rel_ids_in = recv_ids[:, capacity:].reshape(-1)
+    asked_ids = recv_ids.reshape(-1)
 
-    served = jnp.take(entity_table, asked_ids, axis=0).reshape(device_count, capacity, row_width)
+    entity_iota = jnp.arange(entity_rows, dtype=jnp.int32)[None, :]
+    asked_onehot = (asked_ids[:, None] == entity_iota).astype(jnp.bfloat16)
+    served = jnp.einsum(
+        "se,ec->sc", asked_onehot, entity_table, preferred_element_type=jnp.float32
+    ).astype(jnp.bfloat16)
+    served = served.reshape(device_count, capacity, row_width)
     got_rows = lax.all_to_all(served, AXES, split_axis=0, concat_axis=0, tiled=True)
     got_rows = got_rows.reshape(device_count * capacity, row_width)
     ent_place_bf = ent_place.astype(jnp.bfloat16)
@@ -87,9 +86,15 @@
         rel_part.astype(jnp.bfloat16),
         preferred_element_type=jnp.float32,
     ).astype(jnp.bfloat16)
-    back_rel = lax.all_to_all(
-        send_rel.reshape(device_count, rel_capacity, row_width), AXES, split_axis=0, concat_axis=0, tiled=True
-    ).reshape(-1, row_width)
+    send_rel_ids = jnp.sum(jnp.where(rel_place, rel_local[None, :], 0), axis=1)
+    id_row = jnp.zeros((device_count, 1, row_width), jnp.bfloat16)
+    id_row = id_row.at[:, 0, :rel_capacity].set(
+        send_rel_ids.reshape(device_count, rel_capacity).astype(jnp.bfloat16)
+    )
+    send_rel = jnp.concatenate([send_rel.reshape(device_count, rel_capacity, row_width), id_row], axis=1)
+    back_rel = lax.all_to_all(send_rel, AXES, split_axis=0, concat_axis=0, tiled=True)
+    rel_ids_in = back_rel[:, rel_capacity, :rel_capacity].astype(jnp.int32).reshape(-1)
+    back_rel = back_rel[:, :rel_capacity].reshape(-1, row_width)
     rel_onehot = (
         rel_ids_in[:, None] == jnp.arange(rel_per_group, dtype=jnp.int32)[None, :]
     ).astype(jnp.bfloat16)
@@ -111,8 +116,6 @@
     own_weights = (jax.nn.sigmoid(own_scores) / group_neg).astype(jnp.bfloat16)
     neg_grad = jnp.einsum("tk,tc->kc", own_weights, group_query, preferred_element_type=jnp.float32)
 
-    entity_iota = jnp.arange(entity_rows, dtype=jnp.int32)[None, :]
-    asked_onehot = (asked_ids[:, None] == entity_iota).astype(jnp.bfloat16)
     neg_onehot = (negative_ids[:, None] == entity_iota).astype(jnp.bfloat16)
     entity_grad = jnp.einsum(
         "se,sc->ec", asked_onehot, back_ent, preferred_element_type=jnp.float32

time: 169 us -> 175 us (1.036)
  waiting for transfers between devices: 74.2 us -> 89.7 us
  blocking collectives: 14.3 us -> 0 us
  starting transfers between devices: 10.8 us -> 18.6 us
  local copies, waits for them, and re-layouts: 23.2 us -> 18.6 us
    all_to_all x1 -> x2, waiting for transfers between devices: 7.24 us -> 22.8 us  [the longest x1 17.5 us: body(): lax.all_to_all(send_rel, AXES, split_axis=0, concat_axis=0, tiled=True)]
    all_to_all x1 -> x0, blocking collectives: 14.3 us -> none  [body(): lax.all_to_all(send_ids, AXES, split_axis=0, concat_axis=0, tiled=True)]
    all_to_all x1 -> x2, starting transfers between devices: 3.54 us -> 11 us  [the longest x1 7.33 us: body(): lax.all_to_all(send_ent_ids.reshape(device_count, capacity), AXES, split_...]
    gather x1 -> x0, local copies, waits for them, and re-layouts: 3.97 us -> none  [body(): jnp.take(entity_table, asked_ids, axis=0)]
    dot_general x0 -> x1, matrix products: none -> 3.35 us  [body(): jnp.einsum('se,ec->sc', asked_onehot, entity_table, preferred_element_typ...]
    unnamed x36 -> x48, local copies, waits for them, and re-layouts: 7.6 us -> 7.66 us
  transfers between devices with their start and end apart: 6 -> 7, of which waited for: 4 -> 5; matrix products, arithmetic and copies ran while one was open for 23% -> 21% of each run, Pallas kernels for 0% -> 0%
where the time goes in v5:
time: 175 us; the launch traced here: 174 us
  waiting for transfers between devices  89.7 us (51%)
  matrix products  23.2 us (13%)
  local copies, waits for them, and re-layouts  18.6 us (11%)
  starting transfers between devices  18.6 us (11%)
  between operations  14.2 us (8%)
  other arithmetic  9.66 us (6%)
    all_to_all x1, waiting for transfers between devices, body(): lax.all_to_all(send_ent.reshape(device_count, capacity, row_width), AXES,...  30.5 us
    all_to_all x1, waiting for transfers between devices, body(): lax.all_to_all(served, AXES, split_axis=0, concat_axis=0, tiled=True)  18.8 us
    all_gather x1, waiting for transfers between devices, body(): relation_grad = lax.all_gather(own_rel_grad, AXES, axis=0, tiled=True)  17.6 us
    all_to_all x1, waiting for transfers between devices, body(): lax.all_to_all(send_rel, AXES, split_axis=0, concat_axis=0, tiled=True)  17.5 us
    unnamed x48, local copies, waits for them, and re-layouts  7.66 us
    all_to_all x1, starting transfers between devices, body(): lax.all_to_all(send_ent_ids.reshape(device_count, capacity), AXES, split_...  7.33 us
    dot_general x1, matrix products, body(): jnp.einsum('se,sc->ec', asked_onehot, back_ent, preferred_element_type=jn...  5.93 us
    all_to_all x1, waiting for transfers between devices, body(): lax.all_to_all(send_ent_ids.reshape(device_count, capacity), AXES, split_...  5.25 us
  transfers between devices with their start and end apart: 7, of which 5 were waited for; matrix products, arithmetic and copies ran while one was open for 21% of the time, Pallas kernels for 0%

profile of v5, /device:TPU:0, one launch (start us, length us, event | category | flops | bytes accessed | tf_op | source)
XLA Modules:
  0.0 173.9 jit_solution(3229333693187501312)
XLA Ops:
  7.2 1.0 copy.29
  8.4 1.2 reduce-window.14
  9.6 0.2 slice_reduce_fusion
  10.0 0.8 copy.32
  11.0 0.3 select_reduce_fusion
  11.3 0.7 all_to_all.15
  12.0 7.3 %all-to-all-start = ((s32[32,1,32]{2,1,0:T(1,128)}), s32[32,1,32]{2,1,0:T(1,128)S(1)}, u32[]{:S(2)}, u32[]{:S(2)}) async-start(s32[32,1,32]{2,1,0:T(1,128)} %all_to_all.15), calls=%async_computation | async-start | bytes 32768 | tf_op jit(solution)/shard_map/all_to_all | solution.py:41
  19.3 0.7 compare_select_fusion.2
  20.0 1.2 gather_fusion.1
  21.2 5.3 %all-to-all-done = s32[32,1,32]{2,1,0:T(1,128)S(1)} async-done(((s32[32,1,32]{2,1,0:T(1,128)}), s32[32,1,32]{2,1,0:T(1,128)S(1)}, u32[]{:S(2)}, u32[]{:S(2)}) %all-to-all-start) | async-done | bytes 4128 | tf_op jit(solution)/shard_map/all_to_all | solution.py:41
  26.4 0.5 broadcast.213
  26.9 0.7 reduce.13
  27.7 3.3 %fusion.7 = bf16[1024,512]{1,0:T(8,128)(2,1)} fusion(bf16[2048,512]{1,0:T(8,128)(2,1)S(1)} %copy-done, s32[1024]{0:T(1024)S(1)} %eq.123), kind=kOutput, calls=%fused_computation.16 | convolution fusion | flops 2150105088 | bytes 3149824 | tf_op jit(solution)/shard_map/se,ec->sc/dot_general | solution.py:48
  31.0 3.5 %all-to-all-start.1 = ((bf16[32,32,512]{2,1,0:T(8,128)(2,1)}), bf16[32,32,512]{2,1,0:T(8,128)(2,1)}, u32[]{:S(2)}, u32[]{:S(2)}) async-start(bf16[32,32,512]{2,1,0:T(8,128)(2,1)} %bitcast.3), calls=%async_computation.1 | async-start | bytes 2097152 | tf_op jit(solution)/shard_map/all_to_all | solution.py:52
  34.6 0.8 broadcast_select_fusion
  35.6 0.6 reduce-window.16
  36.2 0.2 slice_reduce_fusion.1
  36.7 0.4 copy-done.7
  37.2 3.9 %gather_fusion = bf16[256,512]{1,0:T(8,128)(2,1)S(1)} fusion(bf16[4096,512]{1,0:T(8,128)(2,1)} %param.9, s32[1024]{0:T(1024)S(1)} %pad_clamp_fusion.1), kind=kCustom, calls=%fused_computation | custom fusion | bytes 525312 | tf_op jit(solution)/shard_map/jit(_take)/gather | solution.py:61
  41.2 0.8 broadcast_select_fusion.1
  42.0 18.8 %all-to-all-done.1 = bf16[32,32,512]{2,1,0:T(8,128)(2,1)} async-done(((bf16[32,32,512]{2,1,0:T(8,128)(2,1)}), bf16[32,32,512]{2,1,0:T(8,128)(2,1)}, u32[]{:S(2)}, u32[]{:S(2)}) %all-to-all-start.1) | async-done | bytes 1048608 | tf_op jit(solution)/shard_map/all_to_all | solution.py:52
  60.7 2.0 %fusion.13 = bf16[512,512]{1,0:T(8,128)(2,1)S(1)} fusion(bf16[1024,512]{1,0:T(8,128)(2,1)} %bitcast.4, s32[512]{0:T(512)S(1)} %multiply_add_fusion), kind=kOutput, calls=%fused_computation.23 | convolution fusion | flops 537657344 | bytes 1574912 | tf_op jit(solution)/shard_map/sj,sc->jc/dot_general | solution.py:55
  62.7 0.2 reshape.307
  63.0 0.7 fusion.45
  63.9 0.8 slice_bitcast_fusion.3
  64.7 1.4 fusion.20
  66.1 2.3 %fusion.15 = (f32[256]{0:T(256)S(1)}, f32[256,1024]{1,0:T(8,128)S(1)}) fusion(bf16[256,512]{1,0:T(8,128)(2,1)} %get-tuple-element.22, bf16[1024,512]{1,0:T(8,128)(2,1)} %all-gather.4.cloned.1.call-done), kind=kOutput, calls=%fused_computation.29 | convolution fusion | flops 270270208 | bytes 2360320 | tf_op jit(solution)/shard_map/tc,kc->tk/dot_general | solution.py:70
  68.4 0.6 fusion.40
  69.0 0.6 copy-done.13
  69.6 0.5 convolution_add_fusion
  70.3 0.3 convolution_convert_fusion
  70.7 0.9 fusion.19
  71.6 3.7 %all-to-all-start.2 = ((bf16[32,17,512]{2,1,0:T(8,128)(2,1)}), bf16[32,17,512]{2,1,0:T(8,128)(2,1)}, u32[]{:S(2)}, u32[]{:S(2)}) async-start(bf16[32,17,512]{2,1,0:T(8,128)(2,1)} %fusion.19), calls=%async_computation.2 | async-start | bytes 1572864 | tf_op jit(solution)/shard_map/all_to_all | solution.py:95
  75.3 0.2 all-gather.8.cloned.1.call-start
  75.9 0.5 copy.37
  76.5 0.2 convert_element_type.169
  76.7 1.7 fusion.8
  78.4 17.5 %all-to-all-done.2 = bf16[32,17,512]{2,1,0:T(8,128)(2,1)} async-done(((bf16[32,17,512]{2,1,0:T(8,128)(2,1)}), bf16[32,17,512]{2,1,0:T(8,128)(2,1)}, u32[]{:S(2)}, u32[]{:S(2)}) %all-to-all-start.2) | async-done | bytes 557088 | tf_op jit(solution)/shard_map/all_to_all | solution.py:95
  95.9 0.9 fusion.39
  96.8 1.1 slice.96
  97.9 1.0 convolution_convert_fusion.2
  99.0 3.8 %all-to-all-start.3 = ((bf16[32,32,512]{2,1,0:T(8,128)(2,1)}), bf16[32,32,512]{2,1,0:T(8,128)(2,1)}, u32[]{:S(2)}, u32[]{:S(2)}) async-start(bf16[32,32,512]{2,1,0:T(8,128)(2,1)} %bitcast.87), calls=%async_computation.3 | async-start | bytes 2097152 | tf_op jit(solution)/shard_map/all_to_all | solution.py:111
  102.8 1.3 fusion.14
  104.1 30.5 %all-to-all-done.3 = bf16[32,32,512]{2,1,0:T(8,128)(2,1)} async-done(((bf16[32,32,512]{2,1,0:T(8,128)(2,1)}), bf16[32,32,512]{2,1,0:T(8,128)(2,1)}, u32[]{:S(2)}, u32[]{:S(2)}) %all-to-all-start.3) | async-done | bytes 1048608 | tf_op jit(solution)/shard_map/all_to_all | solution.py:111
  134.6 5.9 %fusion = f32[2048,512]{1,0:T(8,128)} fusion(bf16[1024,512]{1,0:T(8,128)(2,1)} %bitcast.17, s32[1024]{0:T(1024)S(1)} %copy-done.16), kind=kOutput, calls=%fused_computation.3 | convolution fusion | flops 2149580800 | bytes 5246976 | tf_op jit(solution)/shard_map/se,sc->ec/dot_general | solution.py:120
  140.5 4.8 %add_convert_fusion = bf16[2048,512]{1,0:T(8,128)(2,1)} fusion(f32[2048,512]{1,0:T(8,128)} %fusion, bf16[1024,256]{1,0:T(8,128)(2,1)} %fusion.14, bf16[1024,512]{1,0:T(8,128)(2,1)S(1)} %copy-done.1, s32[256]{0:T(256)S(1)} %copy-done.12), kind=kOutput, calls=%fused_computation.5 | convolution fusion | flops 808058880 | bytes 7865344 | tf_op jit(solution)/shard_map/se,sc->ec/dot_general | solution.py:122
  145.3 17.6 %all-gather.8.cloned.1.call-done = bf16[4096,512]{1,0:T(8,128)(2,1)} async-done(((bf16[128,512]{1,0:T(8,128)(2,1)}), bf16[4096,512]{1,0:T(8,128)(2,1)}) %all-gather.8.cloned.1.call-update) | async-done | bytes 4194320 | tf_op jit(solution)/shard_map/all_gather | solution.py:110
  162.9 4.5 %copy.53 = bf16[4096,512]{1,0:T(8,128)(2,1)} copy(bf16[4096,512]{1,0:T(8,128)(2,1)} %all-gather.8.cloned.1.call-done) | data formatting | bytes 8388608
  (77 shorter events, 2.1 us)
Async XLA Ops:
  7.2 12.8 %copy-start = (bf16[2048,512]{1,0:T(8,128)(2,1)S(1)}, bf16[2048,512]{1,0:T(8,128)(2,1)}, u32[]{:S(2)}) copy-start(bf16[2048,512]{1,0:T(8,128)(2,1)} %param.8) | copy-start | bytes 6291460
  10.0 50.7 %copy-start.9 = (s32[512]{0:T(512)}, s32[512]{0:T(512)S(1)}, u32[]{:S(2)}) copy-start(s32[512]{0:T(512)S(1)} %multiply_add_fusion) | copy-start | bytes 6148
  12.0 14.4 %all-to-all-start = ((s32[32,1,32]{2,1,0:T(1,128)}), s32[32,1,32]{2,1,0:T(1,128)S(1)}, u32[]{:S(2)}, u32[]{:S(2)}) async-start(s32[32,1,32]{2,1,0:T(1,128)} %all_to_all.15), calls=%async_computation | async-start | bytes 32768 | tf_op jit(solution)/shard_map/all_to_all | solution.py:41
  27.7 3.4 %copy-start.15 = (s32[1024]{0:T(1024)}, s32[1024]{0:T(1024)S(1)}, u32[]{:S(2)}) copy-start(s32[1024]{0:T(1024)S(1)} %eq.123) | copy-start | bytes 12292
  31.0 3.6 %copy-start.11 = (s32[256]{0:T(256)S(1)}, s32[256]{0:T(256)}, u32[]{:S(2)}) copy-start(s32[256]{0:T(256)} %param.13) | copy-start | bytes 3076
  31.0 4.5 %copy-start.20 = (s32[256]{0:T(256)S(1)}, s32[256]{0:T(256)}, u32[]{:S(2)}) copy-start(s32[256]{0:T(256)} %param.10) | copy-start | bytes 3076
  31.0 29.7 %all-to-all-start.1 = ((bf16[32,32,512]{2,1,0:T(8,128)(2,1)}), bf16[32,32,512]{2,1,0:T(8,128)(2,1)}, u32[]{:S(2)}, u32[]{:S(2)}) async-start(bf16[32,32,512]{2,1,0:T(8,128)(2,1)} %bitcast.3), calls=%async_computation.1 | async-start | bytes 2097152 | tf_op jit(solution)/shard_map/all_to_all | solution.py:52
  34.6 31.5 %all-gather.4.cloned.1.call-start = ((), (), s32[]{:S(2)}) async-start(), calls=%async_computation.4 | async-start | bytes 1310720 | tf_op jit(solution)/shard_map/all_gather | solution.py:68
  35.5 63.5 %all-gather.6.cloned.1.call-start = ((), (), s32[]{:S(2)}) async-start(), calls=%async_computation.5 | async-start | bytes 1310720 | tf_op jit(solution)/shard_map/all_gather | solution.py:81
  36.5 0.6 copy-start.7
  41.2 21.8 %copy-start.18 = (pred[256]{0:T(512)(128)(4,1)}, pred[256]{0:T(512)(128)(4,1)S(1)}, u32[]{:S(2)}) copy-start(pred[256]{0:T(512)(128)(4,1)S(1)} %compare_and_fusion.1) | copy-start | bytes 772
  62.9 1.0 copy-start.3
  66.0 2.4 %copy-start.17 = (f32[256]{0:T(256)S(1)}, f32[256]{0:T(256)}, u32[]{:S(2)}) copy-start(f32[256]{0:T(256)} %get-tuple-element.21) | copy-start | bytes 3076
  66.1 3.5 %copy-start.21 = (bf16[1024,512]{1,0:T(8,128)(2,1)S(1)}, bf16[1024,512]{1,0:T(8,128)(2,1)}, u32[]{:S(2)}) copy-start(bf16[1024,512]{1,0:T(8,128)(2,1)} %all-gather.4.cloned.1.call-done) | copy-start | bytes 3145732
  69.0 0.6 copy-start.13
  69.6 0.7 copy-start.8
  70.3 5.2 %copy-start.4 = (bf16[256,1,256]{2,0,1:T(8,128)(2,1)S(1)}, bf16[256,1,256]{2,0,1:T(8,128)(2,1)}, u32[]{:S(2)}) copy-start(bf16[256,1,256]{2,0,1:T(8,128)(2,1)} %get-tuple-element.32) | copy-start | bytes 393220
  70.3 5.2 %copy-start.5 = (bf16[256,1,256]{2,0,1:T(8,128)(2,1)S(1)}, bf16[256,1,256]{2,0,1:T(8,128)(2,1)}, u32[]{:S(2)}) copy-start(bf16[256,1,256]{2,0,1:T(8,128)(2,1)} %get-tuple-element.46) | copy-start | bytes 393220
  70.6 4.9 %copy-start.6 = (bf16[256,1,256]{2,0,1:T(8,128)(2,1)S(1)}, bf16[256,1,256]{2,0,1:T(8,128)(2,1)}, u32[]{:S(2)}) copy-start(bf16[256,1,256]{2,0,1:T(8,128)(2,1)} %get-tuple-element.47) | copy-start | bytes 393220
  70.7 4.9 %copy-start.14 = (f32[256]{0:T(256)S(1)}, f32[256]{0:T(256)}, u32[]{:S(2)}) copy-start(f32[256]{0:T(256)} %copy-done.13) | copy-start | bytes 3076
  70.7 5.0 %copy-start.19 = (pred[256]{0:T(512)(128)(4,1)S(1)}, pred[256]{0:T(512)(128)(4,1)}, u32[]{:S(2)}) copy-start(pred[256]{0:T(512)(128)(4,1)} %copy-done.18) | copy-start | bytes 772
  71.6 24.2 %all-to-all-start.2 = ((bf16[32,17,512]{2,1,0:T(8,128)(2,1)}), bf16[32,17,512]{2,1,0:T(8,128)(2,1)}, u32[]{:S(2)}, u32[]{:S(2)}) async-start(bf16[32,17,512]{2,1,0:T(8,128)(2,1)} %fusion.19), calls=%async_computation.2 | async-start | bytes 1572864 | tf_op jit(solution)/shard_map/all_to_all | solution.py:95
  75.3 87.6 %all-gather.8.cloned.1.call-start = ((), (), s32[]{:S(2)}) async-start(), calls=%async_computation.6 | async-start | bytes 4325376 | tf_op jit(solution)/shard_map/all_gather | solution.py:110
  75.7 1.0 copy-start.10
  78.3 24.4 %copy-start.2 = (bf16[256,512]{1,0:T(8,128)(2,1)S(1)}, bf16[256,512]{1,0:T(8,128)(2,1)}, u32[]{:S(2)}) copy-start(bf16[256,512]{1,0:T(8,128)(2,1)} %broadcast_select_fusion) | copy-start | bytes 786436
  99.0 3.8 %copy-start.1 = (bf16[1024,512]{1,0:T(8,128)(2,1)S(1)}, bf16[1024,512]{1,0:T(8,128)(2,1)}, u32[]{:S(2)}) copy-start(bf16[1024,512]{1,0:T(8,128)(2,1)} %all-gather.6.cloned.1.call-done) | copy-start | bytes 3145732
  99.0 35.6 %all-to-all-start.3 = ((bf16[32,32,512]{2,1,0:T(8,128)(2,1)}), bf16[32,32,512]{2,1,0:T(8,128)(2,1)}, u32[]{:S(2)}, u32[]{:S(2)}) async-start(bf16[32,32,512]{2,1,0:T(8,128)(2,1)} %bitcast.87), calls=%async_computation.3 | async-start | bytes 2097152 | tf_op jit(solution)/shard_map/all_to_all | solution.py:111
  102.8 31.8 %copy-start.16 = (s32[1024]{0:T(1024)S(1)}, s32[1024]{0:T(1024)}, u32[]{:S(2)}) copy-start(s32[1024]{0:T(1024)} %copy-done.15) | copy-start | bytes 12292
  134.5 5.9 %copy-start.12 = (s32[256]{0:T(256)S(1)}, s32[256]{0:T(256)}, u32[]{:S(2)}) copy-start(s32[256]{0:T(256)} %param.13) | copy-start | bytes 3076
Sparse Core Ops, SparseCore 0:
  36.9 19.7 all-gather.3
  66.2 21.9 all-gather.5
  99.1 63.7 all-gather.7

commit v6 on v4

--- a/solution.py
+++ b/solution.py
@@ -38,18 +38,25 @@
     rel_place = jnp.arange(device_count * rel_capacity, dtype=jnp.int32)[:, None] == rel_pos[None, :]
     send_ent_ids = jnp.sum(jnp.where(ent_place, local_rows[None, :], 0), axis=1)
     send_rel_ids = jnp.sum(jnp.where(rel_place, rel_local[None, :], 0), axis=1)
-    send_ids = jnp.concatenate(
+    send_ids = jnp.stack(
         [
             send_ent_ids.reshape(device_count, capacity),
-            send_rel_ids.reshape(device_count, rel_capacity),
+            jnp.pad(
+                send_rel_ids.reshape(device_count, rel_capacity), ((0, 0), (0, capacity - rel_capacity))
+            ),
         ],
         axis=1,
     )
     recv_ids = lax.all_to_all(send_ids, AXES, split_axis=0, concat_axis=0, tiled=True)
-    asked_ids = recv_ids[:, :capacity].reshape(-1)
-    rel_ids_in = recv_ids[:, capacity:].reshape(-1)
+    asked_ids = recv_ids[:, 0].reshape(-1)
+    rel_ids_in = recv_ids[:, 1, :rel_capacity].reshape(-1)
 
-    served = jnp.take(entity_table, asked_ids, axis=0).reshape(device_count, capacity, row_width)
+    entity_iota = jnp.arange(entity_rows, dtype=jnp.int32)[None, :]
+    asked_onehot = (asked_ids[:, None] == entity_iota).astype(jnp.bfloat16)
+    served = jnp.einsum(
+        "se,ec->sc", asked_onehot, entity_table, preferred_element_type=jnp.float32
+    ).astype(jnp.bfloat16)
+    served = served.reshape(device_count, capacity, row_width)
     got_rows = lax.all_to_all(served, AXES, split_axis=0, concat_axis=0, tiled=True)
     got_rows = got_rows.reshape(device_count * capacity, row_width)
     ent_place_bf = ent_place.astype(jnp.bfloat16)
@@ -111,8 +118,6 @@
     own_weights = (jax.nn.sigmoid(own_scores) / group_neg).astype(jnp.bfloat16)
     neg_grad = jnp.einsum("tk,tc->kc", own_weights, group_query, preferred_element_type=jnp.float32)
 
-    entity_iota = jnp.arange(entity_rows, dtype=jnp.int32)[None, :]
-    asked_onehot = (asked_ids[:, None] == entity_iota).astype(jnp.bfloat16)
     neg_onehot = (negative_ids[:, None] == entity_iota).astype(jnp.bfloat16)
     entity_grad = jnp.einsum(
         "se,sc->ec", asked_onehot, back_ent, preferred_element_type=jnp.float32

time: 169 us -> 167 us (0.988)
  local copies, waits for them, and re-layouts: 23.2 us -> 18.7 us
  matrix products: 21.7 us -> 25 us
  other arithmetic: 10.1 us -> 8.25 us
    gather x1 -> x0, local copies, waits for them, and re-layouts: 3.97 us -> none  [body(): jnp.take(entity_table, asked_ids, axis=0)]
    dot_general x0 -> x1, matrix products: none -> 3.35 us  [body(): jnp.einsum('se,ec->sc', asked_onehot, entity_table, preferred_element_typ...]
    another operation x6 -> x7, other arithmetic: 3.74 us -> 3.74 us
  transfers between devices with their start and end apart: 6 -> 6, of which waited for: 4 -> 4; matrix products, arithmetic and copies ran while one was open for 23% -> 22% of each run, Pallas kernels for 0% -> 0%
where the time goes in v6:
time: 167 us; the launch traced here: 166 us
  waiting for transfers between devices  74.8 us (45%)
  matrix products  25 us (15%)
  local copies, waits for them, and re-layouts  18.7 us (11%)
  blocking collectives  14.4 us (9%)
  between operations  14.1 us (8%)
  starting transfers between devices  10.9 us (7%)
  other arithmetic  8.25 us (5%)
    all_to_all x1, waiting for transfers between devices, body(): lax.all_to_all(send_ent.reshape(device_count, capacity, row_width), AXES,...  31 us
    all_to_all x1, waiting for transfers between devices, body(): lax.all_to_all(served, AXES, split_axis=0, concat_axis=0, tiled=True)  19.2 us
    all_gather x1, waiting for transfers between devices, body(): relation_grad = lax.all_gather(own_rel_grad, AXES, axis=0, tiled=True)  16.9 us
    all_to_all x1, blocking collectives, body(): lax.all_to_all(send_ids, AXES, split_axis=0, concat_axis=0, tiled=True)  14.4 us
    unnamed x36, local copies, waits for them, and re-layouts  7.67 us
    all_to_all x1, waiting for transfers between devices, body(): lax.all_to_all(send_rel.reshape(device_count, rel_capacity, row_width), A...  7.64 us
    dot_general x1, matrix products, body(): jnp.einsum('se,sc->ec', asked_onehot, back_ent, preferred_element_type=jn...  5.94 us
    dot_general x1, matrix products, body(): jnp.einsum('se,sc->ec', neg_onehot, neg_grad.astype(jnp.bfloat16), prefer...  4.82 us
  transfers between devices with their start and end apart: 6, of which 4 were waited for; matrix products, arithmetic and copies ran while one was open for 22% of the time, Pallas kernels for 0%

profile of v6, /device:TPU:0, one launch (start us, length us, event | category | flops | bytes accessed | tf_op | source)
XLA Modules:
  0.0 166.2 jit_solution(8007374933340005161)
XLA Ops:
  7.2 1.0 copy.28
  8.1 0.1 eq.119
  8.4 0.7 multiply_subtract_fusion
  9.1 0.6 reduce-window.16
  9.7 0.2 slice_reduce_fusion.1
  10.1 0.2 select_reduce_fusion.1
  10.3 1.2 reduce-window.14
  11.5 0.2 slice_reduce_fusion
  11.9 0.8 copy.31
  12.9 0.3 select_reduce_fusion
  13.3 14.4 %all_to_all.20 = s32[32,2,32]{2,1,0:T(2,128)S(1)} all-to-all(s32[32,2,32]{2,1,0:T(2,128)S(1)} %copy.33), channel_id=1, replica_groups=mesh['wide'=8,'narrow'=4] {'wide','narrow'}, dimensions={0} | all-to-all | bytes 16384 | tf_op jit(solution)/shard_map/all_to_all | solution.py:50
  27.7 0.6 copy-done.4
  28.4 3.3 %fusion.6 = bf16[1024,512]{1,0:T(8,128)(2,1)} fusion(bf16[2048,512]{1,0:T(8,128)(2,1)S(1)} %copy-done, s32[1024]{0:T(1024)S(1)} %eq.135), kind=kOutput, calls=%fused_computation.14 | convolution fusion | flops 2150105088 | bytes 3149824 | tf_op jit(solution)/shard_map/se,ec->sc/dot_general | solution.py:56
  31.7 3.5 %all-to-all-start.1 = ((bf16[32,32,512]{2,1,0:T(8,128)(2,1)}), bf16[32,32,512]{2,1,0:T(8,128)(2,1)}, u32[]{:S(2)}, u32[]{:S(2)}) async-start(bf16[32,32,512]{2,1,0:T(8,128)(2,1)} %bitcast.4), calls=%async_computation.1 | async-start | bytes 2097152 | tf_op jit(solution)/shard_map/all_to_all | solution.py:60
  35.3 1.2 gather_fusion.1
  36.5 0.8 broadcast_select_fusion
  37.4 3.9 %gather_fusion = bf16[256,512]{1,0:T(8,128)(2,1)S(1)} fusion(bf16[4096,512]{1,0:T(8,128)(2,1)} %param.7, s32[1024]{0:T(1024)S(1)} %pad_clamp_fusion.1), kind=kCustom, calls=%fused_computation | custom fusion | bytes 525312 | tf_op jit(solution)/shard_map/jit(_take)/gather | solution.py:69
  41.4 0.8 broadcast_select_fusion.1
  42.2 19.2 %all-to-all-done.1 = bf16[32,32,512]{2,1,0:T(8,128)(2,1)} async-done(((bf16[32,32,512]{2,1,0:T(8,128)(2,1)}), bf16[32,32,512]{2,1,0:T(8,128)(2,1)}, u32[]{:S(2)}, u32[]{:S(2)}) %all-to-all-start.1) | async-done | bytes 1048608 | tf_op jit(solution)/shard_map/all_to_all | solution.py:60
  61.4 2.0 %fusion.12 = bf16[512,512]{1,0:T(8,128)(2,1)S(1)} fusion(bf16[1024,512]{1,0:T(8,128)(2,1)} %bitcast.5, s32[512]{0:T(512)S(1)} %multiply_add_fusion), kind=kOutput, calls=%fused_computation.21 | convolution fusion | flops 537657344 | bytes 1574912 | tf_op jit(solution)/shard_map/sj,sc->jc/dot_general | solution.py:63
  63.4 0.2 reshape.255
  63.6 0.7 fusion.42
  64.4 0.2 copy-done.3
  64.6 0.8 slice_bitcast_fusion.3
  65.4 0.8 fusion.18
  66.3 2.3 %fusion.14 = (f32[256]{0:T(256)S(1)}, f32[256,1024]{1,0:T(8,128)S(1)}) fusion(bf16[256,512]{1,0:T(8,128)(2,1)} %get-tuple-element.10, bf16[1024,512]{1,0:T(8,128)(2,1)} %all-gather.4.cloned.1.call-done), kind=kOutput, calls=%fused_computation.27 | convolution fusion | flops 270270208 | bytes 2360320 | tf_op jit(solution)/shard_map/tc,kc->tk/dot_general | solution.py:78
  68.6 0.6 fusion.37
  69.2 0.6 copy-done.10
  69.8 0.5 convolution_add_fusion
  70.3 1.1 convolution_convert_fusion
  71.4 3.6 %all-to-all-start.2 = ((bf16[32,16,512]{2,1,0:T(8,128)(2,1)}), bf16[32,16,512]{2,1,0:T(8,128)(2,1)S(1)}, u32[]{:S(2)}, u32[]{:S(2)}) async-start(bf16[32,16,512]{2,1,0:T(8,128)(2,1)} %bitcast.8), calls=%async_computation.2 | async-start | bytes 1048576 | tf_op jit(solution)/shard_map/all_to_all | solution.py:97
  75.0 0.2 all-gather.8.cloned.1.call-start
  75.2 0.8 slice_reduce_fusion.2
  76.0 0.7 eq.139
  76.7 1.1 multiply_convert_fusion.2
  77.8 0.8 fusion.22
  78.7 0.5 copy.36
  79.2 1.0 convert_element_type.144
  80.2 2.7 %fusion.7 = bf16[1024,512]{1,0:T(8,128)(2,1)} fusion(bf16[512,512]{1,0:T(8,128)(2,1)} %convert_element_type.144, s32[512]{0:T(512)S(1)} %copy-done.7), kind=kOutput, calls=%fused_computation.15 | convolution fusion | flops 537919488 | bytes 1574912 | tf_op jit(solution)/shard_map/sj,jc->sc/dot_general | solution.py:108
  83.0 7.6 %all-to-all-done.2 = bf16[32,16,512]{2,1,0:T(8,128)(2,1)S(1)} async-done(((bf16[32,16,512]{2,1,0:T(8,128)(2,1)}), bf16[32,16,512]{2,1,0:T(8,128)(2,1)S(1)}, u32[]{:S(2)}, u32[]{:S(2)}) %all-to-all-start.2) | async-done | bytes 524320 | tf_op jit(solution)/shard_map/all_to_all | solution.py:97
  90.6 1.0 convolution_convert_fusion.2
  91.7 3.5 %all-to-all-start.3 = ((bf16[32,32,512]{2,1,0:T(8,128)(2,1)}), bf16[32,32,512]{2,1,0:T(8,128)(2,1)}, u32[]{:S(2)}, u32[]{:S(2)}) async-start(bf16[32,32,512]{2,1,0:T(8,128)(2,1)} %bitcast.88), calls=%async_computation.3 | async-start | bytes 2097152 | tf_op jit(solution)/shard_map/all_to_all | solution.py:113
  95.2 1.3 fusion.13
  96.5 31.0 %all-to-all-done.3 = bf16[32,32,512]{2,1,0:T(8,128)(2,1)} async-done(((bf16[32,32,512]{2,1,0:T(8,128)(2,1)}), bf16[32,32,512]{2,1,0:T(8,128)(2,1)}, u32[]{:S(2)}, u32[]{:S(2)}) %all-to-all-start.3) | async-done | bytes 1048608 | tf_op jit(solution)/shard_map/all_to_all | solution.py:113
  127.5 5.9 %fusion = f32[2048,512]{1,0:T(8,128)} fusion(bf16[1024,512]{1,0:T(8,128)(2,1)} %bitcast.18, s32[1024]{0:T(1024)S(1)} %copy-done.12), kind=kOutput, calls=%fused_computation.3 | convolution fusion | flops 2149580800 | bytes 5246976 | tf_op jit(solution)/shard_map/se,sc->ec/dot_general | solution.py:122
  133.4 4.8 %add_convert_fusion = bf16[2048,512]{1,0:T(8,128)(2,1)} fusion(f32[2048,512]{1,0:T(8,128)} %fusion, bf16[1024,256]{1,0:T(8,128)(2,1)} %fusion.13, bf16[1024,512]{1,0:T(8,128)(2,1)S(1)} %copy-done.1, s32[256]{0:T(256)S(1)} %copy-done.9), kind=kOutput, calls=%fused_computation.5 | convolution fusion | flops 808058880 | bytes 7865344 | tf_op jit(solution)/shard_map/se,sc->ec/dot_general | solution.py:124
  138.3 16.9 %all-gather.8.cloned.1.call-done = bf16[4096,512]{1,0:T(8,128)(2,1)} async-done(((bf16[128,512]{1,0:T(8,128)(2,1)}), bf16[4096,512]{1,0:T(8,128)(2,1)}) %all-gather.8.cloned.1.call-update) | async-done | bytes 4194320 | tf_op jit(solution)/shard_map/all_gather | solution.py:112
  155.2 4.5 %copy.51 = bf16[4096,512]{1,0:T(8,128)(2,1)} copy(bf16[4096,512]{1,0:T(8,128)(2,1)} %all-gather.8.cloned.1.call-done) | data formatting | bytes 8388608
  (63 shorter events, 1.3 us)
Async XLA Ops:
  7.2 21.2 %copy-start = (bf16[2048,512]{1,0:T(8,128)(2,1)S(1)}, bf16[2048,512]{1,0:T(8,128)(2,1)}, u32[]{:S(2)}) copy-start(bf16[2048,512]{1,0:T(8,128)(2,1)} %param.6) | copy-start | bytes 6291460
  11.9 49.5 %copy-start.6 = (s32[512]{0:T(512)}, s32[512]{0:T(512)S(1)}, u32[]{:S(2)}) copy-start(s32[512]{0:T(512)S(1)} %multiply_add_fusion) | copy-start | bytes 6148
  27.7 0.6 copy-start.4
  28.4 3.4 %copy-start.11 = (s32[1024]{0:T(1024)}, s32[1024]{0:T(1024)S(1)}, u32[]{:S(2)}) copy-start(s32[1024]{0:T(1024)S(1)} %eq.135) | copy-start | bytes 12292
  31.7 3.6 %copy-start.8 = (s32[256]{0:T(256)S(1)}, s32[256]{0:T(256)}, u32[]{:S(2)}) copy-start(s32[256]{0:T(256)} %param.11) | copy-start | bytes 3076
  31.7 29.7 %all-to-all-start.1 = ((bf16[32,32,512]{2,1,0:T(8,128)(2,1)}), bf16[32,32,512]{2,1,0:T(8,128)(2,1)}, u32[]{:S(2)}, u32[]{:S(2)}) async-start(bf16[32,32,512]{2,1,0:T(8,128)(2,1)} %bitcast.4), calls=%async_computation.1 | async-start | bytes 2097152 | tf_op jit(solution)/shard_map/all_to_all | solution.py:60
  35.3 31.0 %all-gather.4.cloned.1.call-start = ((), (), s32[]{:S(2)}) async-start(), calls=%async_computation.4 | async-start | bytes 1310720 | tf_op jit(solution)/shard_map/all_gather | solution.py:76
  36.5 4.9 %copy-start.14 = (s32[256]{0:T(256)S(1)}, s32[256]{0:T(256)}, u32[]{:S(2)}) copy-start(s32[256]{0:T(256)} %param.8) | copy-start | bytes 3076
  37.4 54.3 %all-gather.6.cloned.1.call-start = ((), (), s32[]{:S(2)}) async-start(), calls=%async_computation.5 | async-start | bytes 1310720 | tf_op jit(solution)/shard_map/all_gather | solution.py:89
  41.4 22.2 %copy-start.13 = (pred[256]{0:T(512)(128)(4,1)}, pred[256]{0:T(512)(128)(4,1)S(1)}, u32[]{:S(2)}) copy-start(pred[256]{0:T(512)(128)(4,1)S(1)} %compare_and_fusion.1) | copy-start | bytes 772
  63.6 1.0 copy-start.3
  66.3 3.5 %copy-start.15 = (bf16[1024,512]{1,0:T(8,128)(2,1)S(1)}, bf16[1024,512]{1,0:T(8,128)(2,1)}, u32[]{:S(2)}) copy-start(bf16[1024,512]{1,0:T(8,128)(2,1)} %all-gather.4.cloned.1.call-done) | copy-start | bytes 3145732
  69.2 0.6 copy-start.10
  71.4 19.2 %all-to-all-start.2 = ((bf16[32,16,512]{2,1,0:T(8,128)(2,1)}), bf16[32,16,512]{2,1,0:T(8,128)(2,1)S(1)}, u32[]{:S(2)}, u32[]{:S(2)}) async-start(bf16[32,16,512]{2,1,0:T(8,128)(2,1)} %bitcast.8), calls=%async_computation.2 | async-start | bytes 1048576 | tf_op jit(solution)/shard_map/all_to_all | solution.py:97
  75.0 80.2 %all-gather.8.cloned.1.call-start = ((), (), s32[]{:S(2)}) async-start(), calls=%async_computation.6 | async-start | bytes 4325376 | tf_op jit(solution)/shard_map/all_gather | solution.py:112
  77.8 2.4 %copy-start.7 = (s32[512]{0:T(512)S(1)}, s32[512]{0:T(512)}, u32[]{:S(2)}) copy-start(s32[512]{0:T(512)} %copy-done.6) | copy-start | bytes 6148
  79.2 11.4 %copy-start.5 = (s32[512]{0:T(512)S(1)}, s32[512]{0:T(512)}, u32[]{:S(2)}) copy-start(s32[512]{0:T(512)} %eq.139) | copy-start | bytes 6148
  83.0 12.2 %copy-start.2 = (bf16[256,512]{1,0:T(8,128)(2,1)S(1)}, bf16[256,512]{1,0:T(8,128)(2,1)}, u32[]{:S(2)}) copy-start(bf16[256,512]{1,0:T(8,128)(2,1)} %broadcast_select_fusion) | copy-start | bytes 786436
  91.6 3.6 %copy-start.1 = (bf16[1024,512]{1,0:T(8,128)(2,1)S(1)}, bf16[1024,512]{1,0:T(8,128)(2,1)}, u32[]{:S(2)}) copy-start(bf16[1024,512]{1,0:T(8,128)(2,1)} %all-gather.6.cloned.1.call-done) | copy-start | bytes 3145732
  91.7 35.8 %all-to-all-start.3 = ((bf16[32,32,512]{2,1,0:T(8,128)(2,1)}), bf16[32,32,512]{2,1,0:T(8,128)(2,1)}, u32[]{:S(2)}, u32[]{:S(2)}) async-start(bf16[32,32,512]{2,1,0:T(8,128)(2,1)} %bitcast.88), calls=%async_computation.3 | async-start | bytes 2097152 | tf_op jit(solution)/shard_map/all_to_all | solution.py:113
  95.2 32.3 %copy-start.12 = (s32[1024]{0:T(1024)S(1)}, s32[1024]{0:T(1024)}, u32[]{:S(2)}) copy-start(s32[1024]{0:T(1024)} %copy-done.11) | copy-start | bytes 12292
  127.5 5.9 %copy-start.9 = (s32[256]{0:T(256)S(1)}, s32[256]{0:T(256)}, u32[]{:S(2)}) copy-start(s32[256]{0:T(256)} %param.11) | copy-start | bytes 3076
Sparse Core Ops, SparseCore 0:
  37.6 19.7 all-gather.3
  66.3 19.8 all-gather.5
  91.8 63.3 all-gather.7

commit v7 on v6

--- a/solution.py
+++ b/solution.py
@@ -109,7 +109,13 @@
         "sj,jc->sc", ent_place_bf, ent_grads.astype(jnp.bfloat16), preferred_element_type=jnp.float32
     ).astype(jnp.bfloat16)
     own_rel_grad, send_ent, group_query = lax.optimization_barrier((own_rel_grad, send_ent, group_query))
-    relation_grad = lax.all_gather(own_rel_grad, AXES, axis=0, tiled=True)
+    core = lax.axis_index("narrow") % 2
+    pair_perm = [(i, i ^ 1) for i in range(narrow_count)]
+    core_groups = [[d for d in range(device_count) if d % 2 == k] for k in range(2)]
+    mine = lax.all_gather(own_rel_grad, AXES, axis=0, tiled=False, axis_index_groups=core_groups)
+    other = lax.ppermute(mine, "narrow", pair_perm)
+    parity = jnp.arange(2, dtype=jnp.int32)[None, :, None, None]
+    relation_grad = jnp.where(parity == core, mine[:, None], other[:, None]).reshape(-1, row_width)
     back_ent = lax.all_to_all(
         send_ent.reshape(device_count, capacity, row_width), AXES, split_axis=0, concat_axis=0, tiled=True
     ).reshape(-1, row_width)

time: 167 us -> 177 us (1.060)
  waiting for transfers between devices: 74.8 us -> 85.7 us
  local copies, waits for them, and re-layouts: 18.7 us -> 14.4 us
  other arithmetic: 8.25 us -> 12.1 us
    all_gather x1, waiting for transfers between devices: 16.9 us -> 58.8 us  [body(): lax.all_gather(own_rel_grad, AXES, axis=0, tiled=False, axis_index_groups...]
    all_to_all x1, waiting for transfers between devices: 31 us -> 0.01 us  [body(): lax.all_to_all(send_ent.reshape(device_count, capacity, row_width), AXES,...]
    unnamed x36 -> x35, local copies, waits for them, and re-layouts: 7.67 us -> 3.23 us
    select_n x0 -> x1, other arithmetic: none -> 3.9 us  [body(): jnp.where(parity == core, mine[:, None], other[:, None])]
  transfers between devices with their start and end apart: 6 -> 7, of which waited for: 4 -> 3; matrix products, arithmetic and copies ran while one was open for 22% -> 21% of each run, Pallas kernels for 0% -> 0%
where the time goes in v7:
time: 177 us
  waiting for transfers between devices  85.7 us (48%)
  matrix products  25 us (14%)
  local copies, waits for them, and re-layouts  14.4 us (8%)
  blocking collectives  14.4 us (8%)
  between operations  14.1 us (8%)
  other arithmetic  12.1 us (7%)
  starting transfers between devices  10.9 us (6%)
    all_gather x1, waiting for transfers between devices, body(): lax.all_gather(own_rel_grad, AXES, axis=0, tiled=False, axis_index_groups...  58.8 us
    all_to_all x1, waiting for transfers between devices, body(): lax.all_to_all(served, AXES, split_axis=0, concat_axis=0, tiled=True)  19.2 us
    all_to_all x1, blocking collectives, body(): lax.all_to_all(send_ids, AXES, split_axis=0, concat_axis=0, tiled=True)  14.4 us
    all_to_all x1, waiting for transfers between devices, body(): lax.all_to_all(send_rel.reshape(device_count, rel_capacity, row_width), A...  7.65 us
    dot_general x1, matrix products, body(): jnp.einsum('se,sc->ec', asked_onehot, back_ent, preferred_element_type=jn...  5.92 us
    dot_general x1, matrix products, body(): jnp.einsum('se,sc->ec', neg_onehot, neg_grad.astype(jnp.bfloat16), prefer...  4.82 us
    gather x1, local copies, waits for them, and re-layouts, body(): rel_rows = jnp.take(relation_table, triple_rel, axis=0)  3.94 us
    select_n x1, other arithmetic, body(): jnp.where(parity == core, mine[:, None], other[:, None])  3.9 us
  transfers between devices with their start and end apart: 7, of which 3 were waited for; matrix products, arithmetic and copies ran while one was open for 21% of the time, Pallas kernels for 0%

profile of v7, /device:TPU:0, one launch (start us, length us, event | category | flops | bytes accessed | tf_op | source)
XLA Modules:
  0.0 176.6 jit_solution(1557447414804663370)
XLA Ops:
  7.2 1.0 copy.28
  8.1 0.1 reshape.260
  8.4 0.7 multiply_subtract_fusion
  9.1 0.6 reduce-window.16
  9.7 0.2 slice_reduce_fusion.1
  10.1 0.2 select_reduce_fusion.1
  10.3 0.8 copy.31
  11.1 0.1 broadcast_in_dim.100
  11.3 1.2 reduce-window.14
  12.5 0.2 slice_reduce_fusion
  12.9 0.3 select_reduce_fusion
  13.3 14.4 %all_to_all.20 = s32[32,2,32]{2,1,0:T(2,128)S(1)} all-to-all(s32[32,2,32]{2,1,0:T(2,128)S(1)} %copy.33), channel_id=1, replica_groups=mesh['wide'=8,'narrow'=4] {'wide','narrow'}, dimensions={0} | all-to-all | bytes 16384 | tf_op jit(solution)/shard_map/all_to_all | solution.py:50
  27.7 0.6 copy-done.4
  28.4 3.3 %fusion.6 = bf16[1024,512]{1,0:T(8,128)(2,1)} fusion(bf16[2048,512]{1,0:T(8,128)(2,1)S(1)} %copy-done, s32[1024]{0:T(1024)S(1)} %eq.148), kind=kOutput, calls=%fused_computation.15 | convolution fusion | flops 2150105088 | bytes 3149824 | tf_op jit(solution)/shard_map/se,ec->sc/dot_general | solution.py:56
  31.7 3.5 %all-to-all-start.1 = ((bf16[32,32,512]{2,1,0:T(8,128)(2,1)}), bf16[32,32,512]{2,1,0:T(8,128)(2,1)}, u32[]{:S(2)}, u32[]{:S(2)}) async-start(bf16[32,32,512]{2,1,0:T(8,128)(2,1)} %bitcast.4), calls=%async_computation.1 | async-start | bytes 2097152 | tf_op jit(solution)/shard_map/all_to_all | solution.py:60
  35.3 1.2 gather_fusion.1
  36.5 0.8 broadcast_select_fusion
  37.4 3.9 %gather_fusion = bf16[256,512]{1,0:T(8,128)(2,1)S(1)} fusion(bf16[4096,512]{1,0:T(8,128)(2,1)} %param.7, s32[1024]{0:T(1024)S(1)} %pad_clamp_fusion.1), kind=kCustom, calls=%fused_computation | custom fusion | bytes 525312 | tf_op jit(solution)/shard_map/jit(_take)/gather | solution.py:69
  41.4 0.8 broadcast_select_fusion.1
  42.2 19.2 %all-to-all-done.1 = bf16[32,32,512]{2,1,0:T(8,128)(2,1)} async-done(((bf16[32,32,512]{2,1,0:T(8,128)(2,1)}), bf16[32,32,512]{2,1,0:T(8,128)(2,1)}, u32[]{:S(2)}, u32[]{:S(2)}) %all-to-all-start.1) | async-done | bytes 1048608 | tf_op jit(solution)/shard_map/all_to_all | solution.py:60
  61.4 2.0 %fusion.12 = bf16[512,512]{1,0:T(8,128)(2,1)S(1)} fusion(bf16[1024,512]{1,0:T(8,128)(2,1)} %bitcast.5, s32[512]{0:T(512)S(1)} %multiply_add_fusion), kind=kOutput, calls=%fused_computation.22 | convolution fusion | flops 537657344 | bytes 1574912 | tf_op jit(solution)/shard_map/sj,sc->jc/dot_general | solution.py:63
  63.4 0.2 reshape.266
  63.6 0.7 fusion.42
  64.4 0.2 copy-done.3
  64.6 0.8 slice_bitcast_fusion.3
  65.4 0.8 fusion.18
  66.3 2.3 %fusion.14 = (f32[256]{0:T(256)S(1)}, f32[256,1024]{1,0:T(8,128)S(1)}) fusion(bf16[256,512]{1,0:T(8,128)(2,1)} %get-tuple-element.10, bf16[1024,512]{1,0:T(8,128)(2,1)} %all-gather.5.cloned.1.call-done), kind=kOutput, calls=%fused_computation.28 | convolution fusion | flops 270270208 | bytes 2360320 | tf_op jit(solution)/shard_map/tc,kc->tk/dot_general | solution.py:78
  68.6 0.6 fusion.37
  69.2 0.6 copy-done.10
  69.8 0.5 convolution_add_fusion
  70.3 1.1 convolution_convert_fusion
  71.5 3.5 %all-to-all-start.2 = ((bf16[32,16,512]{2,1,0:T(8,128)(2,1)}), bf16[32,16,512]{2,1,0:T(8,128)(2,1)S(1)}, u32[]{:S(2)}, u32[]{:S(2)}) async-start(bf16[32,16,512]{2,1,0:T(8,128)(2,1)} %bitcast.8), calls=%async_computation.2 | async-start | bytes 1048576 | tf_op jit(solution)/shard_map/all_to_all | solution.py:97
  75.0 0.2 all-gather.9.cloned.1.call-start
  75.2 0.8 slice_reduce_fusion.2
  76.1 0.7 eq.152
  76.7 1.1 multiply_convert_fusion.2
  77.9 0.8 fusion.22
  78.7 0.5 copy.36
  79.3 1.0 convert_element_type.144
  80.2 2.7 %fusion.7 = bf16[1024,512]{1,0:T(8,128)(2,1)} fusion(bf16[512,512]{1,0:T(8,128)(2,1)} %convert_element_type.144, s32[512]{0:T(512)S(1)} %copy-done.7), kind=kOutput, calls=%fused_computation.16 | convolution fusion | flops 537919488 | bytes 1574912 | tf_op jit(solution)/shard_map/sj,jc->sc/dot_general | solution.py:108
  83.0 7.6 %all-to-all-done.2 = bf16[32,16,512]{2,1,0:T(8,128)(2,1)S(1)} async-done(((bf16[32,16,512]{2,1,0:T(8,128)(2,1)}), bf16[32,16,512]{2,1,0:T(8,128)(2,1)S(1)}, u32[]{:S(2)}, u32[]{:S(2)}) %all-to-all-start.2) | async-done | bytes 524320 | tf_op jit(solution)/shard_map/all_to_all | solution.py:97
  90.6 1.0 convolution_convert_fusion.2
  91.7 3.5 %all-to-all-start.3 = ((bf16[32,32,512]{2,1,0:T(8,128)(2,1)}), bf16[32,32,512]{2,1,0:T(8,128)(2,1)}, u32[]{:S(2)}, u32[]{:S(2)}) async-start(bf16[32,32,512]{2,1,0:T(8,128)(2,1)} %bitcast.95), calls=%async_computation.3 | async-start | bytes 2097152 | tf_op jit(solution)/shard_map/all_to_all | solution.py:119
  95.2 58.8 %all-gather.9.cloned.1.call-done = bf16[2048,512]{1,0:T(8,128)(2,1)} async-done(((bf16[128,512]{1,0:T(8,128)(2,1)}), bf16[2048,512]{1,0:T(8,128)(2,1)}) %all-gather.9.cloned.1.call-update) | async-done | bytes 2097168 | tf_op jit(solution)/shard_map/all_gather | solution.py:115
  154.1 1.3 fusion.13
  155.4 5.9 %fusion = f32[2048,512]{1,0:T(8,128)} fusion(bf16[1024,512]{1,0:T(8,128)(2,1)} %bitcast.18, s32[1024]{0:T(1024)S(1)} %copy-done.12), kind=kOutput, calls=%fused_computation.3 | convolution fusion | flops 2149580800 | bytes 5246976 | tf_op jit(solution)/shard_map/se,sc->ec/dot_general | solution.py:128
  161.4 4.8 %add_convert_fusion = bf16[2048,512]{1,0:T(8,128)(2,1)} fusion(f32[2048,512]{1,0:T(8,128)} %fusion, bf16[1024,256]{1,0:T(8,128)(2,1)} %fusion.13, bf16[1024,512]{1,0:T(8,128)(2,1)S(1)} %copy-done.1, s32[256]{0:T(256)S(1)} %copy-done.9), kind=kOutput, calls=%fused_computation.6 | convolution fusion | flops 808058880 | bytes 7865344 | tf_op jit(solution)/shard_map/se,sc->ec/dot_general | solution.py:130
  166.2 3.9 %bitcast_select_fusion = bf16[4096,512]{1,0:T(8,128)(2,1)} fusion(pred[4096]{0:T(1024)(128)(4,1)S(1)} %broadcast_in_dim.113, bf16[16,128,512]{2,1,0:T(8,128)(2,1)} %collective-permute-done, bf16[16,128,512]{2,1,0:T(8,128)(2,1)} %bitcast.94), kind=kLoop, calls=%fused_computation.5 | loop fusion | flops 2097152 | bytes 8392704 | tf_op jit(solution)/shard_map/jit(_where)/select_n | solution.py:118
  (68 shorter events, 1.3 us)
Async XLA Ops:
  7.2 21.2 %copy-start = (bf16[2048,512]{1,0:T(8,128)(2,1)S(1)}, bf16[2048,512]{1,0:T(8,128)(2,1)}, u32[]{:S(2)}) copy-start(bf16[2048,512]{1,0:T(8,128)(2,1)} %param.6) | copy-start | bytes 6291460
  12.9 48.6 %copy-start.6 = (s32[512]{0:T(512)}, s32[512]{0:T(512)S(1)}, u32[]{:S(2)}) copy-start(s32[512]{0:T(512)S(1)} %multiply_add_fusion) | copy-start | bytes 6148
  27.7 0.6 copy-start.4
  28.4 3.4 %copy-start.11 = (s32[1024]{0:T(1024)}, s32[1024]{0:T(1024)S(1)}, u32[]{:S(2)}) copy-start(s32[1024]{0:T(1024)S(1)} %eq.148) | copy-start | bytes 12292
  31.7 3.6 %copy-start.8 = (s32[256]{0:T(256)S(1)}, s32[256]{0:T(256)}, u32[]{:S(2)}) copy-start(s32[256]{0:T(256)} %param.11) | copy-start | bytes 3076
  31.7 29.7 %all-to-all-start.1 = ((bf16[32,32,512]{2,1,0:T(8,128)(2,1)}), bf16[32,32,512]{2,1,0:T(8,128)(2,1)}, u32[]{:S(2)}, u32[]{:S(2)}) async-start(bf16[32,32,512]{2,1,0:T(8,128)(2,1)} %bitcast.4), calls=%async_computation.1 | async-start | bytes 2097152 | tf_op jit(solution)/shard_map/all_to_all | solution.py:60
  35.3 31.0 %all-gather.5.cloned.1.call-start = ((), (), s32[]{:S(2)}) async-start(), calls=%async_computation.4 | async-start | bytes 1310720 | tf_op jit(solution)/shard_map/all_gather | solution.py:76
  36.5 4.9 %copy-start.14 = (s32[256]{0:T(256)S(1)}, s32[256]{0:T(256)}, u32[]{:S(2)}) copy-start(s32[256]{0:T(256)} %param.8) | copy-start | bytes 3076
  37.4 54.3 %all-gather.7.cloned.1.call-start = ((), (), s32[]{:S(2)}) async-start(), calls=%async_computation.5 | async-start | bytes 1310720 | tf_op jit(solution)/shard_map/all_gather | solution.py:89
  41.4 22.2 %copy-start.13 = (pred[256]{0:T(512)(128)(4,1)}, pred[256]{0:T(512)(128)(4,1)S(1)}, u32[]{:S(2)}) copy-start(pred[256]{0:T(512)(128)(4,1)S(1)} %compare_and_fusion.1) | copy-start | bytes 772
  63.6 1.0 copy-start.3
  66.3 3.5 %copy-start.15 = (bf16[1024,512]{1,0:T(8,128)(2,1)S(1)}, bf16[1024,512]{1,0:T(8,128)(2,1)}, u32[]{:S(2)}) copy-start(bf16[1024,512]{1,0:T(8,128)(2,1)} %all-gather.5.cloned.1.call-done) | copy-start | bytes 3145732
  69.2 0.6 copy-start.10
  71.5 19.2 %all-to-all-start.2 = ((bf16[32,16,512]{2,1,0:T(8,128)(2,1)}), bf16[32,16,512]{2,1,0:T(8,128)(2,1)S(1)}, u32[]{:S(2)}, u32[]{:S(2)}) async-start(bf16[32,16,512]{2,1,0:T(8,128)(2,1)} %bitcast.8), calls=%async_computation.2 | async-start | bytes 1048576 | tf_op jit(solution)/shard_map/all_to_all | solution.py:97
  75.0 79.0 %all-gather.9.cloned.1.call-start = ((), (), s32[]{:S(2)}) async-start(), calls=%async_computation.6 | async-start | bytes 2228224 | tf_op jit(solution)/shard_map/all_gather | solution.py:115
  77.9 2.4 %copy-start.7 = (s32[512]{0:T(512)S(1)}, s32[512]{0:T(512)}, u32[]{:S(2)}) copy-start(s32[512]{0:T(512)} %copy-done.6) | copy-start | bytes 6148
  79.2 11.4 %copy-start.5 = (s32[512]{0:T(512)S(1)}, s32[512]{0:T(512)}, u32[]{:S(2)}) copy-start(s32[512]{0:T(512)} %eq.152) | copy-start | bytes 6148
  83.0 71.1 %copy-start.2 = (bf16[256,512]{1,0:T(8,128)(2,1)S(1)}, bf16[256,512]{1,0:T(8,128)(2,1)}, u32[]{:S(2)}) copy-start(bf16[256,512]{1,0:T(8,128)(2,1)} %broadcast_select_fusion) | copy-start | bytes 786436
  91.7 62.5 %copy-start.1 = (bf16[1024,512]{1,0:T(8,128)(2,1)S(1)}, bf16[1024,512]{1,0:T(8,128)(2,1)}, u32[]{:S(2)}) copy-start(bf16[1024,512]{1,0:T(8,128)(2,1)} %all-gather.7.cloned.1.call-done) | copy-start | bytes 3145732
  91.7 63.7 %all-to-all-start.3 = ((bf16[32,32,512]{2,1,0:T(8,128)(2,1)}), bf16[32,32,512]{2,1,0:T(8,128)(2,1)}, u32[]{:S(2)}, u32[]{:S(2)}) async-start(bf16[32,32,512]{2,1,0:T(8,128)(2,1)} %bitcast.95), calls=%async_computation.3 | async-start | bytes 2097152 | tf_op jit(solution)/shard_map/all_to_all | solution.py:119
  154.0 12.2 %collective-permute-start = (bf16[16,128,512]{2,1,0:T(8,128)(2,1)}, bf16[16,128,512]{2,1,0:T(8,128)(2,1)}, u32[]{:S(2)}, u32[]{:S(2)}) collective-permute-start(bf16[16,128,512]{2,1,0:T(8,128)(2,1)} %bitcast.93), channel_id=1, source_target_pairs={{0,1},{1,0},{2,3},{3,2},{4,5},{5,4},{6,7},{7,6},{8,9},{9,8},{10,11... | collective-permute-start | bytes 6291464 | tf_op jit(solution)/shard_map/ppermute | solution.py:116
  154.1 1.3 copy-start.12
  155.4 5.9 %copy-start.9 = (s32[256]{0:T(256)S(1)}, s32[256]{0:T(256)}, u32[]{:S(2)}) copy-start(s32[256]{0:T(256)} %param.11) | copy-start | bytes 3076
Sparse Core Ops, SparseCore 0:
  37.6 19.7 all-gather.4
  66.3 19.8 all-gather.6
  91.8 62.1 all-gather.8

commit v8 on v6

--- a/solution.py
+++ b/solution.py
@@ -11,9 +11,10 @@
     return jnp.concatenate([rows[..., half_width:], rows[..., :half_width]], axis=-1)
 
 
-def slot_ranks(targets, count):
-    onehot = (targets[:, None] == jnp.arange(count, dtype=jnp.int32)[None, :]).astype(jnp.int32)
-    return jnp.sum((jnp.cumsum(onehot, axis=0) - onehot) * onehot, axis=1)
+def slot_ranks(targets):
+    index = jnp.arange(targets.shape[0], dtype=jnp.int32)
+    earlier_same = (targets[:, None] == targets[None, :]) & (index[:, None] < index[None, :])
+    return jnp.sum(earlier_same.astype(jnp.int32), axis=0)
 
 
 def body(entity_table, relation_table, triple_rel, triple_owners, triple_local, negative_ids):
@@ -27,11 +28,11 @@
     rel_capacity = max(1, 2 * triples // device_count)
     rel_per_group = relation_table.shape[0] // device_count
 
-    owners = triple_owners.reshape(-1)
-    local_rows = triple_local.reshape(-1)
-    ent_pos = owners * capacity + slot_ranks(owners, device_count)
+    owners = jnp.concatenate([triple_owners[:, 0], triple_owners[:, 1]])
+    local_rows = jnp.concatenate([triple_local[:, 0], triple_local[:, 1]])
+    ent_pos = owners * capacity + slot_ranks(owners)
     rel_group = triple_rel // rel_per_group
-    rel_pos = rel_group * rel_capacity + slot_ranks(rel_group, device_count)
+    rel_pos = rel_group * rel_capacity + slot_ranks(rel_group)
     rel_local = triple_rel - rel_group * rel_per_group
 
     ent_place = jnp.arange(device_count * capacity, dtype=jnp.int32)[:, None] == ent_pos[None, :]
@@ -63,9 +64,8 @@
     fetched = jnp.einsum(
         "sj,sc->jc", ent_place_bf, got_rows, preferred_element_type=jnp.float32
     ).astype(jnp.bfloat16)
-    fetched = fetched.reshape(triples, 2, row_width)
-    head_rows = fetched[:, 0]
-    tail_rows = fetched[:, 1]
+    head_rows = fetched[:triples]
+    tail_rows = fetched[triples:]
     rel_rows = jnp.take(relation_table, triple_rel, axis=0)
     query = (
         0.5 * swap_halves(head_rows).astype(jnp.float32) * swap_halves(rel_rows).astype(jnp.float32)
@@ -104,7 +104,7 @@
         "sr,sc->rc", rel_onehot, back_rel, preferred_element_type=jnp.float32
     ).astype(jnp.bfloat16)
 
-    ent_grads = jnp.stack([head_grad, tail_grad], axis=1).reshape(2 * triples, row_width)
+    ent_grads = jnp.concatenate([head_grad, tail_grad], axis=0)
     send_ent = jnp.einsum(
         "sj,jc->sc", ent_place_bf, ent_grads.astype(jnp.bfloat16), preferred_element_type=jnp.float32
     ).astype(jnp.bfloat16)

time: 167 us -> 162 us (0.970)
  local copies, waits for them, and re-layouts: 18.7 us -> 12.7 us
  waiting for transfers between devices: 74.8 us -> 80.1 us
  other arithmetic: 8.25 us -> 4.78 us
    all_to_all x1, waiting for transfers between devices: 7.64 us -> 12.6 us  [body(): lax.all_to_all(send_rel.reshape(device_count, rel_capacity, row_width), A...]
    another operation x7 -> x1, other arithmetic: 3.78 us -> 1.08 us
    unnamed x36 -> x17, local copies, waits for them, and re-layouts: 7.67 us -> 5.2 us
    gather x1 -> x2, local copies, waits for them, and re-layouts: 3.94 us -> 4.07 us  [body(): rel_rows = jnp.take(relation_table, triple_rel, axis=0)]
  transfers between devices with their start and end apart: 6 -> 6, of which waited for: 4 -> 4; matrix products, arithmetic and copies ran while one was open for 22% -> 19% of each run, Pallas kernels for 0% -> 0%
where the time goes in v8:
time: 162 us; the launch traced here: 161 us
  waiting for transfers between devices  80.1 us (49%)
  matrix products  24.3 us (15%)
  blocking collectives  14.4 us (9%)
  between operations  14 us (9%)
  local copies, waits for them, and re-layouts  12.7 us (8%)
  starting transfers between devices  10.9 us (7%)
  other arithmetic  4.78 us (3%)
    all_to_all x1, waiting for transfers between devices, body(): lax.all_to_all(send_ent.reshape(device_count, capacity, row_width), AXES,...  30.7 us
    all_to_all x1, waiting for transfers between devices, body(): lax.all_to_all(served, AXES, split_axis=0, concat_axis=0, tiled=True)  19.8 us
    all_gather x1, waiting for transfers between devices, body(): relation_grad = lax.all_gather(own_rel_grad, AXES, axis=0, tiled=True)  16.9 us
    all_to_all x1, blocking collectives, body(): lax.all_to_all(send_ids, AXES, split_axis=0, concat_axis=0, tiled=True)  14.4 us
    all_to_all x1, waiting for transfers between devices, body(): lax.all_to_all(send_rel.reshape(device_count, rel_capacity, row_width), A...  12.6 us
    dot_general x1, matrix products, body(): jnp.einsum('se,sc->ec', asked_onehot, back_ent, preferred_element_type=jn...  5.92 us
    unnamed x17, local copies, waits for them, and re-layouts  5.2 us
    dot_general x1, matrix products, body(): jnp.einsum('se,sc->ec', neg_onehot, neg_grad.astype(jnp.bfloat16), prefer...  4.84 us
  transfers between devices with their start and end apart: 6, of which 4 were waited for; matrix products, arithmetic and copies ran while one was open for 19% of the time, Pallas kernels for 0%

profile of v8, /device:TPU:0, one launch (start us, length us, event | category | flops | bytes accessed | tf_op | source)
XLA Modules:
  0.0 161.1 jit_solution(13306430086694697640)
XLA Ops:
  7.2 0.0 copy-start
  7.2 0.9 fusion.40
  8.0 0.2 convert_reduce_fusion
  8.2 0.8 fusion.41
  9.0 0.3 select_reduce_fusion
  9.3 0.1 stack_reshape.3
  9.4 0.7 multiply_subtract_fusion
  10.1 0.1 convert_reduce_fusion.1
  10.2 0.2 select_reduce_fusion.1
  10.3 0.1 reshape.73
  10.5 14.4 %all_to_all.20 = s32[32,2,32]{2,1,0:T(2,128)S(1)} all-to-all(s32[32,2,32]{2,1,0:T(2,128)S(1)} %copy.19), channel_id=1, replica_groups=mesh['wide'=8,'narrow'=4] {'wide','narrow'}, dimensions={0} | all-to-all | bytes 16384 | tf_op jit(solution)/shard_map/all_to_all | solution.py:51
  24.9 0.1 eq.107
  25.0 3.3 %fusion.6 = bf16[1024,512]{1,0:T(8,128)(2,1)} fusion(bf16[2048,512]{1,0:T(8,128)(2,1)S(1)} %copy-done, s32[1024]{0:T(1024)S(1)} %eq.107), kind=kOutput, calls=%fused_computation.14 | convolution fusion | flops 2150105088 | bytes 3149824 | tf_op jit(solution)/shard_map/se,ec->sc/dot_general | solution.py:57
  28.3 3.5 %all-to-all-start.1 = ((bf16[32,32,512]{2,1,0:T(8,128)(2,1)}), bf16[32,32,512]{2,1,0:T(8,128)(2,1)}, u32[]{:S(2)}, u32[]{:S(2)}) async-start(bf16[32,32,512]{2,1,0:T(8,128)(2,1)} %bitcast.5), calls=%async_computation.1 | async-start | bytes 2097152 | tf_op jit(solution)/shard_map/all_to_all | solution.py:61
  31.9 0.0 all-gather.4.cloned.1.call-start
  31.9 1.2 gather_fusion.1
  33.1 0.1 copy.21
  33.3 0.7 broadcast_select_fusion
  34.0 0.0 all-gather.4.cloned.1.call-update
  34.0 0.0 all-gather.6.cloned.1.call-start
  34.1 3.9 %gather_fusion = bf16[256,512]{1,0:T(8,128)(2,1)S(1)} fusion(bf16[4096,512]{1,0:T(8,128)(2,1)} %param.7, s32[1024]{0:T(1024)S(1)} %pad_clamp_fusion.1), kind=kCustom, calls=%fused_computation | custom fusion | bytes 525312 | tf_op jit(solution)/shard_map/jit(_take)/gather | solution.py:69
  38.0 0.1 copy.20
  38.2 19.8 %all-to-all-done.1 = bf16[32,32,512]{2,1,0:T(8,128)(2,1)} async-done(((bf16[32,32,512]{2,1,0:T(8,128)(2,1)}), bf16[32,32,512]{2,1,0:T(8,128)(2,1)}, u32[]{:S(2)}, u32[]{:S(2)}) %all-to-all-start.1) | async-done | bytes 1048608 | tf_op jit(solution)/shard_map/all_to_all | solution.py:61
  58.0 2.0 %fusion.12 = bf16[512,512]{0,1:T(8,128)(2,1)S(1)} fusion(bf16[1024,512]{1,0:T(8,128)(2,1)} %bitcast.6, s32[512]{0:T(512)S(1)} %multiply_add_fusion), kind=kOutput, calls=%fused_computation.21 | convolution fusion | flops 537657344 | bytes 1574912 | tf_op jit(solution)/shard_map/sj,sc->jc/dot_general | solution.py:64
  60.1 0.9 fusion.20
  60.9 0.0 all-gather.6.cloned.1.call-update
  60.9 0.0 all-gather.4.cloned.1.call-done
  61.0 2.4 %fusion.14 = (f32[256]{0:T(256)S(1)}, f32[256,1024]{1,0:T(8,128)S(1)}) fusion(bf16[256,512]{0,1:T(8,128)(2,1)} %get-tuple-element.10, bf16[1024,512]{0,1:T(8,128)(2,1)} %all-gather.4.cloned.1.call-done), kind=kOutput, calls=%fused_computation.27 | convolution fusion | flops 270270208 | bytes 2360320 | tf_op jit(solution)/shard_map/tc,kc->tk/dot_general | solution.py:78
  63.4 0.6 fusion.31
  64.0 0.6 convolution_add_fusion
  64.6 0.7 copy-done.4
  65.3 1.1 convolution_convert_fusion
  66.4 3.5 %all-to-all-start.2 = ((bf16[32,16,512]{2,1,0:T(8,128)(2,1)}), bf16[32,16,512]{2,1,0:T(8,128)(2,1)S(1)}, u32[]{:S(2)}, u32[]{:S(2)}) async-start(bf16[32,16,512]{2,1,0:T(8,128)(2,1)} %bitcast.25), calls=%async_computation.2 | async-start | bytes 1048576 | tf_op jit(solution)/shard_map/all_to_all | solution.py:97
  70.0 0.0 all-gather.8.cloned.1.call-start
  70.0 0.1 slice_reduce_fusion
  70.1 0.1 eq.111
  70.2 1.1 fusion.19
  71.2 1.7 %fusion.7 = bf16[1024,512]{1,0:T(8,128)(2,1)} fusion(s32[512]{0:T(512)S(1)} %multiply_add_fusion, bf16[256,512]{0,1:T(8,128)(2,1)S(1)} %get-tuple-element.28, bf16[256,512]{0,1:T(8,128)(2,1)S(1)} %get-tuple-element.29), kind=kOutput, calls=%fused_computation.15 | convolution fusion | flops 538968064 | bytes 1574912 | tf_op jit(solution)/shard_map/sj,jc->sc/dot_general | solution.py:108
  72.9 12.6 %all-to-all-done.2 = bf16[32,16,512]{2,1,0:T(8,128)(2,1)S(1)} async-done(((bf16[32,16,512]{2,1,0:T(8,128)(2,1)}), bf16[32,16,512]{2,1,0:T(8,128)(2,1)S(1)}, u32[]{:S(2)}, u32[]{:S(2)}) %all-to-all-start.2) | async-done | bytes 524320 | tf_op jit(solution)/shard_map/all_to_all | solution.py:97
  85.6 1.0 convolution_convert_fusion.2
  86.6 0.0 all-gather.8.cloned.1.call-update
  86.6 3.7 %all-to-all-start.3 = ((bf16[32,32,512]{2,1,0:T(8,128)(2,1)}), bf16[32,32,512]{2,1,0:T(8,128)(2,1)}, u32[]{:S(2)}, u32[]{:S(2)}) async-start(bf16[32,32,512]{2,1,0:T(8,128)(2,1)} %bitcast.24), calls=%async_computation.3 | async-start | bytes 2097152 | tf_op jit(solution)/shard_map/all_to_all | solution.py:113
  90.4 1.4 fusion.13
  91.7 30.7 %all-to-all-done.3 = bf16[32,32,512]{2,1,0:T(8,128)(2,1)} async-done(((bf16[32,32,512]{2,1,0:T(8,128)(2,1)}), bf16[32,32,512]{2,1,0:T(8,128)(2,1)}, u32[]{:S(2)}, u32[]{:S(2)}) %all-to-all-start.3) | async-done | bytes 1048608 | tf_op jit(solution)/shard_map/all_to_all | solution.py:113
  122.5 5.9 %fusion = f32[2048,512]{1,0:T(8,128)} fusion(bf16[1024,512]{1,0:T(8,128)(2,1)} %bitcast.10, s32[1024]{0:T(1024)S(1)} %eq.107), kind=kOutput, calls=%fused_computation.3 | convolution fusion | flops 2149580800 | bytes 5246976 | tf_op jit(solution)/shard_map/se,sc->ec/dot_general | solution.py:122
  128.4 4.8 %add_convert_fusion = bf16[2048,512]{1,0:T(8,128)(2,1)} fusion(f32[2048,512]{1,0:T(8,128)} %fusion, bf16[1024,256]{1,0:T(8,128)(2,1)} %fusion.13, bf16[1024,512]{0,1:T(8,128)(2,1)S(1)} %copy-done.2, s32[256]{0:T(256)S(1)} %copy-done.5), kind=kOutput, calls=%fused_computation.5 | convolution fusion | flops 808058880 | bytes 7865344 | tf_op jit(solution)/shard_map/se,sc->ec/dot_general | solution.py:124
  133.2 16.9 %all-gather.8.cloned.1.call-done = bf16[4096,512]{1,0:T(8,128)(2,1)} async-done(((bf16[128,512]{1,0:T(8,128)(2,1)}), bf16[4096,512]{1,0:T(8,128)(2,1)}) %all-gather.8.cloned.1.call-update) | async-done | bytes 4194320 | tf_op jit(solution)/shard_map/all_gather | solution.py:112
  150.1 4.5 %copy.25 = bf16[4096,512]{1,0:T(8,128)(2,1)} copy(bf16[4096,512]{1,0:T(8,128)(2,1)} %all-gather.8.cloned.1.call-done) | data formatting | bytes 8388608
  (32 shorter events, 0.3 us)
Async XLA Ops:
  7.2 17.8 %copy-start = (bf16[2048,512]{1,0:T(8,128)(2,1)S(1)}, bf16[2048,512]{1,0:T(8,128)(2,1)}, u32[]{:S(2)}) copy-start(bf16[2048,512]{1,0:T(8,128)(2,1)} %param.6) | copy-start | bytes 6291460
  28.3 3.6 %copy-start.5 = (s32[256]{0:T(256)S(1)}, s32[256]{0:T(256)}, u32[]{:S(2)}) copy-start(s32[256]{0:T(256)} %param.11) | copy-start | bytes 3076
  28.3 29.7 %all-to-all-start.1 = ((bf16[32,32,512]{2,1,0:T(8,128)(2,1)}), bf16[32,32,512]{2,1,0:T(8,128)(2,1)}, u32[]{:S(2)}, u32[]{:S(2)}) async-start(bf16[32,32,512]{2,1,0:T(8,128)(2,1)} %bitcast.5), calls=%async_computation.1 | async-start | bytes 2097152 | tf_op jit(solution)/shard_map/all_to_all | solution.py:61
  31.9 29.1 %all-gather.4.cloned.1.call-start = ((), (), s32[]{:S(2)}) async-start(), calls=%async_computation.4 | async-start | bytes 1310720 | tf_op jit(solution)/shard_map/all_gather | solution.py:76
  33.1 5.1 %copy-start.6 = (s32[256]{0:T(256)S(1)}, s32[256]{0:T(256)}, u32[]{:S(2)}) copy-start(s32[256]{0:T(256)} %param.8) | copy-start | bytes 3076
  34.0 52.6 %all-gather.6.cloned.1.call-start = ((), (), s32[]{:S(2)}) async-start(), calls=%async_computation.5 | async-start | bytes 1310720 | tf_op jit(solution)/shard_map/all_gather | solution.py:89
  61.0 3.0 %copy-start.7 = (bf16[1024,512]{0,1:T(8,128)(2,1)S(1)}, bf16[1024,512]{0,1:T(8,128)(2,1)}, u32[]{:S(2)}) copy-start(bf16[1024,512]{0,1:T(8,128)(2,1)} %all-gather.4.cloned.1.call-done) | copy-start | bytes 3145732
  64.5 5.6 %copy-start.1 = (bf16[256,512]{0,1:T(8,128)(2,1)S(1)}, bf16[256,512]{0,1:T(8,128)(2,1)}, u32[]{:S(2)}) copy-start(bf16[256,512]{0,1:T(8,128)(2,1)} %get-tuple-element.10) | copy-start | bytes 786436
  64.6 0.7 copy-start.4
  66.4 19.1 %all-to-all-start.2 = ((bf16[32,16,512]{2,1,0:T(8,128)(2,1)}), bf16[32,16,512]{2,1,0:T(8,128)(2,1)S(1)}, u32[]{:S(2)}, u32[]{:S(2)}) async-start(bf16[32,16,512]{2,1,0:T(8,128)(2,1)} %bitcast.25), calls=%async_computation.2 | async-start | bytes 1048576 | tf_op jit(solution)/shard_map/all_to_all | solution.py:97
  70.0 80.2 %all-gather.8.cloned.1.call-start = ((), (), s32[]{:S(2)}) async-start(), calls=%async_computation.6 | async-start | bytes 4325376 | tf_op jit(solution)/shard_map/all_gather | solution.py:112
  72.9 17.4 %copy-start.3 = (bf16[256,512]{0,1:T(8,128)(2,1)S(1)}, bf16[256,512]{0,1:T(8,128)(2,1)}, u32[]{:S(2)}) copy-start(bf16[256,512]{0,1:T(8,128)(2,1)} %broadcast_select_fusion) | copy-start | bytes 786436
  86.6 3.8 %copy-start.2 = (bf16[1024,512]{0,1:T(8,128)(2,1)S(1)}, bf16[1024,512]{0,1:T(8,128)(2,1)}, u32[]{:S(2)}) copy-start(bf16[1024,512]{0,1:T(8,128)(2,1)} %all-gather.6.cloned.1.call-done) | copy-start | bytes 3145732
  86.6 35.8 %all-to-all-start.3 = ((bf16[32,32,512]{2,1,0:T(8,128)(2,1)}), bf16[32,32,512]{2,1,0:T(8,128)(2,1)}, u32[]{:S(2)}, u32[]{:S(2)}) async-start(bf16[32,32,512]{2,1,0:T(8,128)(2,1)} %bitcast.24), calls=%async_computation.3 | async-start | bytes 2097152 | tf_op jit(solution)/shard_map/all_to_all | solution.py:113
Sparse Core Ops, SparseCore 0:
  34.2 19.8 all-gather.3
  61.1 19.9 all-gather.5
  86.7 63.3 all-gather.7

commit v9 on v8

--- a/solution.py
+++ b/solution.py
@@ -61,8 +61,11 @@
     got_rows = lax.all_to_all(served, AXES, split_axis=0, concat_axis=0, tiled=True)
     got_rows = got_rows.reshape(device_count * capacity, row_width)
     ent_place_bf = ent_place.astype(jnp.bfloat16)
+    ent_pick = (ent_pos[:, None] == jnp.arange(device_count * capacity, dtype=jnp.int32)[None, :]).astype(
+        jnp.bfloat16
+    )
     fetched = jnp.einsum(
-        "sj,sc->jc", ent_place_bf, got_rows, preferred_element_type=jnp.float32
+        "js,sc->jc", ent_pick, got_rows, preferred_element_type=jnp.float32
     ).astype(jnp.bfloat16)
     head_rows = fetched[:triples]
     tail_rows = fetched[triples:]
@@ -98,10 +101,10 @@
         send_rel.reshape(device_count, rel_capacity, row_width), AXES, split_axis=0, concat_axis=0, tiled=True
     ).reshape(-1, row_width)
     rel_onehot = (
-        rel_ids_in[:, None] == jnp.arange(rel_per_group, dtype=jnp.int32)[None, :]
+        jnp.arange(rel_per_group, dtype=jnp.int32)[:, None] == rel_ids_in[None, :]
     ).astype(jnp.bfloat16)
     own_rel_grad = jnp.einsum(
-        "sr,sc->rc", rel_onehot, back_rel, preferred_element_type=jnp.float32
+        "rs,sc->rc", rel_onehot, back_rel, preferred_element_type=jnp.float32
     ).astype(jnp.bfloat16)
 
     ent_grads = jnp.concatenate([head_grad, tail_grad], axis=0)

time: 162 us -> 162 us (level)
  no operation moved by 1% of the time
where the time goes in v9:
time: 162 us; the launch traced here: 161 us
  waiting for transfers between devices  80.1 us (49%)
  matrix products  24.3 us (15%)
  blocking collectives  14.4 us (9%)
  between operations  14 us (9%)
  local copies, waits for them, and re-layouts  12.7 us (8%)
  starting transfers between devices  10.9 us (7%)
  other arithmetic  4.78 us (3%)
    all_to_all x1, waiting for transfers between devices, body(): lax.all_to_all(send_ent.reshape(device_count, capacity, row_width), AXES,...  30.7 us
    all_to_all x1, waiting for transfers between devices, body(): lax.all_to_all(served, AXES, split_axis=0, concat_axis=0, tiled=True)  19.8 us
    all_gather x1, waiting for transfers between devices, body(): relation_grad = lax.all_gather(own_rel_grad, AXES, axis=0, tiled=True)  16.9 us
    all_to_all x1, blocking collectives, body(): lax.all_to_all(send_ids, AXES, split_axis=0, concat_axis=0, tiled=True)  14.4 us
    all_to_all x1, waiting for transfers between devices, body(): lax.all_to_all(send_rel.reshape(device_count, rel_capacity, row_width), A...  12.6 us
    dot_general x1, matrix products, body(): jnp.einsum('se,sc->ec', asked_onehot, back_ent, preferred_element_type=jn...  5.92 us
    unnamed x17, local copies, waits for them, and re-layouts  5.2 us
    dot_general x1, matrix products, body(): jnp.einsum('se,sc->ec', neg_onehot, neg_grad.astype(jnp.bfloat16), prefer...  4.84 us
  transfers between devices with their start and end apart: 6, of which 4 were waited for; matrix products, arithmetic and copies ran while one was open for 19% of the time, Pallas kernels for 0%

profile of v9, /device:TPU:0, one launch (start us, length us, event | category | flops | bytes accessed | tf_op | source)
XLA Modules:
  0.0 161.1 jit_solution(16709058237782559630)
XLA Ops:
  7.2 0.0 copy-start
  7.2 0.9 fusion.40
  8.0 0.2 convert_reduce_fusion
  8.2 0.8 fusion.41
  9.0 0.3 select_reduce_fusion
  9.3 0.1 stack_reshape.3
  9.4 0.7 multiply_subtract_fusion
  10.1 0.1 convert_reduce_fusion.1
  10.2 0.2 select_reduce_fusion.1
  10.3 0.1 reshape.91
  10.5 14.4 %all_to_all.20 = s32[32,2,32]{2,1,0:T(2,128)S(1)} all-to-all(s32[32,2,32]{2,1,0:T(2,128)S(1)} %copy.19), channel_id=1, replica_groups=mesh['wide'=8,'narrow'=4] {'wide','narrow'}, dimensions={0} | all-to-all | bytes 16384 | tf_op jit(solution)/shard_map/all_to_all | solution.py:51
  24.9 0.1 eq.120
  25.0 3.3 %fusion.6 = bf16[1024,512]{1,0:T(8,128)(2,1)} fusion(bf16[2048,512]{1,0:T(8,128)(2,1)S(1)} %copy-done, s32[1024]{0:T(1024)S(1)} %eq.120), kind=kOutput, calls=%fused_computation.15 | convolution fusion | flops 2150105088 | bytes 3149824 | tf_op jit(solution)/shard_map/se,ec->sc/dot_general | solution.py:57
  28.3 3.5 %all-to-all-start.1 = ((bf16[32,32,512]{2,1,0:T(8,128)(2,1)}), bf16[32,32,512]{2,1,0:T(8,128)(2,1)}, u32[]{:S(2)}, u32[]{:S(2)}) async-start(bf16[32,32,512]{2,1,0:T(8,128)(2,1)} %bitcast.5), calls=%async_computation.1 | async-start | bytes 2097152 | tf_op jit(solution)/shard_map/all_to_all | solution.py:61
  31.9 0.0 all-gather.4.cloned.1.call-start
  31.9 1.2 gather_fusion.1
  33.1 0.1 copy.21
  33.3 0.7 broadcast_select_fusion
  34.0 0.0 all-gather.4.cloned.1.call-update
  34.0 0.0 all-gather.6.cloned.1.call-start
  34.1 3.9 %gather_fusion = bf16[256,512]{1,0:T(8,128)(2,1)S(1)} fusion(bf16[4096,512]{1,0:T(8,128)(2,1)} %param.7, s32[1024]{0:T(1024)S(1)} %pad_clamp_fusion.1), kind=kCustom, calls=%fused_computation | custom fusion | bytes 525312 | tf_op jit(solution)/shard_map/jit(_take)/gather | solution.py:72
  38.0 0.1 copy.20
  38.2 19.8 %all-to-all-done.1 = bf16[32,32,512]{2,1,0:T(8,128)(2,1)} async-done(((bf16[32,32,512]{2,1,0:T(8,128)(2,1)}), bf16[32,32,512]{2,1,0:T(8,128)(2,1)}, u32[]{:S(2)}, u32[]{:S(2)}) %all-to-all-start.1) | async-done | bytes 1048608 | tf_op jit(solution)/shard_map/all_to_all | solution.py:61
  58.0 2.1 %fusion.12 = bf16[512,512]{0,1:T(8,128)(2,1)S(1)} fusion(bf16[1024,512]{1,0:T(8,128)(2,1)} %bitcast.6, s32[512]{0:T(512)S(1)} %multiply_add_fusion), kind=kOutput, calls=%fused_computation.22 | convolution fusion | flops 537657344 | bytes 1574912 | tf_op jit(solution)/shard_map/js,sc->jc/dot_general | solution.py:67
  60.2 0.9 fusion.20
  61.0 0.0 all-gather.6.cloned.1.call-update
  61.0 0.0 all-gather.4.cloned.1.call-done
  61.1 2.4 %fusion.14 = (f32[256]{0:T(256)S(1)}, f32[256,1024]{1,0:T(8,128)S(1)}) fusion(bf16[256,512]{0,1:T(8,128)(2,1)} %get-tuple-element.10, bf16[1024,512]{0,1:T(8,128)(2,1)} %all-gather.4.cloned.1.call-done), kind=kOutput, calls=%fused_computation.28 | convolution fusion | flops 270270208 | bytes 2360320 | tf_op jit(solution)/shard_map/tc,kc->tk/dot_general | solution.py:81
  63.5 0.6 fusion.31
  64.1 0.6 convolution_add_fusion
  64.7 0.7 copy-done.4
  65.4 1.1 convolution_convert_fusion
  66.5 3.5 %all-to-all-start.2 = ((bf16[32,16,512]{2,1,0:T(8,128)(2,1)}), bf16[32,16,512]{2,1,0:T(8,128)(2,1)S(1)}, u32[]{:S(2)}, u32[]{:S(2)}) async-start(bf16[32,16,512]{2,1,0:T(8,128)(2,1)} %bitcast.25), calls=%async_computation.2 | async-start | bytes 1048576 | tf_op jit(solution)/shard_map/all_to_all | solution.py:100
  70.1 0.0 all-gather.8.cloned.1.call-start
  70.1 0.1 slice_reduce_fusion
  70.2 0.1 eq.125
  70.3 1.1 fusion.19
  71.3 1.7 %fusion.7 = bf16[1024,512]{1,0:T(8,128)(2,1)} fusion(s32[512]{0:T(512)S(1)} %multiply_add_fusion, bf16[256,512]{0,1:T(8,128)(2,1)S(1)} %get-tuple-element.28, bf16[256,512]{0,1:T(8,128)(2,1)S(1)} %get-tuple-element.29), kind=kOutput, calls=%fused_computation.16 | convolution fusion | flops 538968064 | bytes 1574912 | tf_op jit(solution)/shard_map/sj,jc->sc/dot_general | solution.py:111
  73.1 12.6 %all-to-all-done.2 = bf16[32,16,512]{2,1,0:T(8,128)(2,1)S(1)} async-done(((bf16[32,16,512]{2,1,0:T(8,128)(2,1)}), bf16[32,16,512]{2,1,0:T(8,128)(2,1)S(1)}, u32[]{:S(2)}, u32[]{:S(2)}) %all-to-all-start.2) | async-done | bytes 524320 | tf_op jit(solution)/shard_map/all_to_all | solution.py:100
  85.7 0.9 convolution_convert_fusion.2
  86.6 0.0 all-gather.8.cloned.1.call-update
  86.6 3.7 %all-to-all-start.3 = ((bf16[32,32,512]{2,1,0:T(8,128)(2,1)}), bf16[32,32,512]{2,1,0:T(8,128)(2,1)}, u32[]{:S(2)}, u32[]{:S(2)}) async-start(bf16[32,32,512]{2,1,0:T(8,128)(2,1)} %bitcast.24), calls=%async_computation.3 | async-start | bytes 2097152 | tf_op jit(solution)/shard_map/all_to_all | solution.py:116
  90.3 1.4 fusion.13
  91.7 30.7 %all-to-all-done.3 = bf16[32,32,512]{2,1,0:T(8,128)(2,1)} async-done(((bf16[32,32,512]{2,1,0:T(8,128)(2,1)}), bf16[32,32,512]{2,1,0:T(8,128)(2,1)}, u32[]{:S(2)}, u32[]{:S(2)}) %all-to-all-start.3) | async-done | bytes 1048608 | tf_op jit(solution)/shard_map/all_to_all | solution.py:116
  122.4 5.9 %fusion = f32[2048,512]{1,0:T(8,128)} fusion(bf16[1024,512]{1,0:T(8,128)(2,1)} %bitcast.10, s32[1024]{0:T(1024)S(1)} %eq.120), kind=kOutput, calls=%fused_computation.3 | convolution fusion | flops 2149580800 | bytes 5246976 | tf_op jit(solution)/shard_map/se,sc->ec/dot_general | solution.py:125
  128.4 4.8 %add_convert_fusion = bf16[2048,512]{1,0:T(8,128)(2,1)} fusion(f32[2048,512]{1,0:T(8,128)} %fusion, bf16[1024,256]{1,0:T(8,128)(2,1)} %fusion.13, bf16[1024,512]{0,1:T(8,128)(2,1)S(1)} %copy-done.2, s32[256]{0:T(256)S(1)} %copy-done.5), kind=kOutput, calls=%fused_computation.5 | convolution fusion | flops 808058880 | bytes 7865344 | tf_op jit(solution)/shard_map/se,sc->ec/dot_general | solution.py:127
  133.2 16.9 %all-gather.8.cloned.1.call-done = bf16[4096,512]{1,0:T(8,128)(2,1)} async-done(((bf16[128,512]{1,0:T(8,128)(2,1)}), bf16[4096,512]{1,0:T(8,128)(2,1)}) %all-gather.8.cloned.1.call-update) | async-done | bytes 4194320 | tf_op jit(solution)/shard_map/all_gather | solution.py:115
  150.1 4.5 %copy.25 = bf16[4096,512]{1,0:T(8,128)(2,1)} copy(bf16[4096,512]{1,0:T(8,128)(2,1)} %all-gather.8.cloned.1.call-done) | data formatting | bytes 8388608
  (32 shorter events, 0.3 us)
Async XLA Ops:
  7.2 17.8 %copy-start = (bf16[2048,512]{1,0:T(8,128)(2,1)S(1)}, bf16[2048,512]{1,0:T(8,128)(2,1)}, u32[]{:S(2)}) copy-start(bf16[2048,512]{1,0:T(8,128)(2,1)} %param.6) | copy-start | bytes 6291460
  28.3 3.6 %copy-start.5 = (s32[256]{0:T(256)S(1)}, s32[256]{0:T(256)}, u32[]{:S(2)}) copy-start(s32[256]{0:T(256)} %param.11) | copy-start | bytes 3076
  28.3 29.7 %all-to-all-start.1 = ((bf16[32,32,512]{2,1,0:T(8,128)(2,1)}), bf16[32,32,512]{2,1,0:T(8,128)(2,1)}, u32[]{:S(2)}, u32[]{:S(2)}) async-start(bf16[32,32,512]{2,1,0:T(8,128)(2,1)} %bitcast.5), calls=%async_computation.1 | async-start | bytes 2097152 | tf_op jit(solution)/shard_map/all_to_all | solution.py:61
  31.9 29.2 %all-gather.4.cloned.1.call-start = ((), (), s32[]{:S(2)}) async-start(), calls=%async_computation.4 | async-start | bytes 1310720 | tf_op jit(solution)/shard_map/all_gather | solution.py:79
  33.1 5.1 %copy-start.6 = (s32[256]{0:T(256)S(1)}, s32[256]{0:T(256)}, u32[]{:S(2)}) copy-start(s32[256]{0:T(256)} %param.8) | copy-start | bytes 3076
  34.0 52.6 %all-gather.6.cloned.1.call-start = ((), (), s32[]{:S(2)}) async-start(), calls=%async_computation.5 | async-start | bytes 1310720 | tf_op jit(solution)/shard_map/all_gather | solution.py:92
  61.1 3.0 %copy-start.7 = (bf16[1024,512]{0,1:T(8,128)(2,1)S(1)}, bf16[1024,512]{0,1:T(8,128)(2,1)}, u32[]{:S(2)}) copy-start(bf16[1024,512]{0,1:T(8,128)(2,1)} %all-gather.4.cloned.1.call-done) | copy-start | bytes 3145732
  64.6 5.6 %copy-start.1 = (bf16[256,512]{0,1:T(8,128)(2,1)S(1)}, bf16[256,512]{0,1:T(8,128)(2,1)}, u32[]{:S(2)}) copy-start(bf16[256,512]{0,1:T(8,128)(2,1)} %get-tuple-element.10) | copy-start | bytes 786436
  64.7 0.7 copy-start.4
  66.5 19.2 %all-to-all-start.2 = ((bf16[32,16,512]{2,1,0:T(8,128)(2,1)}), bf16[32,16,512]{2,1,0:T(8,128)(2,1)S(1)}, u32[]{:S(2)}, u32[]{:S(2)}) async-start(bf16[32,16,512]{2,1,0:T(8,128)(2,1)} %bitcast.25), calls=%async_computation.2 | async-start | bytes 1048576 | tf_op jit(solution)/shard_map/all_to_all | solution.py:100
  70.1 80.0 %all-gather.8.cloned.1.call-start = ((), (), s32[]{:S(2)}) async-start(), calls=%async_computation.6 | async-start | bytes 4325376 | tf_op jit(solution)/shard_map/all_gather | solution.py:115
  73.1 17.3 %copy-start.3 = (bf16[256,512]{0,1:T(8,128)(2,1)S(1)}, bf16[256,512]{0,1:T(8,128)(2,1)}, u32[]{:S(2)}) copy-start(bf16[256,512]{0,1:T(8,128)(2,1)} %broadcast_select_fusion) | copy-start | bytes 786436
  86.6 3.8 %copy-start.2 = (bf16[1024,512]{0,1:T(8,128)(2,1)S(1)}, bf16[1024,512]{0,1:T(8,128)(2,1)}, u32[]{:S(2)}) copy-start(bf16[1024,512]{0,1:T(8,128)(2,1)} %all-gather.6.cloned.1.call-done) | copy-start | bytes 3145732
  86.6 35.8 %all-to-all-start.3 = ((bf16[32,32,512]{2,1,0:T(8,128)(2,1)}), bf16[32,32,512]{2,1,0:T(8,128)(2,1)}, u32[]{:S(2)}, u32[]{:S(2)}) async-start(bf16[32,32,512]{2,1,0:T(8,128)(2,1)} %bitcast.24), calls=%async_computation.3 | async-start | bytes 2097152 | tf_op jit(solution)/shard_map/all_to_all | solution.py:116
Sparse Core Ops, SparseCore 0:
  34.2 19.8 all-gather.3
  61.2 19.9 all-gather.5
  86.7 63.3 all-gather.7

commit v10 on v8

--- a/solution.py
+++ b/solution.py
@@ -110,19 +110,19 @@
     ).astype(jnp.bfloat16)
     own_rel_grad, send_ent, group_query = lax.optimization_barrier((own_rel_grad, send_ent, group_query))
     relation_grad = lax.all_gather(own_rel_grad, AXES, axis=0, tiled=True)
+    own_scores = jnp.einsum("tc,kc->tk", group_query, own_negs, preferred_element_type=jnp.float32)
+    own_weights = (jax.nn.sigmoid(own_scores) / group_neg).astype(jnp.bfloat16)
+    neg_grad = jnp.einsum("tk,tc->kc", own_weights, group_query, preferred_element_type=jnp.float32)
+    neg_onehot = (negative_ids[:, None] == entity_iota).astype(jnp.bfloat16)
+    neg_part = jnp.einsum(
+        "se,sc->ec", neg_onehot, neg_grad.astype(jnp.bfloat16), preferred_element_type=jnp.float32
+    )
+    send_ent, neg_part = lax.optimization_barrier((send_ent, neg_part))
     back_ent = lax.all_to_all(
         send_ent.reshape(device_count, capacity, row_width), AXES, split_axis=0, concat_axis=0, tiled=True
     ).reshape(-1, row_width)
-
-    own_scores = jnp.einsum("tc,kc->tk", group_query, own_negs, preferred_element_type=jnp.float32)
-    own_weights = (jax.nn.sigmoid(own_scores) / group_neg).astype(jnp.bfloat16)
-    neg_grad = jnp.einsum("tk,tc->kc", own_weights, group_query, preferred_element_type=jnp.float32)
-
-    neg_onehot = (negative_ids[:, None] == entity_iota).astype(jnp.bfloat16)
-    entity_grad = jnp.einsum(
-        "se,sc->ec", asked_onehot, back_ent, preferred_element_type=jnp.float32
-    ) + jnp.einsum(
-        "se,sc->ec", neg_onehot, neg_grad.astype(jnp.bfloat16), preferred_element_type=jnp.float32
+    entity_grad = (
+        jnp.einsum("se,sc->ec", asked_onehot, back_ent, preferred_element_type=jnp.float32) + neg_part
     )
     return (entity_grad.astype(jnp.bfloat16), relation_grad, loss)
 

time: 162 us -> 162 us (level)
  blocking collectives: 14.4 us -> 50.8 us
  waiting for transfers between devices: 80.1 us -> 46.4 us
  starting transfers between devices: 10.9 us -> 7.34 us
    all_to_all x0 -> x1, blocking collectives: none -> 36.4 us  [body(): lax.all_to_all(send_ent.reshape(device_count, capacity, row_width), AXES,...]
    all_to_all x1 -> x0, waiting for transfers between devices: 30.7 us -> none  [body(): lax.all_to_all(send_ent.reshape(device_count, capacity, row_width), AXES,...]
    all_to_all x1 -> x0, starting transfers between devices: 3.71 us -> none  [body(): lax.all_to_all(send_ent.reshape(device_count, capacity, row_width), AXES,...]
    all_gather x1, waiting for transfers between devices: 16.9 us -> 14.2 us  [body(): relation_grad = lax.all_gather(own_rel_grad, AXES, axis=0, tiled=True)]
  transfers between devices with their start and end apart: 6 -> 5, of which waited for: 4 -> 3; matrix products, arithmetic and copies ran while one was open for 19% -> 19% of each run, Pallas kernels for 0% -> 0%
where the time goes in v10:
time: 162 us
  blocking collectives  50.8 us (31%)
  waiting for transfers between devices  46.4 us (29%)
  matrix products  25.8 us (16%)
  between operations  14 us (9%)
  local copies, waits for them, and re-layouts  12.7 us (8%)
  starting transfers between devices  7.34 us (5%)
  other arithmetic  4.76 us (3%)
    all_to_all x1, blocking collectives, body(): lax.all_to_all(send_ent.reshape(device_count, capacity, row_width), AXES,...  36.4 us
    all_to_all x1, waiting for transfers between devices, body(): lax.all_to_all(served, AXES, split_axis=0, concat_axis=0, tiled=True)  19.8 us
    all_to_all x1, blocking collectives, body(): lax.all_to_all(send_ids, AXES, split_axis=0, concat_axis=0, tiled=True)  14.4 us
    all_gather x1, waiting for transfers between devices, body(): relation_grad = lax.all_gather(own_rel_grad, AXES, axis=0, tiled=True)  14.2 us
    all_to_all x1, waiting for transfers between devices, body(): lax.all_to_all(send_rel.reshape(device_count, rel_capacity, row_width), A...  12.4 us
    dot_general x1, matrix products, body(): jnp.einsum('se,sc->ec', asked_onehot, back_ent, preferred_element_type=jn...  6.39 us
    unnamed x17, local copies, waits for them, and re-layouts  5.2 us
    dot_general x1, matrix products, body(): jnp.einsum('se,sc->ec', neg_onehot, neg_grad.astype(jnp.bfloat16), prefer...  4.64 us
  transfers between devices with their start and end apart: 5, of which 3 were waited for; matrix products, arithmetic and copies ran while one was open for 19% of the time, Pallas kernels for 0%

profile of v10, /device:TPU:0, one launch (start us, length us, event | category | flops | bytes accessed | tf_op | source)
XLA Modules:
  0.0 161.8 jit_solution(230402098698911555)
XLA Ops:
  7.2 0.0 copy-start
  7.2 0.9 fusion.41
  8.0 0.2 convert_reduce_fusion
  8.2 0.8 fusion.42
  9.0 0.3 select_reduce_fusion
  9.3 0.1 stack_reshape.3
  9.4 0.7 multiply_subtract_fusion
  10.1 0.1 convert_reduce_fusion.1
  10.2 0.2 select_reduce_fusion.1
  10.3 0.1 reshape.73
  10.5 14.4 %all_to_all.20 = s32[32,2,32]{2,1,0:T(2,128)S(1)} all-to-all(s32[32,2,32]{2,1,0:T(2,128)S(1)} %copy.19), channel_id=1, replica_groups=mesh['wide'=8,'narrow'=4] {'wide','narrow'}, dimensions={0} | all-to-all | bytes 16384 | tf_op jit(solution)/shard_map/all_to_all | solution.py:51
  24.9 0.1 eq.107
  25.0 3.3 %fusion.7 = bf16[1024,512]{1,0:T(8,128)(2,1)} fusion(bf16[2048,512]{1,0:T(8,128)(2,1)S(1)} %copy-done, s32[1024]{0:T(1024)S(1)} %eq.107), kind=kOutput, calls=%fused_computation.15 | convolution fusion | flops 2150105088 | bytes 3149824 | tf_op jit(solution)/shard_map/se,ec->sc/dot_general | solution.py:57
  28.3 3.5 %all-to-all-start.1 = ((bf16[32,32,512]{2,1,0:T(8,128)(2,1)}), bf16[32,32,512]{2,1,0:T(8,128)(2,1)}, u32[]{:S(2)}, u32[]{:S(2)}) async-start(bf16[32,32,512]{2,1,0:T(8,128)(2,1)} %bitcast.5), calls=%async_computation.1 | async-start | bytes 2097152 | tf_op jit(solution)/shard_map/all_to_all | solution.py:61
  31.8 0.0 all-gather.4.cloned.1.call-start
  31.9 1.2 gather_fusion.1
  33.1 0.1 copy.21
  33.3 0.7 broadcast_select_fusion
  34.0 0.0 all-gather.4.cloned.1.call-update
  34.0 0.0 all-gather.6.cloned.1.call-start
  34.1 3.9 %gather_fusion = bf16[256,512]{1,0:T(8,128)(2,1)S(1)} fusion(bf16[4096,512]{1,0:T(8,128)(2,1)} %param.7, s32[1024]{0:T(1024)S(1)} %pad_clamp_fusion.1), kind=kCustom, calls=%fused_computation | custom fusion | bytes 525312 | tf_op jit(solution)/shard_map/jit(_take)/gather | solution.py:69
  38.0 0.1 copy.20
  38.2 19.8 %all-to-all-done.1 = bf16[32,32,512]{2,1,0:T(8,128)(2,1)} async-done(((bf16[32,32,512]{2,1,0:T(8,128)(2,1)}), bf16[32,32,512]{2,1,0:T(8,128)(2,1)}, u32[]{:S(2)}, u32[]{:S(2)}) %all-to-all-start.1) | async-done | bytes 1048608 | tf_op jit(solution)/shard_map/all_to_all | solution.py:61
  58.0 2.0 %fusion.13 = bf16[512,512]{0,1:T(8,128)(2,1)S(1)} fusion(bf16[1024,512]{1,0:T(8,128)(2,1)} %bitcast.6, s32[512]{0:T(512)S(1)} %multiply_add_fusion), kind=kOutput, calls=%fused_computation.22 | convolution fusion | flops 537657344 | bytes 1574912 | tf_op jit(solution)/shard_map/sj,sc->jc/dot_general | solution.py:64
  60.1 0.8 fusion.21
  60.9 0.0 all-gather.6.cloned.1.call-update
  60.9 0.0 all-gather.4.cloned.1.call-done
  61.0 2.4 %fusion.15 = (f32[256]{0:T(256)S(1)}, f32[256,1024]{1,0:T(8,128)S(1)}) fusion(bf16[256,512]{0,1:T(8,128)(2,1)} %get-tuple-element.14, bf16[1024,512]{0,1:T(8,128)(2,1)} %all-gather.4.cloned.1.call-done), kind=kOutput, calls=%fused_computation.28 | convolution fusion | flops 270270208 | bytes 2360320 | tf_op jit(solution)/shard_map/tc,kc->tk/dot_general | solution.py:78
  63.3 0.6 fusion.32
  63.9 0.6 convolution_add_fusion
  64.5 0.0 copy-start.4
  64.6 0.7 copy-done.4
  65.3 1.1 convolution_convert_fusion
  66.4 3.5 %all-to-all-start.2 = ((bf16[32,16,512]{2,1,0:T(8,128)(2,1)}), bf16[32,16,512]{2,1,0:T(8,128)(2,1)S(1)}, u32[]{:S(2)}, u32[]{:S(2)}) async-start(bf16[32,16,512]{2,1,0:T(8,128)(2,1)} %bitcast.26), calls=%async_computation.2 | async-start | bytes 1048576 | tf_op jit(solution)/shard_map/all_to_all | solution.py:97
  69.9 0.2 all-gather.8.cloned.1.call-start
  70.2 0.1 slice_reduce_fusion
  70.2 0.1 eq.111
  70.3 1.1 fusion.20
  71.4 1.7 %fusion.8 = bf16[1024,512]{1,0:T(8,128)(2,1)} fusion(s32[512]{0:T(512)S(1)} %multiply_add_fusion, bf16[256,512]{0,1:T(8,128)(2,1)S(1)} %get-tuple-element.32, bf16[256,512]{0,1:T(8,128)(2,1)S(1)} %get-tuple-element.33), kind=kOutput, calls=%fused_computation.16 | convolution fusion | flops 538968064 | bytes 1574912 | tf_op jit(solution)/shard_map/sj,jc->sc/dot_general | solution.py:108
  73.1 12.4 %all-to-all-done.2 = bf16[32,16,512]{2,1,0:T(8,128)(2,1)S(1)} async-done(((bf16[32,16,512]{2,1,0:T(8,128)(2,1)}), bf16[32,16,512]{2,1,0:T(8,128)(2,1)S(1)}, u32[]{:S(2)}, u32[]{:S(2)}) %all-to-all-start.2) | async-done | bytes 524320 | tf_op jit(solution)/shard_map/all_to_all | solution.py:97
  85.5 1.0 convolution_convert_fusion.2
  86.6 0.0 all-gather.8.cloned.1.call-update
  86.6 2.6 %fusion.14 = bf16[1024,256]{1,0:T(8,128)(2,1)} fusion(bf16[1024,512]{0,1:T(8,128)(2,1)} %all-gather.6.cloned.1.call-done, bf16[256,512]{0,1:T(8,128)(2,1)S(1)} %copy-done.2), kind=kOutput, calls=%fused_computation.23 | convolution fusion | flops 269746176 | bytes 1835008 | tf_op jit(solution)/shard_map/tc,kc->tk/dot_general | solution.py:113
  89.2 4.6 %fusion.6 = f32[2048,512]{1,0:T(8,128)} fusion(bf16[1024,256]{1,0:T(8,128)(2,1)} %fusion.14, bf16[1024,512]{0,1:T(8,128)(2,1)} %all-gather.6.cloned.1.call-done, s32[256]{0:T(256)S(1)} %copy-done.5), kind=kOutput, calls=%fused_computation.14 | convolution fusion | flops 805961728 | bytes 5768192 | tf_op jit(solution)/shard_map/se,sc->ec/dot_general | solution.py:117
  93.8 36.4 %all_to_all.21 = bf16[32,32,512]{2,1,0:T(8,128)(2,1)S(1)} all-to-all(bf16[32,32,512]{2,1,0:T(8,128)(2,1)S(1)} %bitcast.24), channel_id=1, replica_groups=mesh['wide'=8,'narrow'=4] {'wide','narrow'}, dimensions={0} | all-to-all | bytes 2097152 | tf_op jit(solution)/shard_map/all_to_all | solution.py:121
  130.2 6.4 %add_convert_fusion = bf16[2048,512]{1,0:T(8,128)(2,1)} fusion(f32[2048,512]{1,0:T(8,128)} %fusion.6, bf16[1024,512]{1,0:T(8,128)(2,1)S(1)} %bitcast.25, s32[1024]{0:T(1024)S(1)} %eq.107), kind=kOutput, calls=%fused_computation.5 | convolution fusion | flops 2151677952 | bytes 7344128 | tf_op jit(solution)/shard_map/se,sc->ec/dot_general | solution.py:125
  136.6 14.2 %all-gather.8.cloned.1.call-done = bf16[4096,512]{1,0:T(8,128)(2,1)} async-done(((bf16[128,512]{1,0:T(8,128)(2,1)}), bf16[4096,512]{1,0:T(8,128)(2,1)}) %all-gather.8.cloned.1.call-update) | async-done | bytes 4194320 | tf_op jit(solution)/shard_map/all_gather | solution.py:112
  150.8 4.5 %copy.25 = bf16[4096,512]{1,0:T(8,128)(2,1)} copy(bf16[4096,512]{1,0:T(8,128)(2,1)} %all-gather.8.cloned.1.call-done) | data formatting | bytes 8388608
  (31 shorter events, 0.3 us)
Async XLA Ops:
  7.2 17.8 %copy-start = (bf16[2048,512]{1,0:T(8,128)(2,1)S(1)}, bf16[2048,512]{1,0:T(8,128)(2,1)}, u32[]{:S(2)}) copy-start(bf16[2048,512]{1,0:T(8,128)(2,1)} %param.6) | copy-start | bytes 6291460
  28.3 3.6 %copy-start.5 = (s32[256]{0:T(256)S(1)}, s32[256]{0:T(256)}, u32[]{:S(2)}) copy-start(s32[256]{0:T(256)} %param.11) | copy-start | bytes 3076
  28.3 29.7 %all-to-all-start.1 = ((bf16[32,32,512]{2,1,0:T(8,128)(2,1)}), bf16[32,32,512]{2,1,0:T(8,128)(2,1)}, u32[]{:S(2)}, u32[]{:S(2)}) async-start(bf16[32,32,512]{2,1,0:T(8,128)(2,1)} %bitcast.5), calls=%async_computation.1 | async-start | bytes 2097152 | tf_op jit(solution)/shard_map/all_to_all | solution.py:61
  31.8 29.1 %all-gather.4.cloned.1.call-start = ((), (), s32[]{:S(2)}) async-start(), calls=%async_computation.4 | async-start | bytes 1310720 | tf_op jit(solution)/shard_map/all_gather | solution.py:76
  33.1 5.1 %copy-start.6 = (s32[256]{0:T(256)S(1)}, s32[256]{0:T(256)}, u32[]{:S(2)}) copy-start(s32[256]{0:T(256)} %param.8) | copy-start | bytes 3076
  34.0 52.6 %all-gather.6.cloned.1.call-start = ((), (), s32[]{:S(2)}) async-start(), calls=%async_computation.5 | async-start | bytes 1310720 | tf_op jit(solution)/shard_map/all_gather | solution.py:89
  60.9 3.0 %copy-start.7 = (bf16[1024,512]{0,1:T(8,128)(2,1)S(1)}, bf16[1024,512]{0,1:T(8,128)(2,1)}, u32[]{:S(2)}) copy-start(bf16[1024,512]{0,1:T(8,128)(2,1)} %all-gather.4.cloned.1.call-done) | copy-start | bytes 3145732
  64.5 5.8 %copy-start.1 = (bf16[256,512]{0,1:T(8,128)(2,1)S(1)}, bf16[256,512]{0,1:T(8,128)(2,1)}, u32[]{:S(2)}) copy-start(bf16[256,512]{0,1:T(8,128)(2,1)} %get-tuple-element.14) | copy-start | bytes 786436
  64.5 0.7 copy-start.4
  66.4 19.2 %all-to-all-start.2 = ((bf16[32,16,512]{2,1,0:T(8,128)(2,1)}), bf16[32,16,512]{2,1,0:T(8,128)(2,1)S(1)}, u32[]{:S(2)}, u32[]{:S(2)}) async-start(bf16[32,16,512]{2,1,0:T(8,128)(2,1)} %bitcast.26), calls=%async_computation.2 | async-start | bytes 1048576 | tf_op jit(solution)/shard_map/all_to_all | solution.py:97
  69.9 80.9 %all-gather.8.cloned.1.call-start = ((), (), s32[]{:S(2)}) async-start(), calls=%async_computation.6 | async-start | bytes 4325376 | tf_op jit(solution)/shard_map/all_gather | solution.py:112
  71.4 15.2 %copy-start.2 = (bf16[256,512]{0,1:T(8,128)(2,1)S(1)}, bf16[256,512]{0,1:T(8,128)(2,1)}, u32[]{:S(2)}) copy-start(bf16[256,512]{0,1:T(8,128)(2,1)} %broadcast_select_fusion) | copy-start | bytes 786436
  89.2 4.6 %copy-start.3 = (bf16[1024,512]{1,0:T(8,128)(2,1)S(1)}, bf16[1024,512]{1,0:T(8,128)(2,1)}, u32[]{:S(2)}) copy-start(bf16[1024,512]{1,0:T(8,128)(2,1)} %fusion.8) | copy-start | bytes 3145732
Sparse Core Ops, SparseCore 0:
  34.2 19.8 all-gather.3
  61.0 19.9 all-gather.5
  86.7 64.0 all-gather.7

commit v11 on v8

--- a/solution.py
+++ b/solution.py
@@ -109,7 +109,7 @@
         "sj,jc->sc", ent_place_bf, ent_grads.astype(jnp.bfloat16), preferred_element_type=jnp.float32
     ).astype(jnp.bfloat16)
     own_rel_grad, send_ent, group_query = lax.optimization_barrier((own_rel_grad, send_ent, group_query))
-    relation_grad = lax.all_gather(own_rel_grad, AXES, axis=0, tiled=True)
+    relation_grad = lax.all_gather(own_rel_grad.reshape(-1), AXES, axis=0, tiled=True).reshape(-1, row_width)
     back_ent = lax.all_to_all(
         send_ent.reshape(device_count, capacity, row_width), AXES, split_axis=0, concat_axis=0, tiled=True
     ).reshape(-1, row_width)

time: 162 us -> 165 us (1.019)
  local copies, waits for them, and re-layouts: 12.7 us -> 15.7 us
    reshape x0 -> x1, local copies, waits for them, and re-layouts: none -> 7.51 us  [body(): lax.all_gather(own_rel_grad.reshape(-1), AXES, axis=0, tiled=True)]
    unnamed x17 -> x19, local copies, waits for them, and re-layouts: 5.2 us -> 0.75 us
  transfers between devices with their start and end apart: 6 -> 6, of which waited for: 4 -> 4; matrix products, arithmetic and copies ran while one was open for 19% -> 18% of each run, Pallas kernels for 0% -> 0%
where the time goes in v11:
time: 165 us
  waiting for transfers between devices  80.2 us (49%)
  matrix products  24.7 us (15%)
  local copies, waits for them, and re-layouts  15.7 us (10%)
  blocking collectives  14.4 us (9%)
  between operations  14 us (8%)
  starting transfers between devices  10.8 us (7%)
  other arithmetic  4.8 us (3%)
    all_to_all x1, waiting for transfers between devices, body(): lax.all_to_all(send_ent.reshape(device_count, capacity, row_width), AXES,...  30.4 us
    all_to_all x1, waiting for transfers between devices, body(): lax.all_to_all(served, AXES, split_axis=0, concat_axis=0, tiled=True)  19.8 us
    all_gather x1, waiting for transfers between devices, body(): lax.all_gather(own_rel_grad.reshape(-1), AXES, axis=0, tiled=True)  17.4 us
    all_to_all x1, blocking collectives, body(): lax.all_to_all(send_ids, AXES, split_axis=0, concat_axis=0, tiled=True)  14.4 us
    all_to_all x1, waiting for transfers between devices, body(): lax.all_to_all(send_rel.reshape(device_count, rel_capacity, row_width), A...  12.6 us
    reshape x1, local copies, waits for them, and re-layouts, body(): lax.all_gather(own_rel_grad.reshape(-1), AXES, axis=0, tiled=True)  7.51 us
    dot_general x1, matrix products, body(): jnp.einsum('se,sc->ec', asked_onehot, back_ent, preferred_element_type=jn...  5.91 us
    dot_general x1, matrix products, body(): jnp.einsum('se,sc->ec', neg_onehot, neg_grad.astype(jnp.bfloat16), prefer...  4.84 us
  transfers between devices with their start and end apart: 6, of which 4 were waited for; matrix products, arithmetic and copies ran while one was open for 18% of the time, Pallas kernels for 0%

profile of v11, /device:TPU:0, one launch (start us, length us, event | category | flops | bytes accessed | tf_op | source)
XLA Modules:
  0.0 164.6 jit_solution(878467544459998753)
XLA Ops:
  7.2 0.9 fusion.40
  8.0 0.2 convert_reduce_fusion
  8.2 0.8 fusion.41
  9.0 0.3 select_reduce_fusion
  9.3 0.1 stack_reshape.3
  9.4 0.7 multiply_subtract_fusion
  10.1 0.1 convert_reduce_fusion.1
  10.2 0.2 select_reduce_fusion.1
  10.3 0.1 reshape.79
  10.5 14.4 %all_to_all.20 = s32[32,2,32]{2,1,0:T(2,128)S(1)} all-to-all(s32[32,2,32]{2,1,0:T(2,128)S(1)} %copy.19), channel_id=1, replica_groups=mesh['wide'=8,'narrow'=4] {'wide','narrow'}, dimensions={0} | all-to-all | bytes 16384 | tf_op jit(solution)/shard_map/all_to_all | solution.py:51
  24.9 0.1 eq.107
  25.0 3.3 %fusion.6 = bf16[1024,512]{1,0:T(8,128)(2,1)} fusion(bf16[2048,512]{1,0:T(8,128)(2,1)S(1)} %copy-done, s32[1024]{0:T(1024)S(1)} %eq.107), kind=kOutput, calls=%fused_computation.14 | convolution fusion | flops 2150105088 | bytes 3149824 | tf_op jit(solution)/shard_map/se,ec->sc/dot_general | solution.py:57
  28.3 3.5 %all-to-all-start.1 = ((bf16[32,32,512]{2,1,0:T(8,128)(2,1)}), bf16[32,32,512]{2,1,0:T(8,128)(2,1)}, u32[]{:S(2)}, u32[]{:S(2)}) async-start(bf16[32,32,512]{2,1,0:T(8,128)(2,1)} %bitcast.5), calls=%async_computation.1 | async-start | bytes 2097152 | tf_op jit(solution)/shard_map/all_to_all | solution.py:61
  31.9 0.0 all-gather.4.cloned.1.call-start
  31.9 1.2 gather_fusion.1
  33.1 0.1 copy.21
  33.3 0.7 broadcast_select_fusion
  34.0 0.0 all-gather.4.cloned.1.call-update
  34.0 0.0 all-gather.6.cloned.1.call-start
  34.1 3.9 %gather_fusion = bf16[256,512]{1,0:T(8,128)(2,1)S(1)} fusion(bf16[4096,512]{1,0:T(8,128)(2,1)} %param.7, s32[1024]{0:T(1024)S(1)} %pad_clamp_fusion.1), kind=kCustom, calls=%fused_computation | custom fusion | bytes 525312 | tf_op jit(solution)/shard_map/jit(_take)/gather | solution.py:69
  38.0 0.1 copy.20
  38.3 19.8 %all-to-all-done.1 = bf16[32,32,512]{2,1,0:T(8,128)(2,1)} async-done(((bf16[32,32,512]{2,1,0:T(8,128)(2,1)}), bf16[32,32,512]{2,1,0:T(8,128)(2,1)}, u32[]{:S(2)}, u32[]{:S(2)}) %all-to-all-start.1) | async-done | bytes 1048608 | tf_op jit(solution)/shard_map/all_to_all | solution.py:61
  58.0 2.0 %fusion.12 = bf16[512,512]{0,1:T(8,128)(2,1)S(1)} fusion(bf16[1024,512]{1,0:T(8,128)(2,1)} %bitcast.6, s32[512]{0:T(512)S(1)} %multiply_add_fusion), kind=kOutput, calls=%fused_computation.21 | convolution fusion | flops 537657344 | bytes 1574912 | tf_op jit(solution)/shard_map/sj,sc->jc/dot_general | solution.py:64
  60.1 0.9 fusion.20
  61.0 0.0 all-gather.6.cloned.1.call-update
  61.0 0.0 all-gather.4.cloned.1.call-done
  61.0 2.4 %fusion.14 = (f32[256]{0:T(256)S(1)}, f32[256,1024]{1,0:T(8,128)S(1)}) fusion(bf16[256,512]{0,1:T(8,128)(2,1)} %get-tuple-element.10, bf16[1024,512]{0,1:T(8,128)(2,1)} %all-gather.4.cloned.1.call-done), kind=kOutput, calls=%fused_computation.27 | convolution fusion | flops 270270208 | bytes 2360320 | tf_op jit(solution)/shard_map/tc,kc->tk/dot_general | solution.py:78
  63.4 0.6 fusion.31
  64.0 0.6 convolution_add_fusion
  64.6 2.2 %convolution_convert_fusion = bf16[512,512]{1,0:T(8,128)(2,1)} fusion(f32[256,256]{0,1:T(8,128)S(1)} %get-tuple-element.14, f32[256,256]{0,1:T(8,128)S(1)} %get-tuple-element.13, bf16[512,512]{0,1:T(8,128)(2,1)} %copy-done.5, s32[256]{0:T(256)S(1)} %multiply_add_fusion.1), kind=kOutput, calls=%fused_computation.23 | convolution fusion | flops 135266304 | bytes 1311744 | tf_op jit(solution)/shard_map/sj,jc->sc/dot_general | solution.py:91
  66.8 3.5 %all-to-all-start.2 = ((bf16[32,16,512]{2,1,0:T(8,128)(2,1)}), bf16[32,16,512]{2,1,0:T(8,128)(2,1)S(1)}, u32[]{:S(2)}, u32[]{:S(2)}) async-start(bf16[32,16,512]{2,1,0:T(8,128)(2,1)} %bitcast.28), calls=%async_computation.2 | async-start | bytes 1048576 | tf_op jit(solution)/shard_map/all_to_all | solution.py:97
  70.4 0.0 all-gather.8.cloned.1.call-start
  70.4 0.1 slice_reduce_fusion
  70.5 0.1 eq.111
  70.6 1.1 fusion.19
  71.6 1.7 %fusion.7 = bf16[1024,512]{1,0:T(8,128)(2,1)} fusion(s32[512]{0:T(512)S(1)} %multiply_add_fusion, bf16[256,512]{0,1:T(8,128)(2,1)S(1)} %get-tuple-element.28, bf16[256,512]{0,1:T(8,128)(2,1)S(1)} %get-tuple-element.29), kind=kOutput, calls=%fused_computation.15 | convolution fusion | flops 538968064 | bytes 1574912 | tf_op jit(solution)/shard_map/sj,jc->sc/dot_general | solution.py:108
  73.4 12.6 %all-to-all-done.2 = bf16[32,16,512]{2,1,0:T(8,128)(2,1)S(1)} async-done(((bf16[32,16,512]{2,1,0:T(8,128)(2,1)}), bf16[32,16,512]{2,1,0:T(8,128)(2,1)S(1)}, u32[]{:S(2)}, u32[]{:S(2)}) %all-to-all-start.2) | async-done | bytes 524320 | tf_op jit(solution)/shard_map/all_to_all | solution.py:97
  86.0 0.4 convolution_convert_fusion.2
  86.3 0.0 all-gather.6.cloned.1.call-done
  86.4 0.7 copy.24
  87.1 0.0 all-gather.8.cloned.1.call-update
  87.1 3.6 %all-to-all-start.3 = ((bf16[32,32,512]{2,1,0:T(8,128)(2,1)}), bf16[32,32,512]{2,1,0:T(8,128)(2,1)}, u32[]{:S(2)}, u32[]{:S(2)}) async-start(bf16[32,32,512]{2,1,0:T(8,128)(2,1)} %bitcast.26), calls=%async_computation.3 | async-start | bytes 2097152 | tf_op jit(solution)/shard_map/all_to_all | solution.py:113
  90.7 1.4 fusion.13
  92.1 30.4 %all-to-all-done.3 = bf16[32,32,512]{2,1,0:T(8,128)(2,1)} async-done(((bf16[32,32,512]{2,1,0:T(8,128)(2,1)}), bf16[32,32,512]{2,1,0:T(8,128)(2,1)}, u32[]{:S(2)}, u32[]{:S(2)}) %all-to-all-start.3) | async-done | bytes 1048608 | tf_op jit(solution)/shard_map/all_to_all | solution.py:113
  122.5 5.9 %fusion = f32[2048,512]{1,0:T(8,128)} fusion(bf16[1024,512]{1,0:T(8,128)(2,1)} %bitcast.10, s32[1024]{0:T(1024)S(1)} %eq.107), kind=kOutput, calls=%fused_computation.3 | convolution fusion | flops 2149580800 | bytes 5246976 | tf_op jit(solution)/shard_map/se,sc->ec/dot_general | solution.py:122
  128.4 4.8 %add_convert_fusion = bf16[2048,512]{1,0:T(8,128)(2,1)} fusion(f32[2048,512]{1,0:T(8,128)} %fusion, bf16[1024,256]{1,0:T(8,128)(2,1)} %fusion.13, bf16[1024,512]{0,1:T(8,128)(2,1)S(1)} %copy-done.2, s32[256]{0:T(256)S(1)} %copy-done.6), kind=kOutput, calls=%fused_computation.5 | convolution fusion | flops 808058880 | bytes 7865344 | tf_op jit(solution)/shard_map/se,sc->ec/dot_general | solution.py:124
  133.2 17.4 %all-gather.8.cloned.1.call-done = bf16[2097152]{0:T(1024)(128)(2,1)} async-done(((bf16[65536]{0:T(1024)(128)(2,1)}), bf16[2097152]{0:T(1024)(128)(2,1)}) %all-gather.8.cloned.1.call-update) | async-done | bytes 4194320 | tf_op jit(solution)/shard_map/all_gather | solution.py:112
  150.6 7.5 %reshape.87 = bf16[4096,512]{1,0:T(8,128)(2,1)} reshape(bf16[2097152]{0:T(1024)(128)(2,1)} %all-gather.8.cloned.1.call-done) | data formatting | bytes 8388608 | tf_op jit(solution)/shard_map/reshape | solution.py:112
  (35 shorter events, 0.3 us)
Async XLA Ops:
  7.2 17.8 %copy-start = (bf16[2048,512]{1,0:T(8,128)(2,1)S(1)}, bf16[2048,512]{1,0:T(8,128)(2,1)}, u32[]{:S(2)}) copy-start(bf16[2048,512]{1,0:T(8,128)(2,1)} %param.6) | copy-start | bytes 6291460
  28.3 3.6 %copy-start.6 = (s32[256]{0:T(256)S(1)}, s32[256]{0:T(256)}, u32[]{:S(2)}) copy-start(s32[256]{0:T(256)} %param.11) | copy-start | bytes 3076
  28.3 29.7 %all-to-all-start.1 = ((bf16[32,32,512]{2,1,0:T(8,128)(2,1)}), bf16[32,32,512]{2,1,0:T(8,128)(2,1)}, u32[]{:S(2)}, u32[]{:S(2)}) async-start(bf16[32,32,512]{2,1,0:T(8,128)(2,1)} %bitcast.5), calls=%async_computation.1 | async-start | bytes 2097152 | tf_op jit(solution)/shard_map/all_to_all | solution.py:61
  31.9 29.1 %all-gather.4.cloned.1.call-start = ((), (), s32[]{:S(2)}) async-start(), calls=%async_computation.4 | async-start | bytes 1310720 | tf_op jit(solution)/shard_map/all_gather | solution.py:76
  33.1 5.1 %copy-start.7 = (s32[256]{0:T(256)S(1)}, s32[256]{0:T(256)}, u32[]{:S(2)}) copy-start(s32[256]{0:T(256)} %param.8) | copy-start | bytes 3076
  34.0 52.3 %all-gather.6.cloned.1.call-start = ((), (), s32[]{:S(2)}) async-start(), calls=%async_computation.5 | async-start | bytes 1310720 | tf_op jit(solution)/shard_map/all_gather | solution.py:89
  60.0 3.9 %copy-start.5 = (bf16[512,512]{0,1:T(8,128)(2,1)}, bf16[512,512]{0,1:T(8,128)(2,1)S(1)}, u32[]{:S(2)}) copy-start(bf16[512,512]{0,1:T(8,128)(2,1)S(1)} %fusion.12) | copy-start | bytes 1572868
  61.0 3.0 %copy-start.8 = (bf16[1024,512]{0,1:T(8,128)(2,1)S(1)}, bf16[1024,512]{0,1:T(8,128)(2,1)}, u32[]{:S(2)}) copy-start(bf16[1024,512]{0,1:T(8,128)(2,1)} %all-gather.4.cloned.1.call-done) | copy-start | bytes 3145732
  64.6 6.0 %copy-start.1 = (bf16[256,512]{0,1:T(8,128)(2,1)S(1)}, bf16[256,512]{0,1:T(8,128)(2,1)}, u32[]{:S(2)}) copy-start(bf16[256,512]{0,1:T(8,128)(2,1)} %get-tuple-element.10) | copy-start | bytes 786436
  64.6 2.2 %copy-start.4 = (f32[256,256]{0,1:T(8,128)}, f32[256,256]{0,1:T(8,128)S(1)}, u32[]{:S(2)}) copy-start(f32[256,256]{0,1:T(8,128)S(1)} %get-tuple-element.14) | copy-start | bytes 786436
  66.8 19.2 %all-to-all-start.2 = ((bf16[32,16,512]{2,1,0:T(8,128)(2,1)}), bf16[32,16,512]{2,1,0:T(8,128)(2,1)S(1)}, u32[]{:S(2)}, u32[]{:S(2)}) async-start(bf16[32,16,512]{2,1,0:T(8,128)(2,1)} %bitcast.28), calls=%async_computation.2 | async-start | bytes 1048576 | tf_op jit(solution)/shard_map/all_to_all | solution.py:97
  70.4 80.2 %all-gather.8.cloned.1.call-start = ((), (), s32[]{:S(2)}) async-start(), calls=%async_computation.6 | async-start | bytes 4325376 | tf_op jit(solution)/shard_map/all_gather | solution.py:112
  73.4 17.3 %copy-start.3 = (bf16[256,512]{0,1:T(8,128)(2,1)S(1)}, bf16[256,512]{0,1:T(8,128)(2,1)}, u32[]{:S(2)}) copy-start(bf16[256,512]{0,1:T(8,128)(2,1)} %broadcast_select_fusion) | copy-start | bytes 786436
  86.4 4.3 %copy-start.2 = (bf16[1024,512]{0,1:T(8,128)(2,1)S(1)}, bf16[1024,512]{0,1:T(8,128)(2,1)}, u32[]{:S(2)}) copy-start(bf16[1024,512]{0,1:T(8,128)(2,1)} %all-gather.6.cloned.1.call-done) | copy-start | bytes 3145732
  87.1 35.3 %all-to-all-start.3 = ((bf16[32,32,512]{2,1,0:T(8,128)(2,1)}), bf16[32,32,512]{2,1,0:T(8,128)(2,1)}, u32[]{:S(2)}, u32[]{:S(2)}) async-start(bf16[32,32,512]{2,1,0:T(8,128)(2,1)} %bitcast.26), calls=%async_computation.3 | async-start | bytes 2097152 | tf_op jit(solution)/shard_map/all_to_all | solution.py:113
Sparse Core Ops, SparseCore 0:
  34.2 19.8 all-gather.3
  61.1 19.9 all-gather.5
  87.2 63.2 all-gather.7

commit v12 on v8

--- a/solution.py
+++ b/solution.py
@@ -76,7 +76,6 @@
     gathered = lax.all_gather(own_negs, "narrow", axis=0, tiled=True)
     group_neg = gathered.shape[0]
     scores = jnp.einsum("tc,kc->tk", query, gathered, preferred_element_type=jnp.float32)
-    loss = jax.nn.softplus(-positive) + jnp.sum(jax.nn.softplus(scores), axis=1) / group_neg
     neg_weights = (jax.nn.sigmoid(scores) / group_neg).astype(jnp.bfloat16)
     pos_weight = -jax.nn.sigmoid(-positive)
     query_grad = pos_weight[:, None] * tail_rows.astype(jnp.float32) + jnp.dot(
@@ -94,9 +93,11 @@
         rel_part.astype(jnp.bfloat16),
         preferred_element_type=jnp.float32,
     ).astype(jnp.bfloat16)
+    send_rel, loss_scores, loss_positive = lax.optimization_barrier((send_rel, scores, positive))
     back_rel = lax.all_to_all(
         send_rel.reshape(device_count, rel_capacity, row_width), AXES, split_axis=0, concat_axis=0, tiled=True
     ).reshape(-1, row_width)
+    loss = jax.nn.softplus(-loss_positive) + jnp.sum(jax.nn.softplus(loss_scores), axis=1) / group_neg
     rel_onehot = (
         rel_ids_in[:, None] == jnp.arange(rel_per_group, dtype=jnp.int32)[None, :]
     ).astype(jnp.bfloat16)

time: 162 us -> 163 us (level)
  waiting for transfers between devices: 80.1 us -> 77.4 us
  matrix products: 24.3 us -> 26.1 us
    all_to_all x1, waiting for transfers between devices: 30.7 us -> 27.9 us  [body(): lax.all_to_all(send_ent.reshape(device_count, capacity, row_width), AXES,...]
    unnamed x17 -> x25, local copies, waits for them, and re-layouts: 5.2 us -> 5.97 us
  transfers between devices with their start and end apart: 6 -> 6, of which waited for: 4 -> 4; matrix products, arithmetic and copies ran while one was open for 19% -> 20% of each run, Pallas kernels for 0% -> 0%
where the time goes in v12:
time: 163 us; the launch traced here: 162 us
  waiting for transfers between devices  77.4 us (47%)
  matrix products  26.1 us (16%)
  blocking collectives  14.4 us (9%)
  between operations  14 us (9%)
  local copies, waits for them, and re-layouts  13.5 us (8%)
  starting transfers between devices  10.9 us (7%)
  other arithmetic  5.59 us (3%)
    all_to_all x1, waiting for transfers between devices, body(): lax.all_to_all(send_ent.reshape(device_count, capacity, row_width), AXES,...  27.9 us
    all_to_all x1, waiting for transfers between devices, body(): lax.all_to_all(served, AXES, split_axis=0, concat_axis=0, tiled=True)  19.8 us
    all_gather x1, waiting for transfers between devices, body(): relation_grad = lax.all_gather(own_rel_grad, AXES, axis=0, tiled=True)  17.2 us
    all_to_all x1, blocking collectives, body(): lax.all_to_all(send_ids, AXES, split_axis=0, concat_axis=0, tiled=True)  14.4 us
    all_to_all x1, waiting for transfers between devices, body(): lax.all_to_all(send_rel.reshape(device_count, rel_capacity, row_width), A...  12.4 us
    dot_general x1, matrix products, body(): jnp.einsum('se,sc->ec', asked_onehot, back_ent, preferred_element_type=jn...  6 us
    unnamed x25, local copies, waits for them, and re-layouts  5.97 us
    dot_general x1, matrix products, body(): jnp.einsum('se,sc->ec', neg_onehot, neg_grad.astype(jnp.bfloat16), prefer...  4.84 us
  transfers between devices with their start and end apart: 6, of which 4 were waited for; matrix products, arithmetic and copies ran while one was open for 20% of the time, Pallas kernels for 0%

profile of v12, /device:TPU:0, one launch (start us, length us, event | category | flops | bytes accessed | tf_op | source)
XLA Modules:
  0.0 161.9 jit_solution(1629123086760071720)
XLA Ops:
  7.2 0.9 fusion.40
  8.0 0.2 convert_reduce_fusion
  8.2 0.8 fusion.41
  9.0 0.3 select_reduce_fusion
  9.3 0.1 stack_reshape.3
  9.4 0.7 multiply_subtract_fusion
  10.1 0.1 convert_reduce_fusion.1
  10.2 0.2 select_reduce_fusion.1
  10.3 0.1 reshape.73
  10.5 14.4 %all_to_all.20 = s32[32,2,32]{2,1,0:T(2,128)S(1)} all-to-all(s32[32,2,32]{2,1,0:T(2,128)S(1)} %copy.19), channel_id=1, replica_groups=mesh['wide'=8,'narrow'=4] {'wide','narrow'}, dimensions={0} | all-to-all | bytes 16384 | tf_op jit(solution)/shard_map/all_to_all | solution.py:51
  24.9 0.1 eq.107
  25.0 3.3 %fusion.6 = bf16[1024,512]{1,0:T(8,128)(2,1)} fusion(bf16[2048,512]{1,0:T(8,128)(2,1)S(1)} %copy-done, s32[1024]{0:T(1024)S(1)} %eq.107), kind=kOutput, calls=%fused_computation.14 | convolution fusion | flops 2150105088 | bytes 3149824 | tf_op jit(solution)/shard_map/se,ec->sc/dot_general | solution.py:57
  28.3 3.5 %all-to-all-start.1 = ((bf16[32,32,512]{2,1,0:T(8,128)(2,1)}), bf16[32,32,512]{2,1,0:T(8,128)(2,1)}, u32[]{:S(2)}, u32[]{:S(2)}) async-start(bf16[32,32,512]{2,1,0:T(8,128)(2,1)} %bitcast.5), calls=%async_computation.1 | async-start | bytes 2097152 | tf_op jit(solution)/shard_map/all_to_all | solution.py:61
  31.8 0.0 all-gather.4.cloned.1.call-start
  31.9 1.2 gather_fusion.1
  33.1 0.1 copy.21
  33.3 0.7 broadcast_select_fusion
  34.0 0.0 all-gather.6.cloned.1.call-start
  34.1 3.9 %gather_fusion = bf16[256,512]{1,0:T(8,128)(2,1)S(1)} fusion(bf16[4096,512]{1,0:T(8,128)(2,1)} %param.7, s32[1024]{0:T(1024)S(1)} %pad_clamp_fusion.1), kind=kCustom, calls=%fused_computation | custom fusion | bytes 525312 | tf_op jit(solution)/shard_map/jit(_take)/gather | solution.py:69
  38.0 0.1 copy.20
  38.2 19.8 %all-to-all-done.1 = bf16[32,32,512]{2,1,0:T(8,128)(2,1)} async-done(((bf16[32,32,512]{2,1,0:T(8,128)(2,1)}), bf16[32,32,512]{2,1,0:T(8,128)(2,1)}, u32[]{:S(2)}, u32[]{:S(2)}) %all-to-all-start.1) | async-done | bytes 1048608 | tf_op jit(solution)/shard_map/all_to_all | solution.py:61
  58.0 2.0 %fusion.12 = bf16[512,512]{0,1:T(8,128)(2,1)S(1)} fusion(bf16[1024,512]{1,0:T(8,128)(2,1)} %bitcast.6, s32[512]{0:T(512)S(1)} %multiply_add_fusion), kind=kOutput, calls=%fused_computation.21 | convolution fusion | flops 537657344 | bytes 1574912 | tf_op jit(solution)/shard_map/sj,sc->jc/dot_general | solution.py:64
  60.1 0.8 copy-done.8
  60.8 0.8 fusion.20
  61.7 0.0 all-gather.6.cloned.1.call-update
  61.7 0.0 all-gather.4.cloned.1.call-done
  61.8 1.9 %fusion.42 = f32[256,1024]{1,0:T(8,128)S(1)} fusion(bf16[256,512]{0,1:T(8,128)(2,1)} %get-tuple-element.16, bf16[1024,512]{0,1:T(8,128)(2,1)} %all-gather.4.cloned.1.call-done), kind=kOutput, calls=%fused_computation.93 | convolution fusion | flops 268435456 | bytes 2359296 | tf_op jit(solution)/shard_map/tc,kc->tk/dot_general | solution.py:78
  63.7 0.6 convolution_add_fusion
  64.3 0.7 copy-done.6
  65.0 1.1 convolution_convert_fusion
  66.2 3.7 %all-to-all-start.2 = ((bf16[32,16,512]{2,1,0:T(8,128)(2,1)}), bf16[32,16,512]{2,1,0:T(8,128)(2,1)}, u32[]{:S(2)}, u32[]{:S(2)}) async-start(bf16[32,16,512]{2,1,0:T(8,128)(2,1)} %bitcast.24), calls=%async_computation.2 | async-start | bytes 1048576 | tf_op jit(solution)/shard_map/all_to_all | solution.py:97
  69.8 0.0 all-gather.8.cloned.1.call-start
  69.9 0.1 slice_reduce_fusion
  69.9 0.1 eq.111
  70.0 1.2 fusion.19
  71.3 1.7 %fusion.7 = bf16[1024,512]{1,0:T(8,128)(2,1)} fusion(s32[512]{0:T(512)S(1)} %multiply_add_fusion, bf16[256,512]{0,1:T(8,128)(2,1)S(1)} %get-tuple-element.30, bf16[256,512]{0,1:T(8,128)(2,1)S(1)} %get-tuple-element.31), kind=kOutput, calls=%fused_computation.15 | convolution fusion | flops 538968064 | bytes 1574912 | tf_op jit(solution)/shard_map/sj,jc->sc/dot_general | solution.py:109
  73.0 12.4 %all-to-all-done.2 = bf16[32,16,512]{2,1,0:T(8,128)(2,1)} async-done(((bf16[32,16,512]{2,1,0:T(8,128)(2,1)}), bf16[32,16,512]{2,1,0:T(8,128)(2,1)}, u32[]{:S(2)}, u32[]{:S(2)}) %all-to-all-start.2) | async-done | bytes 524320 | tf_op jit(solution)/shard_map/all_to_all | solution.py:97
  85.4 2.0 %convolution_convert_fusion.2 = bf16[128,512]{1,0:T(8,128)(2,1)} fusion(bf16[512,512]{1,0:T(8,128)(2,1)} %bitcast.8, s32[512]{0:T(512)S(1)} %eq.111), kind=kOutput, calls=%fused_computation.26 | convolution fusion | flops 67239936 | bytes 657408 | tf_op jit(solution)/shard_map/sr,sc->rc/dot_general | solution.py:104
  87.5 0.0 all-gather.8.cloned.1.call-update
  87.5 3.6 %all-to-all-start.3 = ((bf16[32,32,512]{2,1,0:T(8,128)(2,1)}), bf16[32,32,512]{2,1,0:T(8,128)(2,1)}, u32[]{:S(2)}, u32[]{:S(2)}) async-start(bf16[32,32,512]{2,1,0:T(8,128)(2,1)} %bitcast.23), calls=%async_computation.3 | async-start | bytes 2097152 | tf_op jit(solution)/shard_map/all_to_all | solution.py:114
  91.1 0.7 fusion.14
  91.7 0.6 fusion.31
  92.3 2.6 %fusion.13 = bf16[1024,256]{1,0:T(8,128)(2,1)} fusion(bf16[1024,512]{0,1:T(8,128)(2,1)} %all-gather.6.cloned.1.call-done, bf16[256,512]{0,1:T(8,128)(2,1)S(1)} %copy-done.4), kind=kOutput, calls=%fused_computation.22 | convolution fusion | flops 269746176 | bytes 1835008 | tf_op jit(solution)/shard_map/tc,kc->tk/dot_general | solution.py:118
  94.9 27.9 %all-to-all-done.3 = bf16[32,32,512]{2,1,0:T(8,128)(2,1)} async-done(((bf16[32,32,512]{2,1,0:T(8,128)(2,1)}), bf16[32,32,512]{2,1,0:T(8,128)(2,1)}, u32[]{:S(2)}, u32[]{:S(2)}) %all-to-all-start.3) | async-done | bytes 1048608 | tf_op jit(solution)/shard_map/all_to_all | solution.py:114
  122.8 6.0 %fusion = f32[2048,512]{1,0:T(8,128)} fusion(bf16[1024,512]{1,0:T(8,128)(2,1)} %bitcast.10, s32[1024]{0:T(1024)S(1)} %eq.107), kind=kOutput, calls=%fused_computation.3 | convolution fusion | flops 2149580800 | bytes 5246976 | tf_op jit(solution)/shard_map/se,sc->ec/dot_general | solution.py:123
  128.8 4.8 %add_convert_fusion = bf16[2048,512]{1,0:T(8,128)(2,1)} fusion(f32[2048,512]{1,0:T(8,128)} %fusion, bf16[1024,256]{1,0:T(8,128)(2,1)} %fusion.13, bf16[1024,512]{0,1:T(8,128)(2,1)S(1)} %copy-done.3, s32[256]{0:T(256)S(1)} %copy-done.10), kind=kOutput, calls=%fused_computation.5 | convolution fusion | flops 808058880 | bytes 7865344 | tf_op jit(solution)/shard_map/se,sc->ec/dot_general | solution.py:125
  133.7 17.2 %all-gather.8.cloned.1.call-done = bf16[4096,512]{1,0:T(8,128)(2,1)} async-done(((bf16[128,512]{1,0:T(8,128)(2,1)}), bf16[4096,512]{1,0:T(8,128)(2,1)}) %all-gather.8.cloned.1.call-update) | async-done | bytes 4194320 | tf_op jit(solution)/shard_map/all_gather | solution.py:113
  150.9 4.5 %copy.25 = bf16[4096,512]{1,0:T(8,128)(2,1)} copy(bf16[4096,512]{1,0:T(8,128)(2,1)} %all-gather.8.cloned.1.call-done) | data formatting | bytes 8388608
  (42 shorter events, 0.3 us)
Async XLA Ops:
  7.2 17.8 %copy-start = (bf16[2048,512]{1,0:T(8,128)(2,1)S(1)}, bf16[2048,512]{1,0:T(8,128)(2,1)}, u32[]{:S(2)}) copy-start(bf16[2048,512]{1,0:T(8,128)(2,1)} %param.6) | copy-start | bytes 6291460
  28.3 3.6 %copy-start.10 = (s32[256]{0:T(256)S(1)}, s32[256]{0:T(256)}, u32[]{:S(2)}) copy-start(s32[256]{0:T(256)} %param.11) | copy-start | bytes 3076
  28.3 29.7 %all-to-all-start.1 = ((bf16[32,32,512]{2,1,0:T(8,128)(2,1)}), bf16[32,32,512]{2,1,0:T(8,128)(2,1)}, u32[]{:S(2)}, u32[]{:S(2)}) async-start(bf16[32,32,512]{2,1,0:T(8,128)(2,1)} %bitcast.5), calls=%async_computation.1 | async-start | bytes 2097152 | tf_op jit(solution)/shard_map/all_to_all | solution.py:61
  31.8 29.9 %all-gather.4.cloned.1.call-start = ((), (), s32[]{:S(2)}) async-start(), calls=%async_computation.4 | async-start | bytes 1310720 | tf_op jit(solution)/shard_map/all_gather | solution.py:76
  33.1 5.1 %copy-start.11 = (s32[256]{0:T(256)S(1)}, s32[256]{0:T(256)}, u32[]{:S(2)}) copy-start(s32[256]{0:T(256)} %param.8) | copy-start | bytes 3076
  34.0 53.5 %all-gather.6.cloned.1.call-start = ((), (), s32[]{:S(2)}) async-start(), calls=%async_computation.5 | async-start | bytes 1310720 | tf_op jit(solution)/shard_map/all_gather | solution.py:88
  38.2 21.9 %copy-start.2 = (bf16[256,512]{0,1:T(8,128)(2,1)}, bf16[256,512]{0,1:T(8,128)(2,1)S(1)}, u32[]{:S(2)}) copy-start(bf16[256,512]{0,1:T(8,128)(2,1)S(1)} %copy.20) | copy-start | bytes 786436
  60.0 0.8 copy-start.8
  61.8 1.9 %copy-start.5 = (bf16[1024,512]{0,1:T(8,128)(2,1)S(1)}, bf16[1024,512]{0,1:T(8,128)(2,1)}, u32[]{:S(2)}) copy-start(bf16[1024,512]{0,1:T(8,128)(2,1)} %all-gather.4.cloned.1.call-done) | copy-start | bytes 3145732
  61.8 1.9 %copy-start.9 = (bf16[512,512]{0,1:T(8,128)(2,1)S(1)}, bf16[512,512]{0,1:T(8,128)(2,1)}, u32[]{:S(2)}) copy-start(bf16[512,512]{0,1:T(8,128)(2,1)} %copy-done.8) | copy-start | bytes 1572868
  64.3 5.8 %copy-start.1 = (bf16[256,512]{0,1:T(8,128)(2,1)S(1)}, bf16[256,512]{0,1:T(8,128)(2,1)}, u32[]{:S(2)}) copy-start(bf16[256,512]{0,1:T(8,128)(2,1)} %get-tuple-element.16) | copy-start | bytes 786436
  64.3 0.7 copy-start.6
  64.3 1.8 %copy-start.7 = (f32[256,256]{0,1:T(8,128)}, f32[256,256]{0,1:T(8,128)S(1)}, u32[]{:S(2)}) copy-start(f32[256,256]{0,1:T(8,128)S(1)} %get-tuple-element.20) | copy-start | bytes 786436
  66.2 19.3 %all-to-all-start.2 = ((bf16[32,16,512]{2,1,0:T(8,128)(2,1)}), bf16[32,16,512]{2,1,0:T(8,128)(2,1)}, u32[]{:S(2)}, u32[]{:S(2)}) async-start(bf16[32,16,512]{2,1,0:T(8,128)(2,1)} %bitcast.24), calls=%async_computation.2 | async-start | bytes 1048576 | tf_op jit(solution)/shard_map/all_to_all | solution.py:97
  69.8 81.1 %all-gather.8.cloned.1.call-start = ((), (), s32[]{:S(2)}) async-start(), calls=%async_computation.6 | async-start | bytes 4325376 | tf_op jit(solution)/shard_map/all_gather | solution.py:113
  73.0 19.3 %copy-start.4 = (bf16[256,512]{0,1:T(8,128)(2,1)S(1)}, bf16[256,512]{0,1:T(8,128)(2,1)}, u32[]{:S(2)}) copy-start(bf16[256,512]{0,1:T(8,128)(2,1)} %broadcast_select_fusion) | copy-start | bytes 786436
  87.5 35.3 %all-to-all-start.3 = ((bf16[32,32,512]{2,1,0:T(8,128)(2,1)}), bf16[32,32,512]{2,1,0:T(8,128)(2,1)}, u32[]{:S(2)}, u32[]{:S(2)}) async-start(bf16[32,32,512]{2,1,0:T(8,128)(2,1)} %bitcast.23), calls=%async_computation.3 | async-start | bytes 2097152 | tf_op jit(solution)/shard_map/all_to_all | solution.py:114
  122.8 6.0 %copy-start.3 = (bf16[1024,512]{0,1:T(8,128)(2,1)S(1)}, bf16[1024,512]{0,1:T(8,128)(2,1)}, u32[]{:S(2)}) copy-start(bf16[1024,512]{0,1:T(8,128)(2,1)} %all-gather.6.cloned.1.call-done) | copy-start | bytes 3145732
Sparse Core Ops, SparseCore 0:
  34.2 19.8 all-gather.3
  61.8 20.3 all-gather.5
  87.6 63.2 all-gather.7
